TPU v7x, 256 devices: a whole 4x4x8 slice. The times are simulated.
256 devices in a mesh: seq: 64 (over z, x, core), tp: 4 (over y).
Axes of the slice: x: 4, y: 4, z: 8, core: 2. Of those that a mesh axis runs over, the one named last changes fastest.
Arguments:
- hidden: bfloat16 [8192, 1024], P('seq'), may hold values from -120 to 120
- page_table: int32 [16, 256], replicated, may hold values from -1 to 2111, as said below
- cache_len: int32 [16], replicated, may hold values from 129 to 32768, as said below
- expert_ids: int32 [8192, 2], P('seq'), may hold values from 0 to 31, all different within a row; in each aligned block of 128 rows (0 to 127, 128 to 255, ...) at most 10 rows name the same one
- w_query: bfloat16 [1024, 1024], P(None, 'tp'), may hold values from -4 to 4
- w_key: bfloat16 [1024, 1024], P(None, 'tp'), may hold values from -0.1875 to 0.1875
- w_value: bfloat16 [1024, 1024], P(None, 'tp'), may hold values from -0.1875 to 0.1875
- w_out: bfloat16 [1024, 1024], P('tp'), may hold values from -0.1875 to 0.1875
- cache_k: bfloat16 [2112, 128, 1024], P('seq', None, 'tp'), may hold values from -4000 to 4000
- cache_v: bfloat16 [2112, 128, 1024], P('seq', None, 'tp'), may hold values from -6 to 6
- moe_gain: float32 [1024], replicated, may hold values from 0.1 to 1.9
- router: float32 [1024, 32], replicated, may hold values from -0.1875 to 0.1875
- w_gate_up: bfloat16 [64, 2, 1024, 1408], P('seq', None, None, 'tp'), may hold values from -0.1875 to 0.1875
- w_down: bfloat16 [64, 1408, 1024], P('seq', 'tp'), may hold values from -0.109375 to 0.109375
Outputs:
- out: bfloat16 [8192, 1024], P('seq', 'tp')
Inputs may be any that keep to these rules, and one draw needn't show every extreme that they name: `page_table`: row r lists the pages of request r's cache in order, ceil(cache_len[r] / 128) of them, then -1; no page number appears twice in the table. `cache_len`: half of the requests have exactly 32768 cached tokens; the others have at most 384. `expert_ids`: A token names 2 different experts; among the 128 tokens of one device no expert is named more than 10 times, and on some device one expert is named exactly 10 times.
All inputs are finite; a program needn't handle non-finite values.
Results may differ from a plain program's by a relative error of at most 0.0085.
Values may be sent and summed in bfloat16 or wider, within the bound.
No kernel may reach another device: no remote copies, remote signals or barrier semaphores. Data moves between devices by JAX's collectives and lax.ppermute only.
A program may use at most 128 MiB of HBM per device.

v0:
```python
import jax
import jax.numpy as jnp
from jax import lax
from jax.sharding import PartitionSpec as P
from jax.experimental import pallas as pl
from jax.experimental.pallas import tpu as pltpu

DH = 64
EXPERTS = 32
TOP = 2
PAGE = 128
MAXP = 256
SPAN_DEVS = 4
CAP = 10


NEGATIVE = -1e30


def passed_along(value, axis, steps):
    count = lax.axis_size(axis)
    pairs = [(source, (source + steps) % count) for source in range(count)]
    return lax.ppermute(value, axis, pairs)


def rms_rows(values):
    return values * lax.rsqrt(jnp.mean(values * values, axis=-1, keepdims=True) + 1e-06)


def online_update(state, queries, keys, values, mask):
    m_old, l_old, accum = state
    scale = queries.shape[2] ** (-0.5)
    scores = jnp.einsum("nhd,khd->hnk", queries, keys, preferred_element_type=jnp.float32) * scale
    scores = jnp.where(mask[None], scores, NEGATIVE)
    m_new = jnp.maximum(m_old, jnp.max(scores, axis=-1).T)
    probs = jnp.where(mask[None], jnp.exp(scores - m_new.T[:, :, None]), 0.0)
    factor = jnp.exp(m_old - m_new)
    l_new = l_old * factor + jnp.sum(probs, axis=-1).T
    weighted = jnp.einsum(
        "hnk,khd->nhd", probs.astype(jnp.bfloat16), values, preferred_element_type=jnp.float32
    )
    return (m_new, l_new, accum * factor[:, :, None] + weighted)


def attend_kernel(
    own_ref, page_ref, limit_ref, offset_ref, fresh_ref,
    q_ref, k_ref, v_ref, nk_ref, nv_ref, acc_ref, stat_ref,
):
    step = pl.program_id(0)
    owner = own_ref[step]
    first = (step == 0) | (own_ref[jnp.maximum(step - 1, 0)] != owner)
    heads = acc_ref.shape[1]

    @pl.when(first)
    def _():
        acc_ref[...] = jnp.zeros(acc_ref.shape, acc_ref.dtype)
        stat_ref[0, :heads, :] = jnp.full((heads, stat_ref.shape[2]), NEGATIVE, jnp.float32)
        stat_ref[0, heads:, :] = jnp.zeros((heads, stat_ref.shape[2]), jnp.float32)

    is_fresh = fresh_ref[step] == 1
    keys = jnp.where(is_fresh, nk_ref[0], k_ref[0])
    vals = jnp.where(is_fresh, nv_ref[0], v_ref[0])
    rows, cols = keys.shape[0], q_ref.shape[1]
    k_pos = lax.broadcasted_iota(jnp.int32, (rows, cols), 0)
    q_pos = lax.broadcasted_iota(jnp.int32, (rows, cols), 1)
    valid = (k_pos < limit_ref[step]) & (q_pos >= offset_ref[step] + k_pos)
    for h in range(heads):
        lanes = slice(h * DH, (h + 1) * DH)
        s = lax.dot_general(
            keys[:, lanes], q_ref[0, :, lanes], (((1,), (1,)), ((), ())),
            preferred_element_type=jnp.float32,
        ) * (DH ** (-0.5))
        s = jnp.where(valid, s, NEGATIVE)
        m_prev = stat_ref[0, h : h + 1, :]
        m_cur = jnp.maximum(m_prev, jnp.max(s, axis=0, keepdims=True))
        p = jnp.where(valid, jnp.exp(s - m_cur), 0.0)
        alpha = jnp.exp(m_prev - m_cur)
        stat_ref[0, heads + h : heads + h + 1, :] = alpha * stat_ref[
            0, heads + h : heads + h + 1, :
        ] + jnp.sum(p, axis=0, keepdims=True)
        pv = lax.dot_general(
            vals[:, lanes], p.astype(jnp.bfloat16), (((0,), (0,)), ((), ())),
            preferred_element_type=jnp.float32,
        )
        acc_ref[0, h] = alpha * acc_ref[0, h] + pv
        stat_ref[0, h : h + 1, :] = m_cur


def local_attention(
    owner, page, limit, offset, fresh, everyone, cache_k, cache_v, new_k, new_v, heads, requests
):
    span_rows, width = everyone.shape[1], everyone.shape[2]
    page_rows = cache_k.shape[1]
    blocks = owner.shape[0]
    by_owner = lambda b, own, pg, lim, off, fr: (own[b], 0, 0)
    by_page = lambda b, own, pg, lim, off, fr: (pg[b], 0, 0)
    fixed = lambda b, own, pg, lim, off, fr: (0, 0, 0)
    acc_map = lambda b, own, pg, lim, off, fr: (own[b], 0, 0, 0)
    grid_spec = pltpu.PrefetchScalarGridSpec(
        num_scalar_prefetch=5,
        grid=(blocks,),
        in_specs=[
            pl.BlockSpec((1, span_rows, width), by_owner),
            pl.BlockSpec((1, page_rows, width), by_page),
            pl.BlockSpec((1, page_rows, width), by_page),
            pl.BlockSpec((1, page_rows, width), fixed),
            pl.BlockSpec((1, page_rows, width), fixed),
        ],
        out_specs=[
            pl.BlockSpec((1, heads, DH, span_rows), acc_map),
            pl.BlockSpec((1, 2 * heads, span_rows), by_owner),
        ],
    )
    return pl.pallas_call(
        attend_kernel,
        grid_spec=grid_spec,
        out_shape=[
            jax.ShapeDtypeStruct((requests, heads, DH, span_rows), jnp.float32),
            jax.ShapeDtypeStruct((requests, 2 * heads, span_rows), jnp.float32),
        ],
        compiler_params=pltpu.CompilerParams(dimension_semantics=("arbitrary",)),
    )(owner, page, limit, offset, fresh, everyone, cache_k, cache_v, new_k, new_v)


def shards(
    hidden,
    page_table,
    cache_len,
    expert_ids,
    w_query,
    w_key,
    w_value,
    w_out,
    cache_k,
    cache_v,
    moe_gain,
    router,
    w_gate_up,
    w_down,
):
    tok_rows = hidden.shape[0]
    span_rows = tok_rows * SPAN_DEVS
    seq_count = lax.axis_size("seq")
    seq_index = lax.axis_index("seq")
    local_heads = w_query.shape[1] // DH
    request_total = page_table.shape[0]
    normed = rms_rows(hidden.astype(jnp.float32)).astype(jnp.bfloat16)
    queries = jnp.dot(normed, w_query, preferred_element_type=jnp.float32).astype(jnp.bfloat16)
    new_keys = (
        jnp.dot(normed, w_key, preferred_element_type=jnp.float32)
        .astype(jnp.bfloat16)
        .reshape(tok_rows, local_heads, DH)
    )
    new_values = (
        jnp.dot(normed, w_value, preferred_element_type=jnp.float32)
        .astype(jnp.bfloat16)
        .reshape(tok_rows, local_heads, DH)
    )
    page_count = cache_k.shape[0]
    page_ids = seq_index * page_count + jnp.arange(page_count, dtype=jnp.int32)
    listing = page_table.reshape(-1)
    matches = listing[None, :] == page_ids[:, None]
    entry_index = jnp.arange(listing.shape[0], dtype=jnp.int32)
    found = jnp.sum(jnp.where(matches, entry_index[None, :] + 1, 0), axis=1) - 1
    page_owner = jnp.where(found >= 0, found // MAXP, -1)
    page_order = jnp.where(found >= 0, found % MAXP, 0)
    page_limit = jnp.where(found >= 0, cache_len[jnp.maximum(page_owner, 0)], 0)
    own_request = seq_index * tok_rows // span_rows
    own_offset = seq_index * tok_rows % span_rows
    slot_range = jnp.arange(PAGE, dtype=jnp.int32)
    page_valid = (found >= 0)[:, None] & (
        page_order[:, None] * PAGE + slot_range[None, :] < page_limit[:, None]
    )
    block_total = page_count + 1
    owners = jnp.concatenate([jnp.maximum(page_owner, 0), own_request[None]], axis=0)
    key_limits = jnp.concatenate(
        [jnp.clip(page_limit - page_order * PAGE, 0, PAGE), jnp.full((1,), PAGE, jnp.int32)], axis=0
    )
    query_offsets = jnp.concatenate(
        [jnp.full((page_count,), -span_rows - PAGE, jnp.int32), own_offset[None]], axis=0
    )
    block_order = jnp.argsort(owners, stable=True).astype(jnp.int32)
    sorted_owner = owners[block_order]
    sorted_limit = key_limits[block_order]
    sorted_offset = query_offsets[block_order]
    sorted_fresh = (block_order == page_count).astype(jnp.int32)
    sorted_page = jnp.minimum(block_order, page_count - 1)
    everyone = lax.all_gather(queries, "seq", axis=0, tiled=True).reshape(
        request_total, span_rows, local_heads * DH
    )
    width_heads = local_heads * DH
    acc_out, stat_out = local_attention(
        sorted_owner,
        sorted_page,
        sorted_limit,
        sorted_offset,
        sorted_fresh,
        everyone,
        cache_k,
        cache_v,
        new_keys.reshape(1, tok_rows, width_heads),
        new_values.reshape(1, tok_rows, width_heads),
        local_heads,
        request_total,
    )
    visited = jnp.any(
        sorted_owner[:, None] == jnp.arange(request_total, dtype=jnp.int32)[None, :], axis=0
    )
    stat_init = jnp.where(jnp.arange(2 * local_heads) < local_heads, NEGATIVE, 0.0)
    acc_req = jnp.where(visited[:, None, None, None], acc_out, 0.0)
    stats = jnp.where(visited[:, None, None], stat_out, stat_init[None, :, None])
    quarters = span_rows // tok_rows
    quarter_bits = quarters.bit_length() - 1
    request_bits = request_total.bit_length() - 1
    acc_req = acc_req.reshape(
        (2,) * request_bits + (local_heads, DH) + (2,) * quarter_bits + (tok_rows,)
    )
    stats = stats.reshape((2,) * request_bits + (2 * local_heads,) + (2,) * quarter_bits + (tok_rows,))
    bit_names = [quarter_bits + k for k in range(request_bits - 1, -1, -1)]
    bit_names += list(range(quarter_bits - 1, -1, -1))
    acc_names = bit_names[:request_bits] + ["h", "d"] + bit_names[request_bits:] + ["q"]
    stat_names = bit_names[:request_bits] + ["s"] + bit_names[request_bits:] + ["q"]
    bit_count = request_bits + quarter_bits
    for bit in ([0, 1, 3, 2, 4, 5] if bit_count == 6 else list(range(bit_count))):
        acc_axis = acc_names.index(bit)
        stat_axis = stat_names.index(bit)
        acc_names.pop(acc_axis)
        stat_names.pop(stat_axis)
        own_bit = (seq_index >> bit) & 1
        keep_acc = lax.dynamic_index_in_dim(acc_req, own_bit, acc_axis, keepdims=False)
        send_acc = lax.dynamic_index_in_dim(acc_req, 1 - own_bit, acc_axis, keepdims=False)
        keep_stats = lax.dynamic_index_in_dim(stats, own_bit, stat_axis, keepdims=False)
        send_stats = lax.dynamic_index_in_dim(stats, 1 - own_bit, stat_axis, keepdims=False)
        pairs = [(source, source ^ (1 << bit)) for source in range(seq_count)]
        got_acc = lax.ppermute(send_acc.astype(jnp.bfloat16), "seq", pairs).astype(jnp.float32)
        got_stats = lax.ppermute(send_stats, "seq", pairs)
        s_axis = stat_names.index("s")
        keep_m = lax.slice_in_dim(keep_stats, 0, local_heads, axis=s_axis)
        keep_l = lax.slice_in_dim(keep_stats, local_heads, 2 * local_heads, axis=s_axis)
        got_m = lax.slice_in_dim(got_stats, 0, local_heads, axis=s_axis)
        got_l = lax.slice_in_dim(got_stats, local_heads, 2 * local_heads, axis=s_axis)
        m_new = jnp.maximum(keep_m, got_m)
        keep_factor = jnp.exp(keep_m - m_new)
        got_factor = jnp.exp(got_m - m_new)
        l_new = keep_l * keep_factor + got_l * got_factor
        d_axis = acc_names.index("d")
        acc_req = keep_acc * jnp.expand_dims(keep_factor, d_axis) + got_acc * jnp.expand_dims(
            got_factor, d_axis
        )
        stats = jnp.concatenate([m_new, l_new], axis=s_axis)
    attention = acc_req / stats[local_heads:][:, None, :]
    attention = jnp.transpose(attention, (2, 0, 1)).reshape(tok_rows, -1).astype(jnp.bfloat16)
    tp_count = lax.axis_size("tp")
    tp_index = lax.axis_index("tp")

    def tp_gather(value, axis):
        pieces = [value] + [
            lax.ppermute(value, "tp", [(i, (i + k) % tp_count) for i in range(tp_count)])
            for k in range(1, tp_count)
        ]
        stacked = jnp.stack(pieces, axis=0)
        ordered = jnp.take(stacked, (tp_index - jnp.arange(tp_count)) % tp_count, axis=0)
        return jnp.concatenate([ordered[j] for j in range(tp_count)], axis=axis)

    full_attention = tp_gather(attention, 1)
    full_w_out = tp_gather(w_out, 0)
    mid = hidden.astype(jnp.float32) + jnp.dot(
        full_attention, full_w_out, preferred_element_type=jnp.float32
    )
    moe_in = (rms_rows(mid) * moe_gain).astype(jnp.bfloat16)
    logits = jnp.dot(moe_in.astype(jnp.float32), router, precision=lax.Precision.HIGHEST)
    chosen = jax.nn.sigmoid(jnp.take_along_axis(logits, expert_ids, axis=1))
    gates = chosen / jnp.sum(chosen, axis=1, keepdims=True)
    flat_ids = expert_ids.reshape(-1)
    onehot = (flat_ids[:, None] == jnp.arange(EXPERTS, dtype=jnp.int32)[None, :]).astype(jnp.int32)
    ranks = jnp.sum((jnp.cumsum(onehot, axis=0) - 1) * onehot, axis=1)
    target = (flat_ids * CAP + ranks).reshape(tok_rows, TOP)
    hits = target[:, :, None] == jnp.arange(EXPERTS * CAP, dtype=jnp.int32)[None, None, :]
    placing = jnp.any(hits, axis=1).astype(jnp.bfloat16)
    combining = jnp.sum(jnp.where(hits, gates[:, :, None], 0.0), axis=1)
    width = moe_in.shape[1]
    tp_width = width // tp_count
    moe_cols = lax.dynamic_slice_in_dim(moe_in, tp_index * tp_width, tp_width, 1)
    packed = jnp.einsum(
        "te,td->ed", placing, moe_cols, preferred_element_type=jnp.float32
    ).astype(jnp.bfloat16)
    splits = max(1, seq_count // EXPERTS)
    per_device = w_gate_up.shape[0]
    outgoing = jnp.repeat(packed.reshape(EXPERTS, CAP, tp_width), splits, axis=0).reshape(
        seq_count, per_device, CAP, tp_width
    )
    received = lax.all_to_all(outgoing, "seq", split_axis=0, concat_axis=0, tiled=True)
    count = received.shape[2]
    rows = tp_gather(received[:, 0].reshape(-1, tp_width), 1)
    gate = jnp.dot(rows, w_gate_up[0, 0], preferred_element_type=jnp.float32)
    upper = jnp.dot(rows, w_gate_up[0, 1], preferred_element_type=jnp.float32)
    inner = (jax.nn.gelu(gate, approximate=True) * upper).astype(jnp.bfloat16)
    results = jnp.dot(inner, w_down[0], preferred_element_type=jnp.float32).astype(jnp.bfloat16)
    share = lax.dynamic_slice_in_dim(results, tp_index * tp_width, tp_width, 1).astype(
        jnp.float32
    )
    for k in range(1, tp_count):
        target_cols = lax.dynamic_slice_in_dim(
            results, ((tp_index + k) % tp_count) * tp_width, tp_width, 1
        )
        share = share + lax.ppermute(
            target_cols, "tp", [(i, (i + k) % tp_count) for i in range(tp_count)]
        ).astype(jnp.float32)
    produced = share.reshape(seq_count, 1, count, tp_width)
    returned = lax.all_to_all(
        produced.astype(jnp.bfloat16), "seq", split_axis=0, concat_axis=0, tiled=True
    ).astype(jnp.float32)
    folded = jnp.sum(returned.reshape(EXPERTS, splits, CAP, tp_width), axis=1).reshape(
        EXPERTS * CAP, tp_width
    )
    mixture = jnp.dot(combining, folded, precision=lax.Precision.HIGHEST)
    mid_part = lax.dynamic_slice_in_dim(mid, tp_index * tp_width, tp_width, 1)
    return (mid_part + mixture).astype(jnp.bfloat16)

def solution(mesh):
    in_specs = (
        P("seq", None),
        P(),
        P(),
        P("seq", None),
        P(None, "tp"),
        P(None, "tp"),
        P(None, "tp"),
        P("tp", None),
        P("seq", None, "tp"),
        P("seq", None, "tp"),
        P(),
        P(),
        P("seq", None, None, "tp"),
        P("seq", "tp", None),
    )
    out_specs = P("seq", "tp")
    return jax.shard_map(shards, mesh=mesh, in_specs=in_specs, out_specs=out_specs, check_vma=False)
```

profile of v0, /device:TPU:1, one launch (start us, length us, event | category | flops | bytes accessed | tf_op | source)
XLA Modules:
  0.0 392.8 jit_solution(2203596004921879752)
XLA Ops:
  7.8 2.1 convolution_convert_fusion.4
  21.1 72.2 %all-gather.2.cloned.1.call-done = bf16[8192,256]{1,0:T(8,128)(2,1)} async-done(((bf16[128,256]{1,0:T(8,128)(2,1)}), bf16[8192,256]{1,0:T(8,128)(2,1)}) %all-gather.2.cloned.1.call-update) | async-done | bytes 4194320 | tf_op jit(solution)/shard_map/all_gather | solution.py:188
  93.3 48.9 %shard_map.136 = (f32[16,4,64,512]{3,2,1,0:T(8,128)}, f32[16,8,512]{2,1,0:T(8,128)}) custom-call(s32[34]{0:T(128)} %copy-done.11, s32[34]{0:T(128)} %get-tuple-element.65.page_ref, s32[34]{0:T(128)} %gather_fusion.2, s32[34]{0:T(128)} %gather_fusion.3, s32[34]{0:T(128)} %compare_convert_fusion.fresh_ref, bf16[16,512,256]{2,1,0:T(8,128)(2,1)} %bitcast.180, ...), custom_call_target="tpu_custom_call" | custom-call | tf_op jit(solution)/shard_map/pallas_call | solution.py:114
  142.2 8.6 %broadcast_select_fusion = f32[16,4,64,512]{3,2,1,0:T(8,128)} fusion(f32[16,4,64,512]{3,2,1,0:T(8,128)} %get-tuple-element.9, pred[16]{0:T(512)(128)(4,1)S(1)} %fusion.84), kind=kLoop, calls=%fused_computation.11 | loop fusion | flops 2097152 | bytes 16777232 | tf_op jit(solution)/shard_map/jit(_where)/select_n | solution.py:210
  150.8 10.6 %reshape.272 = f32[2,2,2,2,4,64,2,2,128]{8,7,6,5,4,3,2,1,0:T(2,128)} reshape(f32[16,4,64,512]{3,2,1,0:T(8,128)} %broadcast_select_fusion) | data formatting | bytes 16777216 | tf_op jit(solution)/shard_map/reshape | solution.py:215
  161.3 9.8 %constant_dynamic-slice_fusion.6 = bf16[2,2,2,2,4,64,2,1,128]{8,7,6,5,4,3,2,1,0:T(2,128)(2,1)} fusion(f32[2,2,2,2,4,64,2,2,128]{8,7,6,5,4,3,2,1,0:T(2,128)} %reshape.272, s32[]{:T(128)S(6)} %select_n.246), kind=kLoop, calls=%fused_computation.177 | loop fusion | bytes 4194308 | tf_op jit(solution)/shard_map/jit(dynamic_index_in_dim)/dynamic_slice | solution.py:231
  171.2 2.8 copy.100
  175.6 2.4 collective-permute-start.16
  182.4 9.8 %constant_dynamic-slice_fusion.7 = f32[2,2,2,2,4,64,2,1,128]{8,7,6,5,4,3,2,1,0:T(1,128)} fusion(f32[2,2,2,2,4,64,2,2,128]{8,7,6,5,4,3,2,1,0:T(2,128)} %reshape.272, s32[]{:T(128)S(6)} %select_n.243), kind=kLoop, calls=%fused_computation.178 | loop fusion | bytes 8388612 | tf_op jit(solution)/shard_map/jit(dynamic_index_in_dim)/dynamic_slice | solution.py:230
  192.3 4.2 %fusion = f32[2,2,2,2,4,64,2,128]{7,5,6,4,3,2,1,0:T(8,128)S(1)} fusion(f32[2,2,2,2,4,64,2,1,128]{8,7,6,5,4,3,2,1,0:T(1,128)} %constant_dynamic-slice_fusion.7, bf16[2,2,2,2,4,64,2,128]{7,5,6,4,3,2,1,0:T(8,128)(2,1)} %collective-permute-done.1, f32[2,2,2,2,4,2,128]{6,5,4,3,2,1,0:T(2,128)S(1)} %copy.84, f32[2,2,2,2,4,2,128]{6,5,4,3,2,1,0:T(2,128)S(1)} %copy.82), kind=kLoop, calls=%fused_computation.10 | loop fusion | flops 4194304 | bytes 10616832 | tf_op jit(solution)/shard_map/add | solution.py:247
  201.4 3.1 pad_maximum_fusion
  204.5 2.3 gather_fusion.5
  206.8 19.2 %collective-permute-done.2 = f32[2,2,2,2,8,128]{5,4,3,2,1,0:T(8,128)S(1)} collective-permute-done((f32[2,2,2,2,8,128]{5,4,3,2,1,0:T(8,128)S(1)}, f32[2,2,2,2,8,128]{5,4,3,2,1,0:T(8,128)S(1)}, u32[]{:S(2)}, u32[]{:S(2)}) %collective-permute-start.2) | collective-permute-done | bytes 65568 | tf_op jit(solution)/shard_map/ppermute | solution.py:236
  226.7 2.5 fusion.10
  232.1 9.6 %collective-permute-done.5 = bf16[2,2,2,4,64,128]{5,4,3,2,1,0:T(8,128)(2,1)S(1)} collective-permute-done((bf16[2,2,2,4,64,128]{5,4,3,2,1,0:T(8,128)(2,1)S(1)}, bf16[2,2,2,4,64,128]{5,4,3,2,1,0:T(8,128)(2,1)S(1)}, u32[]{:S(2)}, u32[]{:S(2)}) %collective-permute-start.5) | collective-permute-done | bytes 524320 | tf_op jit(solution)/shard_map/ppermute | solution.py:235
  242.0 10.6 %collective-permute-start.7 = (bf16[2,2,4,64,128]{4,3,2,1,0:T(8,128)(2,1)S(1)}, bf16[2,2,4,64,128]{4,3,2,1,0:T(8,128)(2,1)S(1)}, u32[]{:S(2)}, u32[]{:S(2)}) collective-permute-start(bf16[2,2,4,64,128]{4,3,2,1,0:T(8,128)(2,1)S(1)} %fusion.45), channel_id=1, source_target_pairs={{0,16},{4,20},{8,24},{12,28},{16,0},{20,4},{24,8},{28,12},{32,48},... | collective-permute-start | bytes 786440 | tf_op jit(solution)/shard_map/ppermute | solution.py:235
  252.6 2.2 collective-permute-start.8
  254.9 3.5 collective-permute-done.7
  260.3 2.9 collective-permute-start.10
  264.8 2.7 collective-permute-start.11
  267.5 4.4 %collective-permute-done.11 = bf16[4,64,128]{2,1,0:T(8,128)(2,1)S(1)} collective-permute-done((bf16[4,64,128]{2,1,0:T(8,128)(2,1)S(1)}, bf16[4,64,128]{2,1,0:T(8,128)(2,1)S(1)}, u32[]{:S(2)}, u32[]{:S(2)}) %collective-permute-start.11) | collective-permute-done | bytes 65568 | tf_op jit(solution)/shard_map/ppermute | solution.py:235
  281.9 30.5 %all_to_all.10 = bf16[64,1,10,256]{3,2,1,0:T(8,128)(2,1)S(1)} all-to-all(bf16[64,1,10,256]{3,2,1,0:T(8,128)(2,1)S(1)} %bitcast.183), channel_id=1, replica_groups=mesh['seq'=64,'tp'=4] {'seq'}, dimensions={0} | all-to-all | bytes 655360 | tf_op jit(solution)/shard_map/all_to_all | solution.py:292
  313.6 2.4 collective-permute-start.19
  316.2 6.4 %collective-permute-done.18 = bf16[640,256]{1,0:T(8,128)(2,1)S(1)} collective-permute-done((bf16[640,256]{1,0:T(8,128)(2,1)S(1)}, bf16[640,256]{1,0:T(8,128)(2,1)S(1)}, u32[]{:S(2)}, u32[]{:S(2)}) %collective-permute-start.18) | collective-permute-done | bytes 327712 | tf_op jit(solution)/shard_map/ppermute | solution.py:258
  322.7 7.8 %collective-permute-done.19 = bf16[640,256]{1,0:T(8,128)(2,1)S(1)} collective-permute-done((bf16[640,256]{1,0:T(8,128)(2,1)S(1)}, bf16[640,256]{1,0:T(8,128)(2,1)S(1)}, u32[]{:S(2)}, u32[]{:S(2)}) %collective-permute-start.19) | collective-permute-done | bytes 327712 | tf_op jit(solution)/shard_map/ppermute | solution.py:258
  334.3 3.2 convolution_convert_fusion
  340.0 2.7 collective-permute-start.22
  343.0 5.6 %collective-permute-done.21 = bf16[640,256]{1,0:T(8,128)(2,1)S(1)} collective-permute-done((bf16[640,256]{1,0:T(8,128)(2,1)}, bf16[640,256]{1,0:T(8,128)(2,1)S(1)}, u32[]{:S(2)}, u32[]{:S(2)}) %collective-permute-start.21) | collective-permute-done | bytes 327712 | tf_op jit(solution)/shard_map/ppermute | solution.py:306
  348.6 8.7 %collective-permute-done.22 = bf16[640,256]{1,0:T(8,128)(2,1)} collective-permute-done((bf16[640,256]{1,0:T(8,128)(2,1)S(1)}, bf16[640,256]{1,0:T(8,128)(2,1)}, u32[]{:S(2)}, u32[]{:S(2)}) %collective-permute-start.22) | collective-permute-done | bytes 327712 | tf_op jit(solution)/shard_map/ppermute | solution.py:306
  359.6 6.3 %all-to-all-start.1 = ((bf16[64,1,10,256]{3,2,1,0:T(8,128)(2,1)}), bf16[64,1,10,256]{3,2,1,0:T(8,128)(2,1)S(1)}, u32[]{:S(2)}, u32[]{:S(2)}) async-start(bf16[64,1,10,256]{3,2,1,0:T(8,128)(2,1)} %bitcast.66), calls=%async_computation.1 | async-start | bytes 1048576 | tf_op jit(solution)/shard_map/all_to_all | solution.py:310
  369.4 14.1 %all-to-all-done.1 = bf16[64,1,10,256]{3,2,1,0:T(8,128)(2,1)S(1)} async-done(((bf16[64,1,10,256]{3,2,1,0:T(8,128)(2,1)}), bf16[64,1,10,256]{3,2,1,0:T(8,128)(2,1)S(1)}, u32[]{:S(2)}, u32[]{:S(2)}) %all-to-all-start.1) | async-done | bytes 327712 | tf_op jit(solution)/shard_map/all_to_all | solution.py:310
  383.7 2.0 fusion.15
  (159 shorter events, 54.3 us)
Async XLA Ops:
  6.5 327.7 %copy-start = (bf16[1,352,1024]{2,1,0:T(8,128)(2,1)S(1)}, bf16[1,352,1024]{2,1,0:T(8,128)(2,1)}, u32[]{:S(2)}) copy-start(bf16[1,352,1024]{2,1,0:T(8,128)(2,1)} %param.27) | copy-start | bytes 2162692
  6.5 12.2 %copy-start.2 = (bf16[128,1024]{1,0:T(8,128)(2,1)S(1)}, bf16[128,1024]{1,0:T(8,128)(2,1)}, u32[]{:S(2)}) copy-start(bf16[128,1024]{1,0:T(8,128)(2,1)} %param.14) | copy-start | bytes 786436
  6.5 12.2 %copy-start.6 = (bf16[1024,256]{1,0:T(8,128)(2,1)S(1)}, bf16[1024,256]{1,0:T(8,128)(2,1)}, u32[]{:S(2)}) copy-start(bf16[1024,256]{1,0:T(8,128)(2,1)} %param.19) | copy-start | bytes 1572868
  6.5 86.8 %all-gather.2.cloned.1.call-start = ((), (), s32[]{:S(2)}) async-start(), calls=%async_computation.2 | async-start | bytes 4259840 | tf_op jit(solution)/shard_map/all_gather | solution.py:188
  7.7 11.9 %copy-start.7 = (bf16[1024,256]{1,0:T(8,128)(2,1)S(1)}, bf16[1024,256]{1,0:T(8,128)(2,1)}, u32[]{:S(2)}) copy-start(bf16[1024,256]{1,0:T(8,128)(2,1)} %param.20) | copy-start | bytes 1572868
  15.9 77.4 %copy-start.11 = (s32[34]{0:T(128)}, s32[34]{0:T(128)S(1)}, u32[]{:S(2)}) copy-start(s32[34]{0:T(128)S(1)} %gather_fusion) | copy-start | bytes 412
  174.0 18.3 %collective-permute-start.1 = (bf16[2,2,2,2,4,64,2,128]{7,5,6,4,3,2,1,0:T(8,128)(2,1)S(1)}, bf16[2,2,2,2,4,64,2,128]{7,5,6,4,3,2,1,0:T(8,128)(2,1)}, u32[]{:S(2)}, u32[]{:S(2)}) collective-permute-start(bf16[2,2,2,2,4,64,2,128]{7,5,6,4,3,2,1,0:T(8,128)(2,1)S(1)} %bitcast.181), channel_id=1, source_target_pairs={{0,4},{4,0},{8,12},{12,8},{16,20},{20,16},{24,28},{28,24},{32,36},... | collective-permute-start | bytes 6291464 | tf_op jit(solution)/shard_map/ppermute | solution.py:235
  174.4 27.0 %collective-permute-start.15 = (bf16[256,1024]{1,0:T(8,128)(2,1)}, bf16[256,1024]{1,0:T(8,128)(2,1)}, u32[]{:S(2)}, u32[]{:S(2)}) collective-permute-start(bf16[256,1024]{1,0:T(8,128)(2,1)} %param.21), channel_id=1, source_target_pairs={{0,1},{1,2},{2,3},{3,0},{4,5},{5,6},{6,7},{7,4},{8,9},{9,10},{10,1... | collective-permute-start | bytes 1572872 | tf_op jit(solution)/shard_map/ppermute | solution.py:258
  175.6 25.8 %collective-permute-start.16 = (bf16[256,1024]{1,0:T(8,128)(2,1)}, bf16[256,1024]{1,0:T(8,128)(2,1)}, u32[]{:S(2)}, u32[]{:S(2)}) collective-permute-start(bf16[256,1024]{1,0:T(8,128)(2,1)} %param.21), channel_id=1, source_target_pairs={{0,2},{1,3},{2,0},{3,1},{4,6},{5,7},{6,4},{7,5},{8,10},{9,11},{10,... | collective-permute-start | bytes 1572872 | tf_op jit(solution)/shard_map/ppermute | solution.py:258
  178.0 23.4 %collective-permute-start.17 = (bf16[256,1024]{1,0:T(8,128)(2,1)}, bf16[256,1024]{1,0:T(8,128)(2,1)}, u32[]{:S(2)}, u32[]{:S(2)}) collective-permute-start(bf16[256,1024]{1,0:T(8,128)(2,1)} %param.21), channel_id=1, source_target_pairs={{0,3},{1,0},{2,1},{3,2},{4,7},{5,4},{6,5},{7,6},{8,11},{9,8},{10,9... | collective-permute-start | bytes 1572872 | tf_op jit(solution)/shard_map/ppermute | solution.py:258
  181.2 10.9 %collective-permute-start = (f32[2,2,2,2,8,2,128]{6,4,5,3,2,1,0:T(8,128)S(1)}, f32[2,2,2,2,8,2,128]{6,4,5,3,2,1,0:T(8,128)S(1)}, u32[]{:S(2)}, u32[]{:S(2)}) collective-permute-start(f32[2,2,2,2,8,2,128]{6,4,5,3,2,1,0:T(8,128)S(1)} %get-tuple-element.52), channel_id=1, source_target_pairs={{0,4},{4,0},{8,12},{12,8},{16,20},{20,16},{24,28},{28,24},{32,36},... | collective-permute-start | bytes 393224 | tf_op jit(solution)/shard_map/ppermute | solution.py:236
  199.7 26.9 %collective-permute-start.3 = (bf16[2,2,2,2,4,64,128]{6,5,4,3,2,1,0:T(8,128)(2,1)}, bf16[2,2,2,2,4,64,128]{6,5,4,3,2,1,0:T(8,128)(2,1)}, u32[]{:S(2)}, u32[]{:S(2)}) collective-permute-start(bf16[2,2,2,2,4,64,128]{6,5,4,3,2,1,0:T(8,128)(2,1)} %fusion.18), channel_id=1, source_target_pairs={{0,8},{4,12},{8,0},{12,4},{16,24},{20,28},{24,16},{28,20},{32,40},... | collective-permute-start | bytes 3145736 | tf_op jit(solution)/shard_map/ppermute | solution.py:235
  199.8 26.2 %collective-permute-start.2 = (f32[2,2,2,2,8,128]{5,4,3,2,1,0:T(8,128)S(1)}, f32[2,2,2,2,8,128]{5,4,3,2,1,0:T(8,128)S(1)}, u32[]{:S(2)}, u32[]{:S(2)}) collective-permute-start(f32[2,2,2,2,8,128]{5,4,3,2,1,0:T(8,128)S(1)} %get-tuple-element.54), channel_id=1, source_target_pairs={{0,8},{4,12},{8,0},{12,4},{16,24},{20,28},{24,16},{28,20},{32,40},... | collective-permute-start | bytes 196616 | tf_op jit(solution)/shard_map/ppermute | solution.py:236
  226.1 4.5 %collective-permute-start.4 = (f32[2,2,2,8,128]{4,3,2,1,0:T(8,128)S(1)}, f32[2,2,2,8,128]{4,3,2,1,0:T(8,128)S(1)}, u32[]{:S(2)}, u32[]{:S(2)}) collective-permute-start(f32[2,2,2,8,128]{4,3,2,1,0:T(8,128)S(1)} %get-tuple-element.56), channel_id=1, source_target_pairs={{0,32},{4,36},{8,40},{12,44},{16,48},{20,52},{24,56},{28,60},{32,0... | collective-permute-start | bytes 98312 | tf_op jit(solution)/shard_map/ppermute | solution.py:236
  229.2 12.4 %collective-permute-start.5 = (bf16[2,2,2,4,64,128]{5,4,3,2,1,0:T(8,128)(2,1)S(1)}, bf16[2,2,2,4,64,128]{5,4,3,2,1,0:T(8,128)(2,1)S(1)}, u32[]{:S(2)}, u32[]{:S(2)}) collective-permute-start(bf16[2,2,2,4,64,128]{5,4,3,2,1,0:T(8,128)(2,1)S(1)} %fusion.38), channel_id=1, source_target_pairs={{0,32},{4,36},{8,40},{12,44},{16,48},{20,52},{24,56},{28,60},{32,0... | collective-permute-start | bytes 1572872 | tf_op jit(solution)/shard_map/ppermute | solution.py:235
  230.6 21.9 %collective-permute-start.6 = (f32[2,2,8,128]{3,2,1,0:T(8,128)S(1)}, f32[2,2,8,128]{3,2,1,0:T(8,128)S(1)}, u32[]{:S(2)}, u32[]{:S(2)}) collective-permute-start(f32[2,2,8,128]{3,2,1,0:T(8,128)S(1)} %get-tuple-element.58), channel_id=1, source_target_pairs={{0,16},{4,20},{8,24},{12,28},{16,0},{20,4},{24,8},{28,12},{32,48},... | collective-permute-start | bytes 49160 | tf_op jit(solution)/shard_map/ppermute | solution.py:236
  242.0 16.4 %collective-permute-start.7 = (bf16[2,2,4,64,128]{4,3,2,1,0:T(8,128)(2,1)S(1)}, bf16[2,2,4,64,128]{4,3,2,1,0:T(8,128)(2,1)S(1)}, u32[]{:S(2)}, u32[]{:S(2)}) collective-permute-start(bf16[2,2,4,64,128]{4,3,2,1,0:T(8,128)(2,1)S(1)} %fusion.45), channel_id=1, source_target_pairs={{0,16},{4,20},{8,24},{12,28},{16,0},{20,4},{24,8},{28,12},{32,48},... | collective-permute-start | bytes 786440 | tf_op jit(solution)/shard_map/ppermute | solution.py:235
  252.6 7.7 %collective-permute-start.8 = (f32[2,8,128]{2,1,0:T(8,128)S(1)}, f32[2,8,128]{2,1,0:T(8,128)S(1)}, u32[]{:S(2)}, u32[]{:S(2)}) collective-permute-start(f32[2,8,128]{2,1,0:T(8,128)S(1)} %get-tuple-element.60), channel_id=1, source_target_pairs={{0,64},{4,68},{8,72},{12,76},{16,80},{20,84},{24,88},{28,92},{32,9... | collective-permute-start | bytes 24584 | tf_op jit(solution)/shard_map/ppermute | solution.py:236
  258.5 6.2 %collective-permute-start.9 = (bf16[2,4,64,128]{3,2,1,0:T(8,128)(2,1)S(1)}, bf16[2,4,64,128]{3,2,1,0:T(8,128)(2,1)S(1)}, u32[]{:S(2)}, u32[]{:S(2)}) collective-permute-start(bf16[2,4,64,128]{3,2,1,0:T(8,128)(2,1)S(1)} %fusion.54), channel_id=1, source_target_pairs={{0,64},{4,68},{8,72},{12,76},{16,80},{20,84},{24,88},{28,92},{32,9... | collective-permute-start | bytes 393224 | tf_op jit(solution)/shard_map/ppermute | solution.py:235
  260.3 7.2 %collective-permute-start.10 = (f32[8,128]{1,0:T(8,128)S(1)}, f32[8,128]{1,0:T(8,128)S(1)}, u32[]{:S(2)}, u32[]{:S(2)}) collective-permute-start(f32[8,128]{1,0:T(8,128)S(1)} %get-tuple-element.62), channel_id=1, source_target_pairs={{0,128},{4,132},{8,136},{12,140},{16,144},{20,148},{24,152},{28,15... | collective-permute-start | bytes 12296 | tf_op jit(solution)/shard_map/ppermute | solution.py:236
  264.8 7.2 %collective-permute-start.11 = (bf16[4,64,128]{2,1,0:T(8,128)(2,1)S(1)}, bf16[4,64,128]{2,1,0:T(8,128)(2,1)S(1)}, u32[]{:S(2)}, u32[]{:S(2)}) collective-permute-start(bf16[4,64,128]{2,1,0:T(8,128)(2,1)S(1)} %fusion.58), channel_id=1, source_target_pairs={{0,128},{4,132},{8,136},{12,140},{16,144},{20,148},{24,152},{28,15... | collective-permute-start | bytes 196616 | tf_op jit(solution)/shard_map/ppermute | solution.py:235
  272.0 4.7 %collective-permute-start.12 = (bf16[128,256]{0,1:T(8,128)(2,1)S(1)}, bf16[128,256]{0,1:T(8,128)(2,1)S(1)}, u32[]{:S(2)}, u32[]{:S(2)}) collective-permute-start(bf16[128,256]{0,1:T(8,128)(2,1)S(1)} %bitcast.188), channel_id=1, source_target_pairs={{0,1},{1,2},{2,3},{3,0},{4,5},{5,6},{6,7},{7,4},{8,9},{9,10},{10,1... | collective-permute-start | bytes 196616 | tf_op jit(solution)/shard_map/ppermute | solution.py:258
  272.4 4.7 %collective-permute-start.13 = (bf16[128,256]{0,1:T(8,128)(2,1)S(1)}, bf16[128,256]{0,1:T(8,128)(2,1)S(1)}, u32[]{:S(2)}, u32[]{:S(2)}) collective-permute-start(bf16[128,256]{0,1:T(8,128)(2,1)S(1)} %bitcast.189), channel_id=1, source_target_pairs={{0,2},{1,3},{2,0},{3,1},{4,6},{5,7},{6,4},{7,5},{8,10},{9,11},{10,... | collective-permute-start | bytes 196616 | tf_op jit(solution)/shard_map/ppermute | solution.py:258
  273.0 4.7 %collective-permute-start.14 = (bf16[128,256]{0,1:T(8,128)(2,1)S(1)}, bf16[128,256]{0,1:T(8,128)(2,1)S(1)}, u32[]{:S(2)}, u32[]{:S(2)}) collective-permute-start(bf16[128,256]{0,1:T(8,128)(2,1)S(1)} %bitcast.190), channel_id=1, source_target_pairs={{0,3},{1,0},{2,1},{3,2},{4,7},{5,4},{6,5},{7,6},{8,11},{9,8},{10,9... | collective-permute-start | bytes 196616 | tf_op jit(solution)/shard_map/ppermute | solution.py:258
  312.5 10.2 %collective-permute-start.18 = (bf16[640,256]{1,0:T(8,128)(2,1)S(1)}, bf16[640,256]{1,0:T(8,128)(2,1)S(1)}, u32[]{:S(2)}, u32[]{:S(2)}) collective-permute-start(bf16[640,256]{1,0:T(8,128)(2,1)S(1)} %reshape_squeeze.3), channel_id=1, source_target_pairs={{0,1},{1,2},{2,3},{3,0},{4,5},{5,6},{6,7},{7,4},{8,9},{9,10},{10,1... | collective-permute-start | bytes 983048 | tf_op jit(solution)/shard_map/ppermute | solution.py:258
  313.6 16.8 %collective-permute-start.19 = (bf16[640,256]{1,0:T(8,128)(2,1)S(1)}, bf16[640,256]{1,0:T(8,128)(2,1)S(1)}, u32[]{:S(2)}, u32[]{:S(2)}) collective-permute-start(bf16[640,256]{1,0:T(8,128)(2,1)S(1)} %reshape_squeeze.3), channel_id=1, source_target_pairs={{0,2},{1,3},{2,0},{3,1},{4,6},{5,7},{6,4},{7,5},{8,10},{9,11},{10,... | collective-permute-start | bytes 983048 | tf_op jit(solution)/shard_map/ppermute | solution.py:258
  316.0 14.4 %collective-permute-start.20 = (bf16[640,256]{1,0:T(8,128)(2,1)S(1)}, bf16[640,256]{1,0:T(8,128)(2,1)S(1)}, u32[]{:S(2)}, u32[]{:S(2)}) collective-permute-start(bf16[640,256]{1,0:T(8,128)(2,1)S(1)} %reshape_squeeze.3), channel_id=1, source_target_pairs={{0,3},{1,0},{2,1},{3,2},{4,7},{5,4},{6,5},{7,6},{8,11},{9,8},{10,9... | collective-permute-start | bytes 983048 | tf_op jit(solution)/shard_map/ppermute | solution.py:258
  338.4 27.5 %copy-start.4 = (bf16[128,1024]{1,0:T(8,128)(2,1)S(1)}, bf16[128,1024]{1,0:T(8,128)(2,1)}, u32[]{:S(2)}) copy-start(bf16[128,1024]{1,0:T(8,128)(2,1)} %copy-done.3) | copy-start | bytes 786436
  338.4 10.3 %collective-permute-start.21 = (bf16[640,256]{1,0:T(8,128)(2,1)}, bf16[640,256]{1,0:T(8,128)(2,1)S(1)}, u32[]{:S(2)}, u32[]{:S(2)}) collective-permute-start(bf16[640,256]{1,0:T(8,128)(2,1)} %get-tuple-element.40), channel_id=1, source_target_pairs={{0,1},{1,2},{2,3},{3,0},{4,5},{5,6},{6,7},{7,4},{8,9},{9,10},{10,1... | collective-permute-start | bytes 983048 | tf_op jit(solution)/shard_map/ppermute | solution.py:306
  340.0 17.4 %collective-permute-start.22 = (bf16[640,256]{1,0:T(8,128)(2,1)S(1)}, bf16[640,256]{1,0:T(8,128)(2,1)}, u32[]{:S(2)}, u32[]{:S(2)}) collective-permute-start(bf16[640,256]{1,0:T(8,128)(2,1)S(1)} %get-tuple-element.42), channel_id=1, source_target_pairs={{0,2},{1,3},{2,0},{3,1},{4,6},{5,7},{6,4},{7,5},{8,10},{9,11},{10,... | collective-permute-start | bytes 983048 | tf_op jit(solution)/shard_map/ppermute | solution.py:306
  342.7 14.6 %collective-permute-start.23 = (bf16[640,256]{1,0:T(8,128)(2,1)S(1)}, bf16[640,256]{1,0:T(8,128)(2,1)}, u32[]{:S(2)}, u32[]{:S(2)}) collective-permute-start(bf16[640,256]{1,0:T(8,128)(2,1)S(1)} %get-tuple-element.41), channel_id=1, source_target_pairs={{0,3},{1,0},{2,1},{3,2},{4,7},{5,4},{6,5},{7,6},{8,11},{9,8},{10,9... | collective-permute-start | bytes 983048 | tf_op jit(solution)/shard_map/ppermute | solution.py:306
  359.6 24.0 %all-to-all-start.1 = ((bf16[64,1,10,256]{3,2,1,0:T(8,128)(2,1)}), bf16[64,1,10,256]{3,2,1,0:T(8,128)(2,1)S(1)}, u32[]{:S(2)}, u32[]{:S(2)}) async-start(bf16[64,1,10,256]{3,2,1,0:T(8,128)(2,1)} %bitcast.66), calls=%async_computation.1 | async-start | bytes 1048576 | tf_op jit(solution)/shard_map/all_to_all | solution.py:310
  (7 other events, 24.6 us)
Sparse Core Ops, SparseCore 0:
  10.1 83.1 all-gather.1
where the time goes:
time: 398 us; the launch traced here: 393 us
  waiting for transfers between devices  155 us (39%)
  local copies, waits for them, and re-layouts  54.6 us (14%)
  Pallas kernels  48.9 us (12%)
  starting transfers between devices  48.6 us (12%)
  blocking collectives  30.5 us (8%)
  other arithmetic  27.2 us (7%)
  between operations  14.2 us (4%)
  matrix products  13.9 us (3%)
    all_gather x1, waiting for transfers between devices, shards(): lax.all_gather(queries, 'seq', axis=0, tiled=True)  72.2 us
    pallas_call x1, Pallas kernels, local_attention(): pl.pallas_call(attend_kernel, grid_spec=grid_spec, out_shape=[jax.ShapeDt...  48.9 us
    all_to_all x1, blocking collectives, shards(): lax.all_to_all(outgoing, 'seq', split_axis=0, concat_axis=0, tiled=True)  30.5 us
    ppermute x6, waiting for transfers between devices, shards(): got_stats = lax.ppermute(send_stats, 'seq', pairs)  19.2 us
    ppermute x6, waiting for transfers between devices, shards(): lax.ppermute(send_acc.astype(jnp.bfloat16), 'seq', pairs)  19 us
    ppermute x6, starting transfers between devices, shards(): lax.ppermute(send_acc.astype(jnp.bfloat16), 'seq', pairs)  16.6 us
    ppermute x9, waiting for transfers between devices, tp_gather(): lax.ppermute(value, 'tp', [(i, (i + k) % tp_count) for i in range(tp_coun...  16 us
    ppermute x3, waiting for transfers between devices, shards(): lax.ppermute(target_cols, 'tp', [(i, (i + k) % tp_count) for i in range(t...  14.4 us
  transfers between devices with their start and end apart: 26, of which 14 were waited for; matrix products, arithmetic and copies ran while one was open for 11% of the time, Pallas kernels for 0%

commit v1 on v0

--- a/solution.py
+++ b/solution.py
@@ -49,21 +49,30 @@
     step = pl.program_id(0)
     owner = own_ref[step]
     first = (step == 0) | (own_ref[jnp.maximum(step - 1, 0)] != owner)
-    heads = acc_ref.shape[1]
+    heads = acc_ref.shape[2]
 
     @pl.when(first)
     def _():
         acc_ref[...] = jnp.zeros(acc_ref.shape, acc_ref.dtype)
-        stat_ref[0, :heads, :] = jnp.full((heads, stat_ref.shape[2]), NEGATIVE, jnp.float32)
-        stat_ref[0, heads:, :] = jnp.zeros((heads, stat_ref.shape[2]), jnp.float32)
+        stat_ref[:, :, :heads, :] = jnp.full(
+            stat_ref.shape[:2] + (heads, stat_ref.shape[3]), NEGATIVE, jnp.float32
+        )
+        stat_ref[:, :, heads:, :] = jnp.zeros(
+            stat_ref.shape[:2] + (heads, stat_ref.shape[3]), jnp.float32
+        )
 
     is_fresh = fresh_ref[step] == 1
     keys = jnp.where(is_fresh, nk_ref[0], k_ref[0])
     vals = jnp.where(is_fresh, nv_ref[0], v_ref[0])
     rows, cols = keys.shape[0], q_ref.shape[1]
+    quarters, piece = acc_ref.shape[0], acc_ref.shape[4]
     k_pos = lax.broadcasted_iota(jnp.int32, (rows, cols), 0)
     q_pos = lax.broadcasted_iota(jnp.int32, (rows, cols), 1)
     valid = (k_pos < limit_ref[step]) & (q_pos >= offset_ref[step] + k_pos)
+
+    def joined(read):
+        return jnp.concatenate([read(c) for c in range(quarters)], axis=1)
+
     for h in range(heads):
         lanes = slice(h * DH, (h + 1) * DH)
         s = lax.dot_general(
@@ -71,23 +80,28 @@
             preferred_element_type=jnp.float32,
         ) * (DH ** (-0.5))
         s = jnp.where(valid, s, NEGATIVE)
-        m_prev = stat_ref[0, h : h + 1, :]
+        m_prev = joined(lambda c: stat_ref[c, 0, h : h + 1, :])
+        l_prev = joined(lambda c: stat_ref[c, 0, heads + h : heads + h + 1, :])
+        acc_prev = joined(lambda c: acc_ref[c, 0, h])
         m_cur = jnp.maximum(m_prev, jnp.max(s, axis=0, keepdims=True))
         p = jnp.where(valid, jnp.exp(s - m_cur), 0.0)
         alpha = jnp.exp(m_prev - m_cur)
-        stat_ref[0, heads + h : heads + h + 1, :] = alpha * stat_ref[
-            0, heads + h : heads + h + 1, :
-        ] + jnp.sum(p, axis=0, keepdims=True)
+        l_cur = alpha * l_prev + jnp.sum(p, axis=0, keepdims=True)
         pv = lax.dot_general(
             vals[:, lanes], p.astype(jnp.bfloat16), (((0,), (0,)), ((), ())),
             preferred_element_type=jnp.float32,
         )
-        acc_ref[0, h] = alpha * acc_ref[0, h] + pv
-        stat_ref[0, h : h + 1, :] = m_cur
+        acc_cur = alpha * acc_prev + pv
+        for c in range(quarters):
+            cut = slice(c * piece, (c + 1) * piece)
+            acc_ref[c, 0, h] = acc_cur[:, cut]
+            stat_ref[c, 0, h : h + 1, :] = m_cur[:, cut]
+            stat_ref[c, 0, heads + h : heads + h + 1, :] = l_cur[:, cut]
 
 
 def local_attention(
-    owner, page, limit, offset, fresh, everyone, cache_k, cache_v, new_k, new_v, heads, requests
+    owner, page, limit, offset, fresh, everyone, cache_k, cache_v, new_k, new_v, heads, requests,
+    piece,
 ):
     span_rows, width = everyone.shape[1], everyone.shape[2]
     page_rows = cache_k.shape[1]
@@ -95,7 +109,9 @@
     by_owner = lambda b, own, pg, lim, off, fr: (own[b], 0, 0)
     by_page = lambda b, own, pg, lim, off, fr: (pg[b], 0, 0)
     fixed = lambda b, own, pg, lim, off, fr: (0, 0, 0)
-    acc_map = lambda b, own, pg, lim, off, fr: (own[b], 0, 0, 0)
+    acc_map = lambda b, own, pg, lim, off, fr: (0, own[b], 0, 0, 0)
+    stat_map = lambda b, own, pg, lim, off, fr: (0, own[b], 0, 0)
+    quarters = span_rows // piece
     grid_spec = pltpu.PrefetchScalarGridSpec(
         num_scalar_prefetch=5,
         grid=(blocks,),
@@ -107,16 +123,16 @@
             pl.BlockSpec((1, page_rows, width), fixed),
         ],
         out_specs=[
-            pl.BlockSpec((1, heads, DH, span_rows), acc_map),
-            pl.BlockSpec((1, 2 * heads, span_rows), by_owner),
+            pl.BlockSpec((quarters, 1, heads, DH, piece), acc_map),
+            pl.BlockSpec((quarters, 1, 2 * heads, piece), stat_map),
         ],
     )
     return pl.pallas_call(
         attend_kernel,
         grid_spec=grid_spec,
         out_shape=[
-            jax.ShapeDtypeStruct((requests, heads, DH, span_rows), jnp.float32),
-            jax.ShapeDtypeStruct((requests, 2 * heads, span_rows), jnp.float32),
+            jax.ShapeDtypeStruct((quarters, requests, heads, DH, piece), jnp.float32),
+            jax.ShapeDtypeStruct((quarters, requests, 2 * heads, piece), jnp.float32),
         ],
         compiler_params=pltpu.CompilerParams(dimension_semantics=("arbitrary",)),
     )(owner, page, limit, offset, fresh, everyone, cache_k, cache_v, new_k, new_v)
@@ -202,24 +218,23 @@
         new_values.reshape(1, tok_rows, width_heads),
         local_heads,
         request_total,
+        tok_rows,
     )
     visited = jnp.any(
         sorted_owner[:, None] == jnp.arange(request_total, dtype=jnp.int32)[None, :], axis=0
     )
     stat_init = jnp.where(jnp.arange(2 * local_heads) < local_heads, NEGATIVE, 0.0)
-    acc_req = jnp.where(visited[:, None, None, None], acc_out, 0.0)
-    stats = jnp.where(visited[:, None, None], stat_out, stat_init[None, :, None])
+    acc_req = jnp.where(visited[None, :, None, None, None], acc_out, 0.0)
+    stats = jnp.where(visited[None, :, None, None], stat_out, stat_init[None, None, :, None])
     quarters = span_rows // tok_rows
     quarter_bits = quarters.bit_length() - 1
     request_bits = request_total.bit_length() - 1
-    acc_req = acc_req.reshape(
-        (2,) * request_bits + (local_heads, DH) + (2,) * quarter_bits + (tok_rows,)
-    )
-    stats = stats.reshape((2,) * request_bits + (2 * local_heads,) + (2,) * quarter_bits + (tok_rows,))
-    bit_names = [quarter_bits + k for k in range(request_bits - 1, -1, -1)]
-    bit_names += list(range(quarter_bits - 1, -1, -1))
-    acc_names = bit_names[:request_bits] + ["h", "d"] + bit_names[request_bits:] + ["q"]
-    stat_names = bit_names[:request_bits] + ["s"] + bit_names[request_bits:] + ["q"]
+    acc_req = acc_req.reshape((2,) * (quarter_bits + request_bits) + (local_heads, DH, tok_rows))
+    stats = stats.reshape((2,) * (quarter_bits + request_bits) + (2 * local_heads, tok_rows))
+    bit_names = list(range(quarter_bits - 1, -1, -1))
+    bit_names += [quarter_bits + k for k in range(request_bits - 1, -1, -1)]
+    acc_names = bit_names + ["h", "d", "q"]
+    stat_names = bit_names + ["s", "q"]
     bit_count = request_bits + quarter_bits
     for bit in ([0, 1, 3, 2, 4, 5] if bit_count == 6 else list(range(bit_count))):
         acc_axis = acc_names.index(bit)

time: 398 us -> 350 us (0.88); the launches traced: 393 us -> 350 us
  local copies, waits for them, and re-layouts: 54.6 us -> 24.5 us
  starting transfers between devices: 48.6 us -> 39.3 us
  other arithmetic: 27.2 us -> 22.8 us
    dynamic_slice x2 -> x0, local copies, waits for them, and re-layouts: 19.6 us -> none  [the longest x1 9.84 us: shards(): lax.dynamic_index_in_dim(acc_req, 1 - own_bit, acc_axis, keepdims=False)]
    reshape x1 -> x0, local copies, waits for them, and re-layouts: 10.6 us -> none  [shards(): acc_req.reshape((2,) * request_bits + (local_heads, DH) + (2,) * quarter_...]
    ppermute x9, waiting for transfers between devices: 16 us -> 25.4 us  [tp_gather(): lax.ppermute(value, 'tp', [(i, (i + k) % tp_count) for i in range(tp_coun...]
    ppermute x6, starting transfers between devices: 16.6 us -> 7.42 us  [shards(): lax.ppermute(send_acc.astype(jnp.bfloat16), 'seq', pairs)]
    ppermute x6, waiting for transfers between devices: 19.2 us -> 10.2 us  [shards(): got_stats = lax.ppermute(send_stats, 'seq', pairs)]
    select_n x2, other arithmetic: 8.67 us -> 4.54 us  [the longest x1 4.44 us: shards(): acc_req = jnp.where(visited[None, :, None, None, None], acc_out, 0.0)]
    unnamed x29 -> x34, local copies, waits for them, and re-layouts: 8.11 us -> 8.55 us
  transfers between devices with their start and end apart: 26 -> 26, of which waited for: 14 -> 16; matrix products, arithmetic and copies ran while one was open for 11% -> 9% of each run, Pallas kernels for 0% -> 0%
where the time goes in v1:
time: 350 us
  waiting for transfers between devices  156 us (45%)
  Pallas kernels  49.2 us (14%)
  starting transfers between devices  39.3 us (11%)
  blocking collectives  31.2 us (9%)
  local copies, waits for them, and re-layouts  24.5 us (7%)
  other arithmetic  22.8 us (7%)
  between operations  14 us (4%)
  matrix products  13 us (4%)
    all_gather x1, waiting for transfers between devices, shards(): lax.all_gather(queries, 'seq', axis=0, tiled=True)  72.1 us
    pallas_call x1, Pallas kernels, local_attention(): pl.pallas_call(attend_kernel, grid_spec=grid_spec, out_shape=[jax.ShapeDt...  49.2 us
    all_to_all x1, blocking collectives, shards(): lax.all_to_all(outgoing, 'seq', split_axis=0, concat_axis=0, tiled=True)  31.2 us
    ppermute x9, waiting for transfers between devices, tp_gather(): lax.ppermute(value, 'tp', [(i, (i + k) % tp_count) for i in range(tp_coun...  25.4 us
    ppermute x6, waiting for transfers between devices, shards(): lax.ppermute(send_acc.astype(jnp.bfloat16), 'seq', pairs)  18.8 us
    all_to_all x1, waiting for transfers between devices, shards(): lax.all_to_all(produced.astype(jnp.bfloat16), 'seq', split_axis=0, concat...  15 us
    ppermute x3, waiting for transfers between devices, shards(): lax.ppermute(target_cols, 'tp', [(i, (i + k) % tp_count) for i in range(t...  14.1 us
    ppermute x9, starting transfers between devices, tp_gather(): lax.ppermute(value, 'tp', [(i, (i + k) % tp_count) for i in range(tp_coun...  11.3 us
  transfers between devices with their start and end apart: 26, of which 16 were waited for; matrix products, arithmetic and copies ran while one was open for 9% of the time, Pallas kernels for 0%

profile of v1, /device:TPU:1, one launch (start us, length us, event | category | flops | bytes accessed | tf_op | source)
XLA Modules:
  0.0 349.6 jit_solution(4042432558156587168)
XLA Ops:
  7.8 2.1 convolution_convert_fusion.4
  12.5 2.1 sort.17
  21.2 72.1 %all-gather.2.cloned.1.call-done = bf16[8192,256]{1,0:T(8,128)(2,1)} async-done(((bf16[128,256]{1,0:T(8,128)(2,1)}), bf16[8192,256]{1,0:T(8,128)(2,1)}) %all-gather.2.cloned.1.call-update) | async-done | bytes 4194320 | tf_op jit(solution)/shard_map/all_gather | solution.py:204
  93.3 49.2 %shard_map.136 = (f32[4,16,4,64,128]{4,3,2,1,0:T(8,128)}, f32[4,16,8,128]{3,2,1,0:T(8,128)}) custom-call(s32[34]{0:T(128)} %copy-done.14, s32[34]{0:T(128)} %get-tuple-element.65.page_ref, s32[34]{0:T(128)} %gather_fusion.2, s32[34]{0:T(128)} %gather_fusion.3, s32[34]{0:T(128)} %compare_convert_fusion.fresh_ref, bf16[16,512,256]{2,1,0:T(8,128)(2,1)} %bitcast.180, ...), custom_call_target="tpu_custom_call" | custom-call | tf_op jit(solution)/shard_map/pallas_call | solution.py:130
  142.5 4.4 %broadcast_select_fusion = f32[4,16,4,64,128]{4,3,2,1,0:T(8,128)S(1)} fusion(f32[4,16,4,64,128]{4,3,2,1,0:T(8,128)} %get-tuple-element.9, pred[16]{0:T(512)(128)(4,1)S(1)} %fusion.84), kind=kLoop, calls=%fused_computation.11 | loop fusion | flops 2097152 | bytes 16777232 | tf_op jit(solution)/shard_map/jit(_where)/select_n | solution.py:227
  147.0 3.2 copy-done.2
  152.3 2.4 collective-permute-start.16
  159.6 4.0 %fusion = f32[2,2,2,2,2,4,64,128]{7,6,5,4,3,2,1,0:T(8,128)S(1)} fusion(bf16[2,2,2,2,2,4,64,128]{7,6,5,4,3,2,1,0:T(8,128)(2,1)} %collective-permute-done.1, f32[2,2,2,2,2,2,4,64,128]{8,7,6,5,4,3,2,1,0:T(8,128)} %bitcast.179, s32[]{:T(128)S(6)} %select_n.243, f32[2,2,2,2,2,4,128]{6,5,4,3,2,1,0:T(4,128)S(1)} %get-tuple-element.34, ...), kind=kLoop, calls=%fused_computation.9 | loop fusion | flops 4194304 | bytes 10616836 | tf_op jit(solution)/shard_map/add | solution.py:262
  163.6 1.9 copy-done.3
  168.5 9.5 %collective-permute-done.16 = bf16[256,1024]{1,0:T(8,128)(2,1)} collective-permute-done((bf16[256,1024]{1,0:T(8,128)(2,1)}, bf16[256,1024]{1,0:T(8,128)(2,1)}, u32[]{:S(2)}, u32[]{:S(2)}) %collective-permute-start.16) | collective-permute-done | bytes 524320 | tf_op jit(solution)/shard_map/ppermute | solution.py:273
  178.0 3.1 pad_maximum_fusion
  181.1 2.3 gather_fusion.5
  183.4 9.5 %collective-permute-done.2 = f32[2,2,2,2,8,128]{5,4,3,2,1,0:T(8,128)S(1)} collective-permute-done((f32[2,2,2,2,8,128]{5,4,3,2,1,0:T(8,128)S(1)}, f32[2,2,2,2,8,128]{5,4,3,2,1,0:T(8,128)S(1)}, u32[]{:S(2)}, u32[]{:S(2)}) %collective-permute-start.2) | collective-permute-done | bytes 65568 | tf_op jit(solution)/shard_map/ppermute | solution.py:251
  193.7 2.5 fusion.10
  199.0 9.4 %collective-permute-done.5 = bf16[2,2,2,4,64,128]{5,4,3,2,1,0:T(8,128)(2,1)S(1)} collective-permute-done((bf16[2,2,2,4,64,128]{5,4,3,2,1,0:T(8,128)(2,1)S(1)}, bf16[2,2,2,4,64,128]{5,4,3,2,1,0:T(8,128)(2,1)S(1)}, u32[]{:S(2)}, u32[]{:S(2)}) %collective-permute-start.5) | collective-permute-done | bytes 524320 | tf_op jit(solution)/shard_map/ppermute | solution.py:250
  210.4 2.2 collective-permute-start.8
  212.6 3.3 collective-permute-done.7
  217.9 2.9 collective-permute-start.10
  222.4 2.6 collective-permute-start.11
  225.0 4.5 %collective-permute-done.11 = bf16[4,64,128]{2,1,0:T(8,128)(2,1)S(1)} collective-permute-done((bf16[4,64,128]{2,1,0:T(8,128)(2,1)S(1)}, bf16[4,64,128]{2,1,0:T(8,128)(2,1)S(1)}, u32[]{:S(2)}, u32[]{:S(2)}) %collective-permute-start.11) | collective-permute-done | bytes 65568 | tf_op jit(solution)/shard_map/ppermute | solution.py:250
  239.5 31.2 %all_to_all.10 = bf16[64,1,10,256]{3,2,1,0:T(8,128)(2,1)S(1)} all-to-all(bf16[64,1,10,256]{3,2,1,0:T(8,128)(2,1)S(1)} %bitcast.182), channel_id=1, replica_groups=mesh['seq'=64,'tp'=4] {'seq'}, dimensions={0} | all-to-all | bytes 655360 | tf_op jit(solution)/shard_map/all_to_all | solution.py:307
  271.9 2.2 collective-permute-start.19
  274.5 6.4 %collective-permute-done.18 = bf16[640,256]{1,0:T(8,128)(2,1)S(1)} collective-permute-done((bf16[640,256]{1,0:T(8,128)(2,1)S(1)}, bf16[640,256]{1,0:T(8,128)(2,1)S(1)}, u32[]{:S(2)}, u32[]{:S(2)}) %collective-permute-start.18) | collective-permute-done | bytes 327712 | tf_op jit(solution)/shard_map/ppermute | solution.py:273
  280.9 7.6 %collective-permute-done.19 = bf16[640,256]{1,0:T(8,128)(2,1)S(1)} collective-permute-done((bf16[640,256]{1,0:T(8,128)(2,1)S(1)}, bf16[640,256]{1,0:T(8,128)(2,1)S(1)}, u32[]{:S(2)}, u32[]{:S(2)}) %collective-permute-start.19) | collective-permute-done | bytes 327712 | tf_op jit(solution)/shard_map/ppermute | solution.py:273
  292.4 3.2 convolution_convert_fusion
  297.5 2.7 collective-permute-start.22
  300.5 5.5 %collective-permute-done.21 = bf16[640,256]{1,0:T(8,128)(2,1)S(1)} collective-permute-done((bf16[640,256]{1,0:T(8,128)(2,1)S(1)}, bf16[640,256]{1,0:T(8,128)(2,1)S(1)}, u32[]{:S(2)}, u32[]{:S(2)}) %collective-permute-start.21) | collective-permute-done | bytes 327712 | tf_op jit(solution)/shard_map/ppermute | solution.py:321
  306.0 8.5 %collective-permute-done.22 = bf16[640,256]{1,0:T(8,128)(2,1)S(1)} collective-permute-done((bf16[640,256]{1,0:T(8,128)(2,1)S(1)}, bf16[640,256]{1,0:T(8,128)(2,1)S(1)}, u32[]{:S(2)}, u32[]{:S(2)}) %collective-permute-start.22) | collective-permute-done | bytes 327712 | tf_op jit(solution)/shard_map/ppermute | solution.py:321
  316.6 6.3 %all-to-all-start.1 = ((bf16[64,1,10,256]{3,2,1,0:T(8,128)(2,1)}), bf16[64,1,10,256]{3,2,1,0:T(8,128)(2,1)S(1)}, u32[]{:S(2)}, u32[]{:S(2)}) async-start(bf16[64,1,10,256]{3,2,1,0:T(8,128)(2,1)} %bitcast.67), calls=%async_computation.1 | async-start | bytes 1048576 | tf_op jit(solution)/shard_map/all_to_all | solution.py:325
  323.3 2.0 gather_fusion.7
  325.6 15.0 %all-to-all-done.1 = bf16[64,1,10,256]{3,2,1,0:T(8,128)(2,1)S(1)} async-done(((bf16[64,1,10,256]{3,2,1,0:T(8,128)(2,1)}), bf16[64,1,10,256]{3,2,1,0:T(8,128)(2,1)S(1)}, u32[]{:S(2)}, u32[]{:S(2)}) %all-to-all-start.1) | async-done | bytes 327712 | tf_op jit(solution)/shard_map/all_to_all | solution.py:325
  340.7 2.0 fusion.15
  (160 shorter events, 49.5 us)
Async XLA Ops:
  6.5 285.9 %copy-start = (bf16[1,352,1024]{2,1,0:T(8,128)(2,1)S(1)}, bf16[1,352,1024]{2,1,0:T(8,128)(2,1)}, u32[]{:S(2)}) copy-start(bf16[1,352,1024]{2,1,0:T(8,128)(2,1)} %param.27) | copy-start | bytes 2162692
  6.5 12.3 %copy-start.8 = (bf16[1024,256]{1,0:T(8,128)(2,1)S(1)}, bf16[1024,256]{1,0:T(8,128)(2,1)}, u32[]{:S(2)}) copy-start(bf16[1024,256]{1,0:T(8,128)(2,1)} %param.19) | copy-start | bytes 1572868
  6.5 86.8 %all-gather.2.cloned.1.call-start = ((), (), s32[]{:S(2)}) async-start(), calls=%async_computation.2 | async-start | bytes 4259840 | tf_op jit(solution)/shard_map/all_gather | solution.py:204
  15.9 77.4 %copy-start.14 = (s32[34]{0:T(128)}, s32[34]{0:T(128)S(1)}, u32[]{:S(2)}) copy-start(s32[34]{0:T(128)S(1)} %gather_fusion) | copy-start | bytes 412
  150.7 8.9 %collective-permute-start.1 = (bf16[2,2,2,2,2,4,64,128]{7,6,5,4,3,2,1,0:T(8,128)(2,1)S(1)}, bf16[2,2,2,2,2,4,64,128]{7,6,5,4,3,2,1,0:T(8,128)(2,1)}, u32[]{:S(2)}, u32[]{:S(2)}) collective-permute-start(bf16[2,2,2,2,2,4,64,128]{7,6,5,4,3,2,1,0:T(8,128)(2,1)S(1)} %fusion.1), channel_id=1, source_target_pairs={{0,4},{4,0},{8,12},{12,8},{16,20},{20,16},{24,28},{28,24},{32,36},... | collective-permute-start | bytes 6291464 | tf_op jit(solution)/shard_map/ppermute | solution.py:250
  151.1 17.4 %collective-permute-start.15 = (bf16[256,1024]{1,0:T(8,128)(2,1)}, bf16[256,1024]{1,0:T(8,128)(2,1)}, u32[]{:S(2)}, u32[]{:S(2)}) collective-permute-start(bf16[256,1024]{1,0:T(8,128)(2,1)} %param.21), channel_id=1, source_target_pairs={{0,1},{1,2},{2,3},{3,0},{4,5},{5,6},{6,7},{7,4},{8,9},{9,10},{10,1... | collective-permute-start | bytes 1572872 | tf_op jit(solution)/shard_map/ppermute | solution.py:273
  152.3 25.7 %collective-permute-start.16 = (bf16[256,1024]{1,0:T(8,128)(2,1)}, bf16[256,1024]{1,0:T(8,128)(2,1)}, u32[]{:S(2)}, u32[]{:S(2)}) collective-permute-start(bf16[256,1024]{1,0:T(8,128)(2,1)} %param.21), channel_id=1, source_target_pairs={{0,2},{1,3},{2,0},{3,1},{4,6},{5,7},{6,4},{7,5},{8,10},{9,11},{10,... | collective-permute-start | bytes 1572872 | tf_op jit(solution)/shard_map/ppermute | solution.py:273
  154.7 23.3 %collective-permute-start.17 = (bf16[256,1024]{1,0:T(8,128)(2,1)}, bf16[256,1024]{1,0:T(8,128)(2,1)}, u32[]{:S(2)}, u32[]{:S(2)}) collective-permute-start(bf16[256,1024]{1,0:T(8,128)(2,1)} %param.21), channel_id=1, source_target_pairs={{0,3},{1,0},{2,1},{3,2},{4,7},{5,4},{6,5},{7,6},{8,11},{9,8},{10,9... | collective-permute-start | bytes 1572872 | tf_op jit(solution)/shard_map/ppermute | solution.py:273
  157.4 2.2 collective-permute-start
  166.8 26.9 %collective-permute-start.3 = (bf16[2,2,2,2,4,64,128]{6,5,4,3,2,1,0:T(8,128)(2,1)}, bf16[2,2,2,2,4,64,128]{6,5,4,3,2,1,0:T(8,128)(2,1)}, u32[]{:S(2)}, u32[]{:S(2)}) collective-permute-start(bf16[2,2,2,2,4,64,128]{6,5,4,3,2,1,0:T(8,128)(2,1)} %fusion.18), channel_id=1, source_target_pairs={{0,8},{4,12},{8,0},{12,4},{16,24},{20,28},{24,16},{28,20},{32,40},... | collective-permute-start | bytes 3145736 | tf_op jit(solution)/shard_map/ppermute | solution.py:250
  166.9 26.0 %collective-permute-start.2 = (f32[2,2,2,2,8,128]{5,4,3,2,1,0:T(8,128)S(1)}, f32[2,2,2,2,8,128]{5,4,3,2,1,0:T(8,128)S(1)}, u32[]{:S(2)}, u32[]{:S(2)}) collective-permute-start(f32[2,2,2,2,8,128]{5,4,3,2,1,0:T(8,128)S(1)} %get-tuple-element.54), channel_id=1, source_target_pairs={{0,8},{4,12},{8,0},{12,4},{16,24},{20,28},{24,16},{28,20},{32,40},... | collective-permute-start | bytes 196616 | tf_op jit(solution)/shard_map/ppermute | solution.py:251
  192.9 4.6 %collective-permute-start.4 = (f32[2,2,2,8,128]{4,3,2,1,0:T(8,128)S(1)}, f32[2,2,2,8,128]{4,3,2,1,0:T(8,128)S(1)}, u32[]{:S(2)}, u32[]{:S(2)}) collective-permute-start(f32[2,2,2,8,128]{4,3,2,1,0:T(8,128)S(1)} %get-tuple-element.56), channel_id=1, source_target_pairs={{0,32},{4,36},{8,40},{12,44},{16,48},{20,52},{24,56},{28,60},{32,0... | collective-permute-start | bytes 98312 | tf_op jit(solution)/shard_map/ppermute | solution.py:251
  196.2 12.2 %collective-permute-start.5 = (bf16[2,2,2,4,64,128]{5,4,3,2,1,0:T(8,128)(2,1)S(1)}, bf16[2,2,2,4,64,128]{5,4,3,2,1,0:T(8,128)(2,1)S(1)}, u32[]{:S(2)}, u32[]{:S(2)}) collective-permute-start(bf16[2,2,2,4,64,128]{5,4,3,2,1,0:T(8,128)(2,1)S(1)} %fusion.38), channel_id=1, source_target_pairs={{0,32},{4,36},{8,40},{12,44},{16,48},{20,52},{24,56},{28,60},{32,0... | collective-permute-start | bytes 1572872 | tf_op jit(solution)/shard_map/ppermute | solution.py:250
  197.7 12.7 %collective-permute-start.6 = (f32[2,2,8,128]{3,2,1,0:T(8,128)S(1)}, f32[2,2,8,128]{3,2,1,0:T(8,128)S(1)}, u32[]{:S(2)}, u32[]{:S(2)}) collective-permute-start(f32[2,2,8,128]{3,2,1,0:T(8,128)S(1)} %get-tuple-element.58), channel_id=1, source_target_pairs={{0,16},{4,20},{8,24},{12,28},{16,0},{20,4},{24,8},{28,12},{32,48},... | collective-permute-start | bytes 49160 | tf_op jit(solution)/shard_map/ppermute | solution.py:251
  208.7 7.2 %collective-permute-start.7 = (bf16[2,2,4,64,128]{4,3,2,1,0:T(8,128)(2,1)S(1)}, bf16[2,2,4,64,128]{4,3,2,1,0:T(8,128)(2,1)S(1)}, u32[]{:S(2)}, u32[]{:S(2)}) collective-permute-start(bf16[2,2,4,64,128]{4,3,2,1,0:T(8,128)(2,1)S(1)} %fusion.45), channel_id=1, source_target_pairs={{0,16},{4,20},{8,24},{12,28},{16,0},{20,4},{24,8},{28,12},{32,48},... | collective-permute-start | bytes 786440 | tf_op jit(solution)/shard_map/ppermute | solution.py:250
  210.4 7.5 %collective-permute-start.8 = (f32[2,8,128]{2,1,0:T(8,128)S(1)}, f32[2,8,128]{2,1,0:T(8,128)S(1)}, u32[]{:S(2)}, u32[]{:S(2)}) collective-permute-start(f32[2,8,128]{2,1,0:T(8,128)S(1)} %get-tuple-element.60), channel_id=1, source_target_pairs={{0,64},{4,68},{8,72},{12,76},{16,80},{20,84},{24,88},{28,92},{32,9... | collective-permute-start | bytes 24584 | tf_op jit(solution)/shard_map/ppermute | solution.py:251
  216.1 6.2 %collective-permute-start.9 = (bf16[2,4,64,128]{3,2,1,0:T(8,128)(2,1)S(1)}, bf16[2,4,64,128]{3,2,1,0:T(8,128)(2,1)S(1)}, u32[]{:S(2)}, u32[]{:S(2)}) collective-permute-start(bf16[2,4,64,128]{3,2,1,0:T(8,128)(2,1)S(1)} %fusion.54), channel_id=1, source_target_pairs={{0,64},{4,68},{8,72},{12,76},{16,80},{20,84},{24,88},{28,92},{32,9... | collective-permute-start | bytes 393224 | tf_op jit(solution)/shard_map/ppermute | solution.py:250
  217.9 7.1 %collective-permute-start.10 = (f32[8,128]{1,0:T(8,128)S(1)}, f32[8,128]{1,0:T(8,128)S(1)}, u32[]{:S(2)}, u32[]{:S(2)}) collective-permute-start(f32[8,128]{1,0:T(8,128)S(1)} %get-tuple-element.62), channel_id=1, source_target_pairs={{0,128},{4,132},{8,136},{12,140},{16,144},{20,148},{24,152},{28,15... | collective-permute-start | bytes 12296 | tf_op jit(solution)/shard_map/ppermute | solution.py:251
  222.4 7.2 %collective-permute-start.11 = (bf16[4,64,128]{2,1,0:T(8,128)(2,1)S(1)}, bf16[4,64,128]{2,1,0:T(8,128)(2,1)S(1)}, u32[]{:S(2)}, u32[]{:S(2)}) collective-permute-start(bf16[4,64,128]{2,1,0:T(8,128)(2,1)S(1)} %fusion.58), channel_id=1, source_target_pairs={{0,128},{4,132},{8,136},{12,140},{16,144},{20,148},{24,152},{28,15... | collective-permute-start | bytes 196616 | tf_op jit(solution)/shard_map/ppermute | solution.py:250
  229.6 4.7 %collective-permute-start.12 = (bf16[128,256]{0,1:T(8,128)(2,1)S(1)}, bf16[128,256]{0,1:T(8,128)(2,1)S(1)}, u32[]{:S(2)}, u32[]{:S(2)}) collective-permute-start(bf16[128,256]{0,1:T(8,128)(2,1)S(1)} %bitcast.187), channel_id=1, source_target_pairs={{0,1},{1,2},{2,3},{3,0},{4,5},{5,6},{6,7},{7,4},{8,9},{9,10},{10,1... | collective-permute-start | bytes 196616 | tf_op jit(solution)/shard_map/ppermute | solution.py:273
  229.9 4.7 %collective-permute-start.13 = (bf16[128,256]{0,1:T(8,128)(2,1)S(1)}, bf16[128,256]{0,1:T(8,128)(2,1)S(1)}, u32[]{:S(2)}, u32[]{:S(2)}) collective-permute-start(bf16[128,256]{0,1:T(8,128)(2,1)S(1)} %bitcast.188), channel_id=1, source_target_pairs={{0,2},{1,3},{2,0},{3,1},{4,6},{5,7},{6,4},{7,5},{8,10},{9,11},{10,... | collective-permute-start | bytes 196616 | tf_op jit(solution)/shard_map/ppermute | solution.py:273
  230.5 4.7 %collective-permute-start.14 = (bf16[128,256]{0,1:T(8,128)(2,1)S(1)}, bf16[128,256]{0,1:T(8,128)(2,1)S(1)}, u32[]{:S(2)}, u32[]{:S(2)}) collective-permute-start(bf16[128,256]{0,1:T(8,128)(2,1)S(1)} %bitcast.189), channel_id=1, source_target_pairs={{0,3},{1,0},{2,1},{3,2},{4,7},{5,4},{6,5},{7,6},{8,11},{9,8},{10,9... | collective-permute-start | bytes 196616 | tf_op jit(solution)/shard_map/ppermute | solution.py:273
  270.8 10.2 %collective-permute-start.18 = (bf16[640,256]{1,0:T(8,128)(2,1)S(1)}, bf16[640,256]{1,0:T(8,128)(2,1)S(1)}, u32[]{:S(2)}, u32[]{:S(2)}) collective-permute-start(bf16[640,256]{1,0:T(8,128)(2,1)S(1)} %reshape_squeeze.3), channel_id=1, source_target_pairs={{0,1},{1,2},{2,3},{3,0},{4,5},{5,6},{6,7},{7,4},{8,9},{9,10},{10,1... | collective-permute-start | bytes 983048 | tf_op jit(solution)/shard_map/ppermute | solution.py:273
  271.9 16.7 %collective-permute-start.19 = (bf16[640,256]{1,0:T(8,128)(2,1)S(1)}, bf16[640,256]{1,0:T(8,128)(2,1)S(1)}, u32[]{:S(2)}, u32[]{:S(2)}) collective-permute-start(bf16[640,256]{1,0:T(8,128)(2,1)S(1)} %reshape_squeeze.3), channel_id=1, source_target_pairs={{0,2},{1,3},{2,0},{3,1},{4,6},{5,7},{6,4},{7,5},{8,10},{9,11},{10,... | collective-permute-start | bytes 983048 | tf_op jit(solution)/shard_map/ppermute | solution.py:273
  274.1 14.4 %collective-permute-start.20 = (bf16[640,256]{1,0:T(8,128)(2,1)S(1)}, bf16[640,256]{1,0:T(8,128)(2,1)S(1)}, u32[]{:S(2)}, u32[]{:S(2)}) collective-permute-start(bf16[640,256]{1,0:T(8,128)(2,1)S(1)} %reshape_squeeze.3), channel_id=1, source_target_pairs={{0,3},{1,0},{2,1},{3,2},{4,7},{5,4},{6,5},{7,6},{8,11},{9,8},{10,9... | collective-permute-start | bytes 983048 | tf_op jit(solution)/shard_map/ppermute | solution.py:273
  295.8 27.1 %copy-start.6 = (bf16[128,1024]{1,0:T(8,128)(2,1)S(1)}, bf16[128,1024]{1,0:T(8,128)(2,1)}, u32[]{:S(2)}) copy-start(bf16[128,1024]{1,0:T(8,128)(2,1)} %copy-done.5) | copy-start | bytes 786436
  295.8 27.1 %copy-start.11 = (f32[1024,32]{0,1:T(8,128)S(1)}, f32[1024,32]{0,1:T(8,128)}, u32[]{:S(2)}) copy-start(f32[1024,32]{0,1:T(8,128)} %param.25) | copy-start | bytes 393220
  295.8 10.2 %collective-permute-start.21 = (bf16[640,256]{1,0:T(8,128)(2,1)S(1)}, bf16[640,256]{1,0:T(8,128)(2,1)S(1)}, u32[]{:S(2)}, u32[]{:S(2)}) collective-permute-start(bf16[640,256]{1,0:T(8,128)(2,1)S(1)} %get-tuple-element.40), channel_id=1, source_target_pairs={{0,1},{1,2},{2,3},{3,0},{4,5},{5,6},{6,7},{7,4},{8,9},{9,10},{10,1... | collective-permute-start | bytes 983048 | tf_op jit(solution)/shard_map/ppermute | solution.py:321
  297.5 17.0 %collective-permute-start.22 = (bf16[640,256]{1,0:T(8,128)(2,1)S(1)}, bf16[640,256]{1,0:T(8,128)(2,1)S(1)}, u32[]{:S(2)}, u32[]{:S(2)}) collective-permute-start(bf16[640,256]{1,0:T(8,128)(2,1)S(1)} %get-tuple-element.42), channel_id=1, source_target_pairs={{0,2},{1,3},{2,0},{3,1},{4,6},{5,7},{6,4},{7,5},{8,10},{9,11},{10,... | collective-permute-start | bytes 983048 | tf_op jit(solution)/shard_map/ppermute | solution.py:321
  300.2 14.3 %collective-permute-start.23 = (bf16[640,256]{1,0:T(8,128)(2,1)S(1)}, bf16[640,256]{1,0:T(8,128)(2,1)}, u32[]{:S(2)}, u32[]{:S(2)}) collective-permute-start(bf16[640,256]{1,0:T(8,128)(2,1)S(1)} %get-tuple-element.41), channel_id=1, source_target_pairs={{0,3},{1,0},{2,1},{3,2},{4,7},{5,4},{6,5},{7,6},{8,11},{9,8},{10,9... | collective-permute-start | bytes 983048 | tf_op jit(solution)/shard_map/ppermute | solution.py:321
  316.6 24.0 %all-to-all-start.1 = ((bf16[64,1,10,256]{3,2,1,0:T(8,128)(2,1)}), bf16[64,1,10,256]{3,2,1,0:T(8,128)(2,1)S(1)}, u32[]{:S(2)}, u32[]{:S(2)}) async-start(bf16[64,1,10,256]{3,2,1,0:T(8,128)(2,1)} %bitcast.67), calls=%async_computation.1 | async-start | bytes 1048576 | tf_op jit(solution)/shard_map/all_to_all | solution.py:325
  323.3 19.5 %copy-start.1 = (bf16[1,352,1024]{2,1,0:T(8,128)(2,1)S(1)}, bf16[1,352,1024]{2,1,0:T(8,128)(2,1)}, u32[]{:S(2)}) copy-start(bf16[1,352,1024]{2,1,0:T(8,128)(2,1)} %param.27) | copy-start | bytes 2162692
  (10 other events, 46.7 us)
Sparse Core Ops, SparseCore 0:
  10.1 83.1 all-gather.1

commit v2 on v1

--- a/solution.py
+++ b/solution.py
@@ -201,9 +201,19 @@
     sorted_offset = query_offsets[block_order]
     sorted_fresh = (block_order == page_count).astype(jnp.int32)
     sorted_page = jnp.minimum(block_order, page_count - 1)
-    everyone = lax.all_gather(queries, "seq", axis=0, tiled=True).reshape(
-        request_total, span_rows, local_heads * DH
-    )
+    gathered = queries
+    held_bits = []
+    gather_count = seq_count.bit_length() - 1
+    for bit in ([5, 4, 2, 3, 1, 0] if gather_count == 6 else list(range(gather_count - 1, -1, -1))):
+        pairs = [(source, source ^ (1 << bit)) for source in range(seq_count)]
+        got = lax.ppermute(gathered, "seq", pairs)
+        low_side = ((seq_index >> bit) & 1) == 0
+        position = sum(1 for held in held_bits if held > bit)
+        gathered = jnp.stack(
+            [jnp.where(low_side, gathered, got), jnp.where(low_side, got, gathered)], axis=position
+        )
+        held_bits.insert(position, bit)
+    everyone = gathered.reshape(request_total, span_rows, local_heads * DH)
     width_heads = local_heads * DH
     acc_out, stat_out = local_attention(
         sorted_owner,

time: 350 us -> 341 us (0.974)
  waiting for transfers between devices: 156 us -> 124 us
  starting transfers between devices: 39.3 us -> 64 us
  between operations: 14 us -> 0.7 us
  other arithmetic: 22.8 us -> 28.4 us
    all_gather x1 -> x0, waiting for transfers between devices: 72.1 us -> none  [shards(): lax.all_gather(queries, 'seq', axis=0, tiled=True)]
    ppermute x0 -> x6, waiting for transfers between devices: none -> 44.3 us  [shards(): got = lax.ppermute(gathered, 'seq', pairs)]
    ppermute x0 -> x6, starting transfers between devices: none -> 19.4 us  [shards(): got = lax.ppermute(gathered, 'seq', pairs)]
    another operation x2 -> x14, other arithmetic: 0.63 us -> 6.25 us  [the longest x12 5.62 us: shards(): jnp.stack([jnp.where(low_side, gathered, got), jnp.where(low_side, got, g...]
    unnamed x34 -> x32, local copies, waits for them, and re-layouts: 8.55 us -> 8.61 us
  transfers between devices with their start and end apart: 26 -> 31, of which waited for: 16 -> 19; matrix products, arithmetic and copies ran while one was open for 9% -> 10% of each run, Pallas kernels for 0% -> 0%
where the time goes in v2:
time: 341 us
  waiting for transfers between devices  124 us (36%)
  starting transfers between devices  64 us (19%)
  Pallas kernels  49.1 us (14%)
  blocking collectives  32.4 us (10%)
  other arithmetic  28.4 us (8%)
  local copies, waits for them, and re-layouts  26.9 us (8%)
  matrix products  15.3 us (4%)
    pallas_call x1, Pallas kernels, local_attention(): pl.pallas_call(attend_kernel, grid_spec=grid_spec, out_shape=[jax.ShapeDt...  49.1 us
    ppermute x6, waiting for transfers between devices, shards(): got = lax.ppermute(gathered, 'seq', pairs)  44.3 us
    all_to_all x1, blocking collectives, shards(): lax.all_to_all(outgoing, 'seq', split_axis=0, concat_axis=0, tiled=True)  32.4 us
    ppermute x9, waiting for transfers between devices, tp_gather(): lax.ppermute(value, 'tp', [(i, (i + k) % tp_count) for i in range(tp_coun...  25.3 us
    ppermute x6, starting transfers between devices, shards(): got = lax.ppermute(gathered, 'seq', pairs)  19.4 us
    ppermute x6, waiting for transfers between devices, shards(): lax.ppermute(send_acc.astype(jnp.bfloat16), 'seq', pairs)  15.3 us
    ppermute x3, waiting for transfers between devices, shards(): lax.ppermute(target_cols, 'tp', [(i, (i + k) % tp_count) for i in range(t...  14.4 us
    all_to_all x1, waiting for transfers between devices, shards(): lax.all_to_all(produced.astype(jnp.bfloat16), 'seq', split_axis=0, concat...  14.1 us
  transfers between devices with their start and end apart: 31, of which 19 were waited for; matrix products, arithmetic and copies ran while one was open for 10% of the time, Pallas kernels for 0%

profile of v2, /device:TPU:1, one launch (start us, length us, event | category | flops | bytes accessed | tf_op | source)
XLA Modules:
  0.0 340.6 jit_solution(8718571082800867962)
XLA Ops:
  2.6 7.8 %collective-permute-start = (bf16[128,256]{1,0:T(8,128)(2,1)S(1)}, bf16[128,256]{1,0:T(8,128)(2,1)S(1)}, u32[]{:S(2)}, u32[]{:S(2)}) collective-permute-start(bf16[128,256]{1,0:T(8,128)(2,1)S(1)} %convolution_convert_fusion.4), channel_id=1, source_target_pairs={{0,128},{4,132},{8,136},{12,140},{16,144},{20,148},{24,152},{28,15... | collective-permute-start | bytes 196616 | tf_op jit(solution)/shard_map/ppermute | solution.py:209
  13.6 5.4 %collective-permute-done.1 = bf16[2,128,256]{2,1,0:T(8,128)(2,1)S(1)} collective-permute-done((bf16[2,128,256]{2,1,0:T(8,128)(2,1)S(1)}, bf16[2,128,256]{2,1,0:T(8,128)(2,1)S(1)}, u32[]{:S(2)}, u32[]{:S(2)}) %collective-permute-start.1) | collective-permute-done | bytes 131104 | tf_op jit(solution)/shard_map/ppermute | solution.py:209
  19.1 4.6 %collective-permute-start.2 = (bf16[2,2,128,256]{3,2,0,1:T(8,128)(2,1)S(1)}, bf16[2,2,128,256]{3,2,0,1:T(8,128)(2,1)S(1)}, u32[]{:S(2)}, u32[]{:S(2)}) collective-permute-start(bf16[2,2,128,256]{3,2,0,1:T(8,128)(2,1)S(1)} %pad_maximum_fusion.7), channel_id=1, source_target_pairs={{0,16},{4,20},{8,24},{12,28},{16,0},{20,4},{24,8},{28,12},{32,48},... | collective-permute-start | bytes 786440 | tf_op jit(solution)/shard_map/ppermute | solution.py:209
  23.7 5.1 %collective-permute-done.2 = bf16[2,2,128,256]{3,2,0,1:T(8,128)(2,1)S(1)} collective-permute-done((bf16[2,2,128,256]{3,2,0,1:T(8,128)(2,1)S(1)}, bf16[2,2,128,256]{3,2,0,1:T(8,128)(2,1)S(1)}, u32[]{:S(2)}, u32[]{:S(2)}) %collective-permute-start.2) | collective-permute-done | bytes 262176 | tf_op jit(solution)/shard_map/ppermute | solution.py:209
  29.0 11.3 %collective-permute-done.3 = bf16[2,2,2,128,256]{4,3,0,1,2:T(8,128)(2,1)S(1)} collective-permute-done((bf16[2,2,2,128,256]{4,3,0,1,2:T(8,128)(2,1)S(1)}, bf16[2,2,2,128,256]{4,3,0,1,2:T(8,128)(2,1)S(1)}, u32[]{:S(2)}, u32[]{:S(2)}) %collective-permute-start.3) | collective-permute-done | bytes 524320 | tf_op jit(solution)/shard_map/ppermute | solution.py:209
  43.3 20.8 %collective-permute-done.4 = bf16[2,2,2,2,128,256]{5,4,0,1,3,2:T(8,128)(2,1)} collective-permute-done((bf16[2,2,2,2,128,256]{5,4,0,1,3,2:T(8,128)(2,1)S(1)}, bf16[2,2,2,2,128,256]{5,4,0,1,3,2:T(8,128)(2,1)}, u32[]{:S(2)}, u32[]{:S(2)}) %collective-permute-start.4) | collective-permute-done | bytes 1048608 | tf_op jit(solution)/shard_map/ppermute | solution.py:209
  67.1 3.5 %collective-permute-start.5 = (bf16[2,2,2,2,2,128,256]{6,5,0,1,3,2,4:T(8,128)(2,1)}, bf16[2,2,2,2,2,128,256]{6,5,0,1,3,2,4:T(8,128)(2,1)}, u32[]{:S(2)}, u32[]{:S(2)}) collective-permute-start(bf16[2,2,2,2,2,128,256]{6,5,0,1,3,2,4:T(8,128)(2,1)} %pad_maximum_fusion.1), channel_id=1, source_target_pairs={{0,4},{4,0},{8,12},{12,8},{16,20},{20,16},{24,28},{28,24},{32,36},... | collective-permute-start | bytes 6291464 | tf_op jit(solution)/shard_map/ppermute | solution.py:209
  86.9 49.1 %shard_map.136 = (f32[4,16,4,64,128]{4,3,2,1,0:T(8,128)}, f32[4,16,8,128]{3,2,1,0:T(8,128)}) custom-call(s32[34]{0:T(128)} %copy-done.13, s32[34]{0:T(128)} %get-tuple-element.77.page_ref, s32[34]{0:T(128)} %gather_fusion.2, s32[34]{0:T(128)} %gather_fusion.3, s32[34]{0:T(128)} %compare_convert_fusion.fresh_ref, bf16[16,512,256]{2,1,0:T(8,128)(2,1)} %bitcast.204, ...), custom_call_target="tpu_custom_call" | custom-call | tf_op jit(solution)/shard_map/pallas_call | solution.py:130
  136.0 4.4 %broadcast_select_fusion = f32[4,16,4,64,128]{4,3,2,1,0:T(8,128)S(1)} fusion(f32[4,16,4,64,128]{4,3,2,1,0:T(8,128)} %get-tuple-element.9, pred[16]{0:T(512)(128)(4,1)S(1)} %fusion.84), kind=kLoop, calls=%fused_computation.12 | loop fusion | flops 2097152 | bytes 16777232 | tf_op jit(solution)/shard_map/jit(_where)/select_n | solution.py:237
  140.5 3.3 copy-done.2
  146.0 2.6 collective-permute-start.22
  153.6 4.0 %fusion = f32[2,2,2,2,2,4,64,128]{7,6,5,4,3,2,1,0:T(8,128)S(1)} fusion(bf16[2,2,2,2,2,4,64,128]{7,6,5,4,3,2,1,0:T(8,128)(2,1)} %collective-permute-done.7, f32[2,2,2,2,2,2,4,64,128]{8,7,6,5,4,3,2,1,0:T(8,128)} %bitcast.203, s32[]{:T(128)S(6)} %select_n.333, f32[2,2,2,2,2,4,128]{6,5,4,3,2,1,0:T(4,128)S(1)} %get-tuple-element.34, ...), kind=kLoop, calls=%fused_computation.10 | loop fusion | flops 4194304 | bytes 10616836 | tf_op jit(solution)/shard_map/add | solution.py:272
  162.5 9.3 %collective-permute-done.22 = bf16[256,1024]{1,0:T(8,128)(2,1)} collective-permute-done((bf16[256,1024]{1,0:T(8,128)(2,1)}, bf16[256,1024]{1,0:T(8,128)(2,1)}, u32[]{:S(2)}, u32[]{:S(2)}) %collective-permute-start.22) | collective-permute-done | bytes 524320 | tf_op jit(solution)/shard_map/ppermute | solution.py:283
  171.8 3.1 pad_maximum_fusion.2
  177.2 9.7 %collective-permute-done.8 = f32[2,2,2,2,8,128]{5,4,3,2,1,0:T(8,128)S(1)} collective-permute-done((f32[2,2,2,2,8,128]{5,4,3,2,1,0:T(8,128)S(1)}, f32[2,2,2,2,8,128]{5,4,3,2,1,0:T(8,128)S(1)}, u32[]{:S(2)}, u32[]{:S(2)}) %collective-permute-start.8) | collective-permute-done | bytes 65568 | tf_op jit(solution)/shard_map/ppermute | solution.py:261
  187.4 2.5 fusion.10
  191.5 2.9 collective-permute-start.12
  194.4 7.7 %collective-permute-done.11 = bf16[2,2,2,4,64,128]{5,4,3,2,1,0:T(8,128)(2,1)S(1)} collective-permute-done((bf16[2,2,2,4,64,128]{5,4,3,2,1,0:T(8,128)(2,1)S(1)}, bf16[2,2,2,4,64,128]{5,4,3,2,1,0:T(8,128)(2,1)S(1)}, u32[]{:S(2)}, u32[]{:S(2)}) %collective-permute-start.11) | collective-permute-done | bytes 524320 | tf_op jit(solution)/shard_map/ppermute | solution.py:260
  202.4 2.9 collective-permute-start.13
  205.4 4.2 %collective-permute-done.13 = bf16[2,2,4,64,128]{4,3,2,1,0:T(8,128)(2,1)S(1)} collective-permute-done((bf16[2,2,4,64,128]{4,3,2,1,0:T(8,128)(2,1)S(1)}, bf16[2,2,4,64,128]{4,3,2,1,0:T(8,128)(2,1)S(1)}, u32[]{:S(2)}, u32[]{:S(2)}) %collective-permute-start.13) | collective-permute-done | bytes 262176 | tf_op jit(solution)/shard_map/ppermute | solution.py:260
  209.9 8.1 %collective-permute-start.16 = (f32[8,128]{1,0:T(8,128)S(1)}, f32[8,128]{1,0:T(8,128)S(1)}, u32[]{:S(2)}, u32[]{:S(2)}) collective-permute-start(f32[8,128]{1,0:T(8,128)S(1)} %get-tuple-element.74), channel_id=1, source_target_pairs={{0,128},{4,132},{8,136},{12,140},{16,144},{20,148},{24,152},{28,15... | collective-permute-start | bytes 12296 | tf_op jit(solution)/shard_map/ppermute | solution.py:261
  218.1 3.8 %collective-permute-start.17 = (bf16[4,64,128]{2,1,0:T(8,128)(2,1)S(1)}, bf16[4,64,128]{2,1,0:T(8,128)(2,1)S(1)}, u32[]{:S(2)}, u32[]{:S(2)}) collective-permute-start(bf16[4,64,128]{2,1,0:T(8,128)(2,1)S(1)} %fusion.58), channel_id=1, source_target_pairs={{0,128},{4,132},{8,136},{12,140},{16,144},{20,148},{24,152},{28,15... | collective-permute-start | bytes 196616 | tf_op jit(solution)/shard_map/ppermute | solution.py:260
  221.8 3.3 collective-permute-done.17
  235.1 32.4 %all_to_all.10 = bf16[64,1,10,256]{3,2,1,0:T(8,128)(2,1)S(1)} all-to-all(bf16[64,1,10,256]{3,2,1,0:T(8,128)(2,1)S(1)} %bitcast.206), channel_id=1, replica_groups=mesh['seq'=64,'tp'=4] {'seq'}, dimensions={0} | all-to-all | bytes 655360 | tf_op jit(solution)/shard_map/all_to_all | solution.py:317
  271.3 6.4 %collective-permute-done.24 = bf16[640,256]{1,0:T(8,128)(2,1)S(1)} collective-permute-done((bf16[640,256]{1,0:T(8,128)(2,1)S(1)}, bf16[640,256]{1,0:T(8,128)(2,1)S(1)}, u32[]{:S(2)}, u32[]{:S(2)}) %collective-permute-start.24) | collective-permute-done | bytes 327712 | tf_op jit(solution)/shard_map/ppermute | solution.py:283
  277.7 7.8 %collective-permute-done.25 = bf16[640,256]{1,0:T(8,128)(2,1)S(1)} collective-permute-done((bf16[640,256]{1,0:T(8,128)(2,1)S(1)}, bf16[640,256]{1,0:T(8,128)(2,1)S(1)}, u32[]{:S(2)}, u32[]{:S(2)}) %collective-permute-start.25) | collective-permute-done | bytes 327712 | tf_op jit(solution)/shard_map/ppermute | solution.py:283
  289.4 3.2 convolution_convert_fusion
  294.9 2.7 collective-permute-start.28
  297.9 5.5 %collective-permute-done.27 = bf16[640,256]{1,0:T(8,128)(2,1)S(1)} collective-permute-done((bf16[640,256]{1,0:T(8,128)(2,1)}, bf16[640,256]{1,0:T(8,128)(2,1)S(1)}, u32[]{:S(2)}, u32[]{:S(2)}) %collective-permute-start.27) | collective-permute-done | bytes 327712 | tf_op jit(solution)/shard_map/ppermute | solution.py:331
  303.4 8.8 %collective-permute-done.28 = bf16[640,256]{1,0:T(8,128)(2,1)} collective-permute-done((bf16[640,256]{1,0:T(8,128)(2,1)S(1)}, bf16[640,256]{1,0:T(8,128)(2,1)}, u32[]{:S(2)}, u32[]{:S(2)}) %collective-permute-start.28) | collective-permute-done | bytes 327712 | tf_op jit(solution)/shard_map/ppermute | solution.py:331
  314.4 6.3 %all-to-all-start.1 = ((bf16[64,1,10,256]{3,2,1,0:T(8,128)(2,1)}), bf16[64,1,10,256]{3,2,1,0:T(8,128)(2,1)S(1)}, u32[]{:S(2)}, u32[]{:S(2)}) async-start(bf16[64,1,10,256]{3,2,1,0:T(8,128)(2,1)} %bitcast.79), calls=%async_computation.1 | async-start | bytes 1048576 | tf_op jit(solution)/shard_map/all_to_all | solution.py:335
  324.3 14.1 %all-to-all-done.1 = bf16[64,1,10,256]{3,2,1,0:T(8,128)(2,1)S(1)} async-done(((bf16[64,1,10,256]{3,2,1,0:T(8,128)(2,1)}), bf16[64,1,10,256]{3,2,1,0:T(8,128)(2,1)S(1)}, u32[]{:S(2)}, u32[]{:S(2)}) %all-to-all-start.1) | async-done | bytes 327712 | tf_op jit(solution)/shard_map/all_to_all | solution.py:335
  (180 shorter events, 73.4 us)
Async XLA Ops:
  0.0 289.4 %copy-start = (bf16[1,352,1024]{2,1,0:T(8,128)(2,1)S(1)}, bf16[1,352,1024]{2,1,0:T(8,128)(2,1)}, u32[]{:S(2)}) copy-start(bf16[1,352,1024]{2,1,0:T(8,128)(2,1)} %param.27) | copy-start | bytes 2162692
  2.6 9.6 %collective-permute-start = (bf16[128,256]{1,0:T(8,128)(2,1)S(1)}, bf16[128,256]{1,0:T(8,128)(2,1)S(1)}, u32[]{:S(2)}, u32[]{:S(2)}) collective-permute-start(bf16[128,256]{1,0:T(8,128)(2,1)S(1)} %convolution_convert_fusion.4), channel_id=1, source_target_pairs={{0,128},{4,132},{8,136},{12,140},{16,144},{20,148},{24,152},{28,15... | collective-permute-start | bytes 196616 | tf_op jit(solution)/shard_map/ppermute | solution.py:209
  12.2 6.9 %collective-permute-start.1 = (bf16[2,128,256]{2,1,0:T(8,128)(2,1)S(1)}, bf16[2,128,256]{2,1,0:T(8,128)(2,1)S(1)}, u32[]{:S(2)}, u32[]{:S(2)}) collective-permute-start(bf16[2,128,256]{2,1,0:T(8,128)(2,1)S(1)} %pad_maximum_fusion.12), channel_id=1, source_target_pairs={{0,64},{4,68},{8,72},{12,76},{16,80},{20,84},{24,88},{28,92},{32,9... | collective-permute-start | bytes 393224 | tf_op jit(solution)/shard_map/ppermute | solution.py:209
  19.1 9.7 %collective-permute-start.2 = (bf16[2,2,128,256]{3,2,0,1:T(8,128)(2,1)S(1)}, bf16[2,2,128,256]{3,2,0,1:T(8,128)(2,1)S(1)}, u32[]{:S(2)}, u32[]{:S(2)}) collective-permute-start(bf16[2,2,128,256]{3,2,0,1:T(8,128)(2,1)S(1)} %pad_maximum_fusion.7), channel_id=1, source_target_pairs={{0,16},{4,20},{8,24},{12,28},{16,0},{20,4},{24,8},{28,12},{32,48},... | collective-permute-start | bytes 786440 | tf_op jit(solution)/shard_map/ppermute | solution.py:209
  28.9 11.4 %collective-permute-start.3 = (bf16[2,2,2,128,256]{4,3,0,1,2:T(8,128)(2,1)S(1)}, bf16[2,2,2,128,256]{4,3,0,1,2:T(8,128)(2,1)S(1)}, u32[]{:S(2)}, u32[]{:S(2)}) collective-permute-start(bf16[2,2,2,128,256]{4,3,0,1,2:T(8,128)(2,1)S(1)} %pad_maximum_fusion.6), channel_id=1, source_target_pairs={{0,32},{4,36},{8,40},{12,44},{16,48},{20,52},{24,56},{28,60},{32,0... | collective-permute-start | bytes 1572872 | tf_op jit(solution)/shard_map/ppermute | solution.py:209
  41.3 22.7 %collective-permute-start.4 = (bf16[2,2,2,2,128,256]{5,4,0,1,3,2:T(8,128)(2,1)S(1)}, bf16[2,2,2,2,128,256]{5,4,0,1,3,2:T(8,128)(2,1)}, u32[]{:S(2)}, u32[]{:S(2)}) collective-permute-start(bf16[2,2,2,2,128,256]{5,4,0,1,3,2:T(8,128)(2,1)S(1)} %pad_maximum_fusion.5), channel_id=1, source_target_pairs={{0,8},{4,12},{8,0},{12,4},{16,24},{20,28},{24,16},{28,20},{32,40},... | collective-permute-start | bytes 3145736 | tf_op jit(solution)/shard_map/ppermute | solution.py:209
  67.1 15.3 %collective-permute-start.5 = (bf16[2,2,2,2,2,128,256]{6,5,0,1,3,2,4:T(8,128)(2,1)}, bf16[2,2,2,2,2,128,256]{6,5,0,1,3,2,4:T(8,128)(2,1)}, u32[]{:S(2)}, u32[]{:S(2)}) collective-permute-start(bf16[2,2,2,2,2,128,256]{6,5,0,1,3,2,4:T(8,128)(2,1)} %pad_maximum_fusion.1), channel_id=1, source_target_pairs={{0,4},{4,0},{8,12},{12,8},{16,20},{20,16},{24,28},{28,24},{32,36},... | collective-permute-start | bytes 6291464 | tf_op jit(solution)/shard_map/ppermute | solution.py:209
  144.3 9.3 %collective-permute-start.7 = (bf16[2,2,2,2,2,4,64,128]{7,6,5,4,3,2,1,0:T(8,128)(2,1)S(1)}, bf16[2,2,2,2,2,4,64,128]{7,6,5,4,3,2,1,0:T(8,128)(2,1)}, u32[]{:S(2)}, u32[]{:S(2)}) collective-permute-start(bf16[2,2,2,2,2,4,64,128]{7,6,5,4,3,2,1,0:T(8,128)(2,1)S(1)} %fusion.1), channel_id=1, source_target_pairs={{0,4},{4,0},{8,12},{12,8},{16,20},{20,16},{24,28},{28,24},{32,36},... | collective-permute-start | bytes 6291464 | tf_op jit(solution)/shard_map/ppermute | solution.py:260
  144.4 18.1 %collective-permute-start.21 = (bf16[256,1024]{1,0:T(8,128)(2,1)}, bf16[256,1024]{1,0:T(8,128)(2,1)}, u32[]{:S(2)}, u32[]{:S(2)}) collective-permute-start(bf16[256,1024]{1,0:T(8,128)(2,1)} %param.21), channel_id=1, source_target_pairs={{0,1},{1,2},{2,3},{3,0},{4,5},{5,6},{6,7},{7,4},{8,9},{9,10},{10,1... | collective-permute-start | bytes 1572872 | tf_op jit(solution)/shard_map/ppermute | solution.py:283
  146.0 25.7 %collective-permute-start.22 = (bf16[256,1024]{1,0:T(8,128)(2,1)}, bf16[256,1024]{1,0:T(8,128)(2,1)}, u32[]{:S(2)}, u32[]{:S(2)}) collective-permute-start(bf16[256,1024]{1,0:T(8,128)(2,1)} %param.21), channel_id=1, source_target_pairs={{0,2},{1,3},{2,0},{3,1},{4,6},{5,7},{6,4},{7,5},{8,10},{9,11},{10,... | collective-permute-start | bytes 1572872 | tf_op jit(solution)/shard_map/ppermute | solution.py:283
  148.6 23.1 %collective-permute-start.23 = (bf16[256,1024]{1,0:T(8,128)(2,1)}, bf16[256,1024]{1,0:T(8,128)(2,1)}, u32[]{:S(2)}, u32[]{:S(2)}) collective-permute-start(bf16[256,1024]{1,0:T(8,128)(2,1)} %param.21), channel_id=1, source_target_pairs={{0,3},{1,0},{2,1},{3,2},{4,7},{5,4},{6,5},{7,6},{8,11},{9,8},{10,9... | collective-permute-start | bytes 1572872 | tf_op jit(solution)/shard_map/ppermute | solution.py:283
  151.2 2.3 collective-permute-start.6
  160.8 26.6 %collective-permute-start.9 = (bf16[2,2,2,2,4,64,128]{6,5,4,3,2,1,0:T(8,128)(2,1)}, bf16[2,2,2,2,4,64,128]{6,5,4,3,2,1,0:T(8,128)(2,1)}, u32[]{:S(2)}, u32[]{:S(2)}) collective-permute-start(bf16[2,2,2,2,4,64,128]{6,5,4,3,2,1,0:T(8,128)(2,1)} %fusion.18), channel_id=1, source_target_pairs={{0,8},{4,12},{8,0},{12,4},{16,24},{20,28},{24,16},{28,20},{32,40},... | collective-permute-start | bytes 3145736 | tf_op jit(solution)/shard_map/ppermute | solution.py:260
  162.2 24.7 %collective-permute-start.8 = (f32[2,2,2,2,8,128]{5,4,3,2,1,0:T(8,128)S(1)}, f32[2,2,2,2,8,128]{5,4,3,2,1,0:T(8,128)S(1)}, u32[]{:S(2)}, u32[]{:S(2)}) collective-permute-start(f32[2,2,2,2,8,128]{5,4,3,2,1,0:T(8,128)S(1)} %get-tuple-element.64), channel_id=1, source_target_pairs={{0,8},{4,12},{8,0},{12,4},{16,24},{20,28},{24,16},{28,20},{32,40},... | collective-permute-start | bytes 196616 | tf_op jit(solution)/shard_map/ppermute | solution.py:261
  187.0 4.5 %collective-permute-start.10 = (f32[2,2,2,8,128]{4,3,2,1,0:T(8,128)S(1)}, f32[2,2,2,8,128]{4,3,2,1,0:T(8,128)S(1)}, u32[]{:S(2)}, u32[]{:S(2)}) collective-permute-start(f32[2,2,2,8,128]{4,3,2,1,0:T(8,128)S(1)} %get-tuple-element.68), channel_id=1, source_target_pairs={{0,32},{4,36},{8,40},{12,44},{16,48},{20,52},{24,56},{28,60},{32,0... | collective-permute-start | bytes 98312 | tf_op jit(solution)/shard_map/ppermute | solution.py:261
  189.9 12.2 %collective-permute-start.11 = (bf16[2,2,2,4,64,128]{5,4,3,2,1,0:T(8,128)(2,1)S(1)}, bf16[2,2,2,4,64,128]{5,4,3,2,1,0:T(8,128)(2,1)S(1)}, u32[]{:S(2)}, u32[]{:S(2)}) collective-permute-start(bf16[2,2,2,4,64,128]{5,4,3,2,1,0:T(8,128)(2,1)S(1)} %fusion.38), channel_id=1, source_target_pairs={{0,32},{4,36},{8,40},{12,44},{16,48},{20,52},{24,56},{28,60},{32,0... | collective-permute-start | bytes 1572872 | tf_op jit(solution)/shard_map/ppermute | solution.py:260
  191.5 13.8 %collective-permute-start.12 = (f32[2,2,8,128]{3,2,1,0:T(8,128)S(1)}, f32[2,2,8,128]{3,2,1,0:T(8,128)S(1)}, u32[]{:S(2)}, u32[]{:S(2)}) collective-permute-start(f32[2,2,8,128]{3,2,1,0:T(8,128)S(1)} %get-tuple-element.70), channel_id=1, source_target_pairs={{0,16},{4,20},{8,24},{12,28},{16,0},{20,4},{24,8},{28,12},{32,48},... | collective-permute-start | bytes 49160 | tf_op jit(solution)/shard_map/ppermute | solution.py:261
  202.4 7.2 %collective-permute-start.13 = (bf16[2,2,4,64,128]{4,3,2,1,0:T(8,128)(2,1)S(1)}, bf16[2,2,4,64,128]{4,3,2,1,0:T(8,128)(2,1)S(1)}, u32[]{:S(2)}, u32[]{:S(2)}) collective-permute-start(bf16[2,2,4,64,128]{4,3,2,1,0:T(8,128)(2,1)S(1)} %fusion.45), channel_id=1, source_target_pairs={{0,16},{4,20},{8,24},{12,28},{16,0},{20,4},{24,8},{28,12},{32,48},... | collective-permute-start | bytes 786440 | tf_op jit(solution)/shard_map/ppermute | solution.py:260
  205.3 4.6 %collective-permute-start.14 = (f32[2,8,128]{2,1,0:T(8,128)S(1)}, f32[2,8,128]{2,1,0:T(8,128)S(1)}, u32[]{:S(2)}, u32[]{:S(2)}) collective-permute-start(f32[2,8,128]{2,1,0:T(8,128)S(1)} %get-tuple-element.72), channel_id=1, source_target_pairs={{0,64},{4,68},{8,72},{12,76},{16,80},{20,84},{24,88},{28,92},{32,9... | collective-permute-start | bytes 24584 | tf_op jit(solution)/shard_map/ppermute | solution.py:261
  209.7 8.2 %collective-permute-start.15 = (bf16[2,4,64,128]{3,2,1,0:T(8,128)(2,1)S(1)}, bf16[2,4,64,128]{3,2,1,0:T(8,128)(2,1)S(1)}, u32[]{:S(2)}, u32[]{:S(2)}) collective-permute-start(bf16[2,4,64,128]{3,2,1,0:T(8,128)(2,1)S(1)} %fusion.54), channel_id=1, source_target_pairs={{0,64},{4,68},{8,72},{12,76},{16,80},{20,84},{24,88},{28,92},{32,9... | collective-permute-start | bytes 393224 | tf_op jit(solution)/shard_map/ppermute | solution.py:260
  209.9 11.9 %collective-permute-start.16 = (f32[8,128]{1,0:T(8,128)S(1)}, f32[8,128]{1,0:T(8,128)S(1)}, u32[]{:S(2)}, u32[]{:S(2)}) collective-permute-start(f32[8,128]{1,0:T(8,128)S(1)} %get-tuple-element.74), channel_id=1, source_target_pairs={{0,128},{4,132},{8,136},{12,140},{16,144},{20,148},{24,152},{28,15... | collective-permute-start | bytes 12296 | tf_op jit(solution)/shard_map/ppermute | solution.py:261
  218.1 7.1 %collective-permute-start.17 = (bf16[4,64,128]{2,1,0:T(8,128)(2,1)S(1)}, bf16[4,64,128]{2,1,0:T(8,128)(2,1)S(1)}, u32[]{:S(2)}, u32[]{:S(2)}) collective-permute-start(bf16[4,64,128]{2,1,0:T(8,128)(2,1)S(1)} %fusion.58), channel_id=1, source_target_pairs={{0,128},{4,132},{8,136},{12,140},{16,144},{20,148},{24,152},{28,15... | collective-permute-start | bytes 196616 | tf_op jit(solution)/shard_map/ppermute | solution.py:260
  225.2 4.4 %collective-permute-start.18 = (bf16[128,256]{0,1:T(8,128)(2,1)S(1)}, bf16[128,256]{0,1:T(8,128)(2,1)S(1)}, u32[]{:S(2)}, u32[]{:S(2)}) collective-permute-start(bf16[128,256]{0,1:T(8,128)(2,1)S(1)} %bitcast.211), channel_id=1, source_target_pairs={{0,1},{1,2},{2,3},{3,0},{4,5},{5,6},{6,7},{7,4},{8,9},{9,10},{10,1... | collective-permute-start | bytes 196616 | tf_op jit(solution)/shard_map/ppermute | solution.py:283
  225.7 4.6 %collective-permute-start.19 = (bf16[128,256]{0,1:T(8,128)(2,1)S(1)}, bf16[128,256]{0,1:T(8,128)(2,1)S(1)}, u32[]{:S(2)}, u32[]{:S(2)}) collective-permute-start(bf16[128,256]{0,1:T(8,128)(2,1)S(1)} %bitcast.212), channel_id=1, source_target_pairs={{0,2},{1,3},{2,0},{3,1},{4,6},{5,7},{6,4},{7,5},{8,10},{9,11},{10,... | collective-permute-start | bytes 196616 | tf_op jit(solution)/shard_map/ppermute | solution.py:283
  226.2 4.7 %collective-permute-start.20 = (bf16[128,256]{0,1:T(8,128)(2,1)S(1)}, bf16[128,256]{0,1:T(8,128)(2,1)S(1)}, u32[]{:S(2)}, u32[]{:S(2)}) collective-permute-start(bf16[128,256]{0,1:T(8,128)(2,1)S(1)} %bitcast.213), channel_id=1, source_target_pairs={{0,3},{1,0},{2,1},{3,2},{4,7},{5,4},{6,5},{7,6},{8,11},{9,8},{10,9... | collective-permute-start | bytes 196616 | tf_op jit(solution)/shard_map/ppermute | solution.py:283
  267.6 10.2 %collective-permute-start.24 = (bf16[640,256]{1,0:T(8,128)(2,1)S(1)}, bf16[640,256]{1,0:T(8,128)(2,1)S(1)}, u32[]{:S(2)}, u32[]{:S(2)}) collective-permute-start(bf16[640,256]{1,0:T(8,128)(2,1)S(1)} %reshape_squeeze.3), channel_id=1, source_target_pairs={{0,1},{1,2},{2,3},{3,0},{4,5},{5,6},{6,7},{7,4},{8,9},{9,10},{10,1... | collective-permute-start | bytes 983048 | tf_op jit(solution)/shard_map/ppermute | solution.py:283
  268.7 16.9 %collective-permute-start.25 = (bf16[640,256]{1,0:T(8,128)(2,1)S(1)}, bf16[640,256]{1,0:T(8,128)(2,1)S(1)}, u32[]{:S(2)}, u32[]{:S(2)}) collective-permute-start(bf16[640,256]{1,0:T(8,128)(2,1)S(1)} %reshape_squeeze.3), channel_id=1, source_target_pairs={{0,2},{1,3},{2,0},{3,1},{4,6},{5,7},{6,4},{7,5},{8,10},{9,11},{10,... | collective-permute-start | bytes 983048 | tf_op jit(solution)/shard_map/ppermute | solution.py:283
  271.1 14.4 %collective-permute-start.26 = (bf16[640,256]{1,0:T(8,128)(2,1)S(1)}, bf16[640,256]{1,0:T(8,128)(2,1)S(1)}, u32[]{:S(2)}, u32[]{:S(2)}) collective-permute-start(bf16[640,256]{1,0:T(8,128)(2,1)S(1)} %reshape_squeeze.3), channel_id=1, source_target_pairs={{0,3},{1,0},{2,1},{3,2},{4,7},{5,4},{6,5},{7,6},{8,11},{9,8},{10,9... | collective-permute-start | bytes 983048 | tf_op jit(solution)/shard_map/ppermute | solution.py:283
  293.5 9.9 %collective-permute-start.27 = (bf16[640,256]{1,0:T(8,128)(2,1)}, bf16[640,256]{1,0:T(8,128)(2,1)S(1)}, u32[]{:S(2)}, u32[]{:S(2)}) collective-permute-start(bf16[640,256]{1,0:T(8,128)(2,1)} %get-tuple-element.44), channel_id=1, source_target_pairs={{0,1},{1,2},{2,3},{3,0},{4,5},{5,6},{6,7},{7,4},{8,9},{9,10},{10,1... | collective-permute-start | bytes 983048 | tf_op jit(solution)/shard_map/ppermute | solution.py:331
  294.9 17.4 %collective-permute-start.28 = (bf16[640,256]{1,0:T(8,128)(2,1)S(1)}, bf16[640,256]{1,0:T(8,128)(2,1)}, u32[]{:S(2)}, u32[]{:S(2)}) collective-permute-start(bf16[640,256]{1,0:T(8,128)(2,1)S(1)} %get-tuple-element.46), channel_id=1, source_target_pairs={{0,2},{1,3},{2,0},{3,1},{4,6},{5,7},{6,4},{7,5},{8,10},{9,11},{10,... | collective-permute-start | bytes 983048 | tf_op jit(solution)/shard_map/ppermute | solution.py:331
  297.6 14.6 %collective-permute-start.29 = (bf16[640,256]{1,0:T(8,128)(2,1)S(1)}, bf16[640,256]{1,0:T(8,128)(2,1)}, u32[]{:S(2)}, u32[]{:S(2)}) collective-permute-start(bf16[640,256]{1,0:T(8,128)(2,1)S(1)} %get-tuple-element.45), channel_id=1, source_target_pairs={{0,3},{1,0},{2,1},{3,2},{4,7},{5,4},{6,5},{7,6},{8,11},{9,8},{10,9... | collective-permute-start | bytes 983048 | tf_op jit(solution)/shard_map/ppermute | solution.py:331
  314.4 24.0 %all-to-all-start.1 = ((bf16[64,1,10,256]{3,2,1,0:T(8,128)(2,1)}), bf16[64,1,10,256]{3,2,1,0:T(8,128)(2,1)S(1)}, u32[]{:S(2)}, u32[]{:S(2)}) async-start(bf16[64,1,10,256]{3,2,1,0:T(8,128)(2,1)} %bitcast.79), calls=%async_computation.1 | async-start | bytes 1048576 | tf_op jit(solution)/shard_map/all_to_all | solution.py:335
  (14 other events, 81.3 us)

commit v3 on v2

--- a/solution.py
+++ b/solution.py
@@ -64,8 +64,8 @@
     is_fresh = fresh_ref[step] == 1
     keys = jnp.where(is_fresh, nk_ref[0], k_ref[0])
     vals = jnp.where(is_fresh, nv_ref[0], v_ref[0])
-    rows, cols = keys.shape[0], q_ref.shape[1]
     quarters, piece = acc_ref.shape[0], acc_ref.shape[4]
+    rows, cols = keys.shape[0], quarters * piece
     k_pos = lax.broadcasted_iota(jnp.int32, (rows, cols), 0)
     q_pos = lax.broadcasted_iota(jnp.int32, (rows, cols), 1)
     valid = (k_pos < limit_ref[step]) & (q_pos >= offset_ref[step] + k_pos)
@@ -75,10 +75,8 @@
 
     for h in range(heads):
         lanes = slice(h * DH, (h + 1) * DH)
-        s = lax.dot_general(
-            keys[:, lanes], q_ref[0, :, lanes], (((1,), (1,)), ((), ())),
-            preferred_element_type=jnp.float32,
-        ) * (DH ** (-0.5))
+        q_cols = jnp.concatenate([q_ref[0, c, h] for c in range(quarters)], axis=1)
+        s = jnp.dot(keys[:, lanes], q_cols, preferred_element_type=jnp.float32) * (DH ** (-0.5))
         s = jnp.where(valid, s, NEGATIVE)
         m_prev = joined(lambda c: stat_ref[c, 0, h : h + 1, :])
         l_prev = joined(lambda c: stat_ref[c, 0, heads + h : heads + h + 1, :])
@@ -87,10 +85,7 @@
         p = jnp.where(valid, jnp.exp(s - m_cur), 0.0)
         alpha = jnp.exp(m_prev - m_cur)
         l_cur = alpha * l_prev + jnp.sum(p, axis=0, keepdims=True)
-        pv = lax.dot_general(
-            vals[:, lanes], p.astype(jnp.bfloat16), (((0,), (0,)), ((), ())),
-            preferred_element_type=jnp.float32,
-        )
+        pv = jnp.dot(vals[lanes, :], p.astype(jnp.bfloat16), preferred_element_type=jnp.float32)
         acc_cur = alpha * acc_prev + pv
         for c in range(quarters):
             cut = slice(c * piece, (c + 1) * piece)
@@ -103,7 +98,7 @@
     owner, page, limit, offset, fresh, everyone, cache_k, cache_v, new_k, new_v, heads, requests,
     piece,
 ):
-    span_rows, width = everyone.shape[1], everyone.shape[2]
+    span_rows, width = everyone.shape[1] * everyone.shape[4], cache_k.shape[2]
     page_rows = cache_k.shape[1]
     blocks = owner.shape[0]
     by_owner = lambda b, own, pg, lim, off, fr: (own[b], 0, 0)
@@ -116,11 +111,11 @@
         num_scalar_prefetch=5,
         grid=(blocks,),
         in_specs=[
-            pl.BlockSpec((1, span_rows, width), by_owner),
+            pl.BlockSpec((1,) + everyone.shape[1:], lambda b, own, pg, lim, off, fr: (own[b], 0, 0, 0, 0)),
             pl.BlockSpec((1, page_rows, width), by_page),
-            pl.BlockSpec((1, page_rows, width), by_page),
+            pl.BlockSpec((1, width, page_rows), by_page),
             pl.BlockSpec((1, page_rows, width), fixed),
-            pl.BlockSpec((1, page_rows, width), fixed),
+            pl.BlockSpec((1, width, page_rows), fixed),
         ],
         out_specs=[
             pl.BlockSpec((quarters, 1, heads, DH, piece), acc_map),
@@ -201,7 +196,7 @@
     sorted_offset = query_offsets[block_order]
     sorted_fresh = (block_order == page_count).astype(jnp.int32)
     sorted_page = jnp.minimum(block_order, page_count - 1)
-    gathered = queries
+    gathered = jnp.transpose(queries.reshape(tok_rows, local_heads, DH), (1, 2, 0))
     held_bits = []
     gather_count = seq_count.bit_length() - 1
     for bit in ([5, 4, 2, 3, 1, 0] if gather_count == 6 else list(range(gather_count - 1, -1, -1))):
@@ -213,7 +208,9 @@
             [jnp.where(low_side, gathered, got), jnp.where(low_side, got, gathered)], axis=position
         )
         held_bits.insert(position, bit)
-    everyone = gathered.reshape(request_total, span_rows, local_heads * DH)
+    everyone = gathered.reshape(
+        request_total, span_rows // tok_rows, local_heads, DH, tok_rows
+    )
     width_heads = local_heads * DH
     acc_out, stat_out = local_attention(
         sorted_owner,
@@ -223,9 +220,9 @@
         sorted_fresh,
         everyone,
         cache_k,
-        cache_v,
+        jnp.swapaxes(cache_v, 1, 2),
         new_keys.reshape(1, tok_rows, width_heads),
-        new_values.reshape(1, tok_rows, width_heads),
+        new_values.reshape(tok_rows, width_heads).T[None],
         local_heads,
         request_total,
         tok_rows,

time: 341 us -> 357 us (1.047); the launches traced: 341 us -> 352 us
  starting transfers between devices: 64 us -> 73.4 us
  local copies, waits for them, and re-layouts: 26.9 us -> 31.8 us
    ppermute x9, starting transfers between devices: 11.9 us -> 21.3 us  [tp_gather(): lax.ppermute(value, 'tp', [(i, (i + k) % tp_count) for i in range(tp_coun...]
    unnamed x32 -> x33, local copies, waits for them, and re-layouts: 8.61 us -> 12.8 us
  transfers between devices with their start and end apart: 31 -> 31, of which waited for: 19 -> 18; matrix products, arithmetic and copies ran while one was open for 10% -> 10% of each run, Pallas kernels for 0% -> 0%
where the time goes in v3:
time: 357 us; the launch traced here: 352 us
  waiting for transfers between devices  124 us (35%)
  starting transfers between devices  73.4 us (21%)
  Pallas kernels  46 us (13%)
  blocking collectives  32.3 us (9%)
  local copies, waits for them, and re-layouts  31.8 us (9%)
  other arithmetic  28.3 us (8%)
  matrix products  15.4 us (4%)
    pallas_call x1, Pallas kernels, local_attention(): pl.pallas_call(attend_kernel, grid_spec=grid_spec, out_shape=[jax.ShapeDt...  46 us
    ppermute x6, waiting for transfers between devices, shards(): got = lax.ppermute(gathered, 'seq', pairs)  44.3 us
    all_to_all x1, blocking collectives, shards(): lax.all_to_all(outgoing, 'seq', split_axis=0, concat_axis=0, tiled=True)  32.3 us
    ppermute x9, waiting for transfers between devices, tp_gather(): lax.ppermute(value, 'tp', [(i, (i + k) % tp_count) for i in range(tp_coun...  24.8 us
    ppermute x9, starting transfers between devices, tp_gather(): lax.ppermute(value, 'tp', [(i, (i + k) % tp_count) for i in range(tp_coun...  21.3 us
    ppermute x6, starting transfers between devices, shards(): got = lax.ppermute(gathered, 'seq', pairs)  19.4 us
    ppermute x6, waiting for transfers between devices, shards(): lax.ppermute(send_acc.astype(jnp.bfloat16), 'seq', pairs)  15.4 us
    ppermute x3, waiting for transfers between devices, shards(): lax.ppermute(target_cols, 'tp', [(i, (i + k) % tp_count) for i in range(t...  14.4 us
  transfers between devices with their start and end apart: 31, of which 18 were waited for; matrix products, arithmetic and copies ran while one was open for 10% of the time, Pallas kernels for 0%

profile of v3, /device:TPU:1, one launch (start us, length us, event | category | flops | bytes accessed | tf_op | source)
XLA Modules:
  0.0 351.8 jit_solution(17704227075668622118)
XLA Ops:
  2.7 7.8 %collective-permute-start = (bf16[4,64,128]{2,1,0:T(8,128)(2,1)S(1)}, bf16[4,64,128]{2,1,0:T(8,128)(2,1)S(1)}, u32[]{:S(2)}, u32[]{:S(2)}) collective-permute-start(bf16[4,64,128]{2,1,0:T(8,128)(2,1)S(1)} %bitcast.218), channel_id=1, source_target_pairs={{0,128},{4,132},{8,136},{12,140},{16,144},{20,148},{24,152},{28,15... | collective-permute-start | bytes 196616 | tf_op jit(solution)/shard_map/ppermute | solution.py:204
  13.7 5.4 %collective-permute-done.1 = bf16[2,4,64,128]{3,2,1,0:T(8,128)(2,1)S(1)} collective-permute-done((bf16[2,4,64,128]{3,2,1,0:T(8,128)(2,1)S(1)}, bf16[2,4,64,128]{3,2,1,0:T(8,128)(2,1)S(1)}, u32[]{:S(2)}, u32[]{:S(2)}) %collective-permute-start.1) | collective-permute-done | bytes 131104 | tf_op jit(solution)/shard_map/ppermute | solution.py:204
  19.2 4.6 %collective-permute-start.2 = (bf16[2,2,4,64,128]{4,3,2,0,1:T(8,128)(2,1)S(1)}, bf16[2,2,4,64,128]{4,3,2,0,1:T(8,128)(2,1)S(1)}, u32[]{:S(2)}, u32[]{:S(2)}) collective-permute-start(bf16[2,2,4,64,128]{4,3,2,0,1:T(8,128)(2,1)S(1)} %pad_maximum_fusion.7), channel_id=1, source_target_pairs={{0,16},{4,20},{8,24},{12,28},{16,0},{20,4},{24,8},{28,12},{32,48},... | collective-permute-start | bytes 786440 | tf_op jit(solution)/shard_map/ppermute | solution.py:204
  23.8 5.1 %collective-permute-done.2 = bf16[2,2,4,64,128]{4,3,2,0,1:T(8,128)(2,1)S(1)} collective-permute-done((bf16[2,2,4,64,128]{4,3,2,0,1:T(8,128)(2,1)S(1)}, bf16[2,2,4,64,128]{4,3,2,0,1:T(8,128)(2,1)S(1)}, u32[]{:S(2)}, u32[]{:S(2)}) %collective-permute-start.2) | collective-permute-done | bytes 262176 | tf_op jit(solution)/shard_map/ppermute | solution.py:204
  29.1 11.3 %collective-permute-done.3 = bf16[2,2,2,4,64,128]{5,4,3,0,1,2:T(8,128)(2,1)S(1)} collective-permute-done((bf16[2,2,2,4,64,128]{5,4,3,0,1,2:T(8,128)(2,1)S(1)}, bf16[2,2,2,4,64,128]{5,4,3,0,1,2:T(8,128)(2,1)S(1)}, u32[]{:S(2)}, u32[]{:S(2)}) %collective-permute-start.3) | collective-permute-done | bytes 524320 | tf_op jit(solution)/shard_map/ppermute | solution.py:204
  43.4 20.8 %collective-permute-done.4 = bf16[2,2,2,2,4,64,128]{6,5,4,0,1,3,2:T(8,128)(2,1)} collective-permute-done((bf16[2,2,2,2,4,64,128]{6,5,4,0,1,3,2:T(8,128)(2,1)S(1)}, bf16[2,2,2,2,4,64,128]{6,5,4,0,1,3,2:T(8,128)(2,1)}, u32[]{:S(2)}, u32[]{:S(2)}) %collective-permute-start.4) | collective-permute-done | bytes 1048608 | tf_op jit(solution)/shard_map/ppermute | solution.py:204
  67.2 3.5 collective-permute-start.5
  77.8 4.2 %copy.73 = bf16[33,128,256]{1,2,0:T(8,128)(2,1)} copy(bf16[33,128,256]{2,1,0:T(8,128)(2,1)} %param.23) | data formatting | bytes 4325376 | tf_op args[9]
  88.9 3.0 copy.72
  91.9 46.0 %shard_map.136 = (f32[4,16,4,64,128]{4,3,2,1,0:T(8,128)}, f32[4,16,8,128]{3,2,1,0:T(8,128)}) custom-call(s32[34]{0:T(128)} %copy-done.13, s32[34]{0:T(128)} %get-tuple-element.77.page_ref, s32[34]{0:T(128)} %gather_fusion.2, s32[34]{0:T(128)} %gather_fusion.3, s32[34]{0:T(128)} %compare_convert_fusion.fresh_ref, bf16[16,4,4,64,128]{4,3,2,1,0:T(8,128)(2,1)} %bitcast.210, ...), custom_call_target="tpu_custom_call" | custom-call | tf_op jit(solution)/shard_map/pallas_call | solution.py:125
  137.8 4.4 %broadcast_select_fusion = f32[4,16,4,64,128]{4,3,2,1,0:T(8,128)S(1)} fusion(f32[4,16,4,64,128]{4,3,2,1,0:T(8,128)} %get-tuple-element.9, pred[16]{0:T(512)(128)(4,1)S(1)} %fusion.84), kind=kLoop, calls=%fused_computation.12 | loop fusion | flops 2097152 | bytes 16777232 | tf_op jit(solution)/shard_map/jit(_where)/select_n | solution.py:234
  142.3 3.3 copy-done.2
  147.8 2.9 collective-permute-start.22
  155.6 4.0 %fusion = f32[2,2,2,2,2,4,64,128]{7,6,5,4,3,2,1,0:T(8,128)S(1)} fusion(bf16[2,2,2,2,2,4,64,128]{7,6,5,4,3,2,1,0:T(8,128)(2,1)} %collective-permute-done.7, f32[2,2,2,2,2,2,4,64,128]{8,7,6,5,4,3,2,1,0:T(8,128)} %bitcast.209, s32[]{:T(128)S(6)} %select_n.333, f32[2,2,2,2,2,4,128]{6,5,4,3,2,1,0:T(4,128)S(1)} %get-tuple-element.34, ...), kind=kLoop, calls=%fused_computation.10 | loop fusion | flops 4194304 | bytes 10616836 | tf_op jit(solution)/shard_map/add | solution.py:269
  164.5 9.0 %collective-permute-done.22 = bf16[256,1024]{1,0:T(8,128)(2,1)} collective-permute-done((bf16[256,1024]{1,0:T(8,128)(2,1)}, bf16[256,1024]{1,0:T(8,128)(2,1)}, u32[]{:S(2)}, u32[]{:S(2)}) %collective-permute-start.22) | collective-permute-done | bytes 524320 | tf_op jit(solution)/shard_map/ppermute | solution.py:280
  173.6 3.1 pad_maximum_fusion.2
  179.0 9.9 %collective-permute-done.8 = f32[2,2,2,2,8,128]{5,4,3,2,1,0:T(8,128)S(1)} collective-permute-done((f32[2,2,2,2,8,128]{5,4,3,2,1,0:T(8,128)S(1)}, f32[2,2,2,2,8,128]{5,4,3,2,1,0:T(8,128)S(1)}, u32[]{:S(2)}, u32[]{:S(2)}) %collective-permute-start.8) | collective-permute-done | bytes 65568 | tf_op jit(solution)/shard_map/ppermute | solution.py:258
  193.5 2.9 collective-permute-start.12
  196.4 7.7 %collective-permute-done.11 = bf16[2,2,2,4,64,128]{5,4,3,2,1,0:T(8,128)(2,1)S(1)} collective-permute-done((bf16[2,2,2,4,64,128]{5,4,3,2,1,0:T(8,128)(2,1)S(1)}, bf16[2,2,2,4,64,128]{5,4,3,2,1,0:T(8,128)(2,1)S(1)}, u32[]{:S(2)}, u32[]{:S(2)}) %collective-permute-start.11) | collective-permute-done | bytes 524320 | tf_op jit(solution)/shard_map/ppermute | solution.py:257
  207.4 4.3 %collective-permute-done.13 = bf16[2,2,4,64,128]{4,3,2,1,0:T(8,128)(2,1)S(1)} collective-permute-done((bf16[2,2,4,64,128]{4,3,2,1,0:T(8,128)(2,1)S(1)}, bf16[2,2,4,64,128]{4,3,2,1,0:T(8,128)(2,1)S(1)}, u32[]{:S(2)}, u32[]{:S(2)}) %collective-permute-start.13) | collective-permute-done | bytes 262176 | tf_op jit(solution)/shard_map/ppermute | solution.py:257
  212.0 8.1 %collective-permute-start.16 = (f32[8,128]{1,0:T(8,128)S(1)}, f32[8,128]{1,0:T(8,128)S(1)}, u32[]{:S(2)}, u32[]{:S(2)}) collective-permute-start(f32[8,128]{1,0:T(8,128)S(1)} %get-tuple-element.74), channel_id=1, source_target_pairs={{0,128},{4,132},{8,136},{12,140},{16,144},{20,148},{24,152},{28,15... | collective-permute-start | bytes 12296 | tf_op jit(solution)/shard_map/ppermute | solution.py:258
  220.2 3.8 %collective-permute-start.17 = (bf16[4,64,128]{2,1,0:T(8,128)(2,1)S(1)}, bf16[4,64,128]{2,1,0:T(8,128)(2,1)S(1)}, u32[]{:S(2)}, u32[]{:S(2)}) collective-permute-start(bf16[4,64,128]{2,1,0:T(8,128)(2,1)S(1)} %fusion.58), channel_id=1, source_target_pairs={{0,128},{4,132},{8,136},{12,140},{16,144},{20,148},{24,152},{28,15... | collective-permute-start | bytes 196616 | tf_op jit(solution)/shard_map/ppermute | solution.py:257
  224.0 3.3 collective-permute-done.17
  227.8 9.4 %collective-permute-start.19 = (bf16[128,256]{0,1:T(8,128)(2,1)S(1)}, bf16[128,256]{0,1:T(8,128)(2,1)S(1)}, u32[]{:S(2)}, u32[]{:S(2)}) collective-permute-start(bf16[128,256]{0,1:T(8,128)(2,1)S(1)} %bitcast.221), channel_id=1, source_target_pairs={{0,2},{1,3},{2,0},{3,1},{4,6},{5,7},{6,4},{7,5},{8,10},{9,11},{10,... | collective-permute-start | bytes 196616 | tf_op jit(solution)/shard_map/ppermute | solution.py:280
  246.1 32.3 %all_to_all.10 = bf16[64,1,10,256]{3,2,1,0:T(8,128)(2,1)S(1)} all-to-all(bf16[64,1,10,256]{3,2,1,0:T(8,128)(2,1)S(1)} %bitcast.213), channel_id=1, replica_groups=mesh['seq'=64,'tp'=4] {'seq'}, dimensions={0} | all-to-all | bytes 655360 | tf_op jit(solution)/shard_map/all_to_all | solution.py:314
  282.3 6.4 %collective-permute-done.24 = bf16[640,256]{1,0:T(8,128)(2,1)S(1)} collective-permute-done((bf16[640,256]{1,0:T(8,128)(2,1)S(1)}, bf16[640,256]{1,0:T(8,128)(2,1)S(1)}, u32[]{:S(2)}, u32[]{:S(2)}) %collective-permute-start.24) | collective-permute-done | bytes 327712 | tf_op jit(solution)/shard_map/ppermute | solution.py:280
  288.7 7.9 %collective-permute-done.25 = bf16[640,256]{1,0:T(8,128)(2,1)S(1)} collective-permute-done((bf16[640,256]{1,0:T(8,128)(2,1)S(1)}, bf16[640,256]{1,0:T(8,128)(2,1)S(1)}, u32[]{:S(2)}, u32[]{:S(2)}) %collective-permute-start.25) | collective-permute-done | bytes 327712 | tf_op jit(solution)/shard_map/ppermute | solution.py:280
  300.5 3.2 convolution_convert_fusion
  308.9 5.5 %collective-permute-done.27 = bf16[640,256]{1,0:T(8,128)(2,1)S(1)} collective-permute-done((bf16[640,256]{1,0:T(8,128)(2,1)}, bf16[640,256]{1,0:T(8,128)(2,1)S(1)}, u32[]{:S(2)}, u32[]{:S(2)}) %collective-permute-start.27) | collective-permute-done | bytes 327712 | tf_op jit(solution)/shard_map/ppermute | solution.py:328
  314.3 8.9 %collective-permute-done.28 = bf16[640,256]{1,0:T(8,128)(2,1)} collective-permute-done((bf16[640,256]{1,0:T(8,128)(2,1)S(1)}, bf16[640,256]{1,0:T(8,128)(2,1)}, u32[]{:S(2)}, u32[]{:S(2)}) %collective-permute-start.28) | collective-permute-done | bytes 327712 | tf_op jit(solution)/shard_map/ppermute | solution.py:328
  325.4 6.3 %all-to-all-start.1 = ((bf16[64,1,10,256]{3,2,1,0:T(8,128)(2,1)}), bf16[64,1,10,256]{3,2,1,0:T(8,128)(2,1)S(1)}, u32[]{:S(2)}, u32[]{:S(2)}) async-start(bf16[64,1,10,256]{3,2,1,0:T(8,128)(2,1)} %bitcast.84), calls=%async_computation.1 | async-start | bytes 1048576 | tf_op jit(solution)/shard_map/all_to_all | solution.py:332
  335.3 14.1 %all-to-all-done.1 = bf16[64,1,10,256]{3,2,1,0:T(8,128)(2,1)S(1)} async-done(((bf16[64,1,10,256]{3,2,1,0:T(8,128)(2,1)}), bf16[64,1,10,256]{3,2,1,0:T(8,128)(2,1)S(1)}, u32[]{:S(2)}, u32[]{:S(2)}) %all-to-all-start.1) | async-done | bytes 327712 | tf_op jit(solution)/shard_map/all_to_all | solution.py:332
  (182 shorter events, 78.6 us)
Async XLA Ops:
  0.0 300.5 %copy-start = (bf16[1,352,1024]{2,1,0:T(8,128)(2,1)S(1)}, bf16[1,352,1024]{2,1,0:T(8,128)(2,1)}, u32[]{:S(2)}) copy-start(bf16[1,352,1024]{2,1,0:T(8,128)(2,1)} %param.27) | copy-start | bytes 2162692
  2.7 9.6 %collective-permute-start = (bf16[4,64,128]{2,1,0:T(8,128)(2,1)S(1)}, bf16[4,64,128]{2,1,0:T(8,128)(2,1)S(1)}, u32[]{:S(2)}, u32[]{:S(2)}) collective-permute-start(bf16[4,64,128]{2,1,0:T(8,128)(2,1)S(1)} %bitcast.218), channel_id=1, source_target_pairs={{0,128},{4,132},{8,136},{12,140},{16,144},{20,148},{24,152},{28,15... | collective-permute-start | bytes 196616 | tf_op jit(solution)/shard_map/ppermute | solution.py:204
  12.3 6.9 %collective-permute-start.1 = (bf16[2,4,64,128]{3,2,1,0:T(8,128)(2,1)S(1)}, bf16[2,4,64,128]{3,2,1,0:T(8,128)(2,1)S(1)}, u32[]{:S(2)}, u32[]{:S(2)}) collective-permute-start(bf16[2,4,64,128]{3,2,1,0:T(8,128)(2,1)S(1)} %pad_maximum_fusion.12), channel_id=1, source_target_pairs={{0,64},{4,68},{8,72},{12,76},{16,80},{20,84},{24,88},{28,92},{32,9... | collective-permute-start | bytes 393224 | tf_op jit(solution)/shard_map/ppermute | solution.py:204
  19.2 9.7 %collective-permute-start.2 = (bf16[2,2,4,64,128]{4,3,2,0,1:T(8,128)(2,1)S(1)}, bf16[2,2,4,64,128]{4,3,2,0,1:T(8,128)(2,1)S(1)}, u32[]{:S(2)}, u32[]{:S(2)}) collective-permute-start(bf16[2,2,4,64,128]{4,3,2,0,1:T(8,128)(2,1)S(1)} %pad_maximum_fusion.7), channel_id=1, source_target_pairs={{0,16},{4,20},{8,24},{12,28},{16,0},{20,4},{24,8},{28,12},{32,48},... | collective-permute-start | bytes 786440 | tf_op jit(solution)/shard_map/ppermute | solution.py:204
  29.0 11.4 %collective-permute-start.3 = (bf16[2,2,2,4,64,128]{5,4,3,0,1,2:T(8,128)(2,1)S(1)}, bf16[2,2,2,4,64,128]{5,4,3,0,1,2:T(8,128)(2,1)S(1)}, u32[]{:S(2)}, u32[]{:S(2)}) collective-permute-start(bf16[2,2,2,4,64,128]{5,4,3,0,1,2:T(8,128)(2,1)S(1)} %pad_maximum_fusion.6), channel_id=1, source_target_pairs={{0,32},{4,36},{8,40},{12,44},{16,48},{20,52},{24,56},{28,60},{32,0... | collective-permute-start | bytes 1572872 | tf_op jit(solution)/shard_map/ppermute | solution.py:204
  41.4 22.7 %collective-permute-start.4 = (bf16[2,2,2,2,4,64,128]{6,5,4,0,1,3,2:T(8,128)(2,1)S(1)}, bf16[2,2,2,2,4,64,128]{6,5,4,0,1,3,2:T(8,128)(2,1)}, u32[]{:S(2)}, u32[]{:S(2)}) collective-permute-start(bf16[2,2,2,2,4,64,128]{6,5,4,0,1,3,2:T(8,128)(2,1)S(1)} %pad_maximum_fusion.5), channel_id=1, source_target_pairs={{0,8},{4,12},{8,0},{12,4},{16,24},{20,28},{24,16},{28,20},{32,40},... | collective-permute-start | bytes 3145736 | tf_op jit(solution)/shard_map/ppermute | solution.py:204
  67.2 19.5 %collective-permute-start.5 = (bf16[2,2,2,2,2,4,64,128]{7,6,5,0,1,3,2,4:T(8,128)(2,1)}, bf16[2,2,2,2,2,4,64,128]{7,6,5,0,1,3,2,4:T(8,128)(2,1)}, u32[]{:S(2)}, u32[]{:S(2)}) collective-permute-start(bf16[2,2,2,2,2,4,64,128]{7,6,5,0,1,3,2,4:T(8,128)(2,1)} %pad_maximum_fusion.1), channel_id=1, source_target_pairs={{0,4},{4,0},{8,12},{12,8},{16,20},{20,16},{24,28},{28,24},{32,36},... | collective-permute-start | bytes 6291464 | tf_op jit(solution)/shard_map/ppermute | solution.py:204
  146.1 9.6 %collective-permute-start.7 = (bf16[2,2,2,2,2,4,64,128]{7,6,5,4,3,2,1,0:T(8,128)(2,1)S(1)}, bf16[2,2,2,2,2,4,64,128]{7,6,5,4,3,2,1,0:T(8,128)(2,1)}, u32[]{:S(2)}, u32[]{:S(2)}) collective-permute-start(bf16[2,2,2,2,2,4,64,128]{7,6,5,4,3,2,1,0:T(8,128)(2,1)S(1)} %fusion.1), channel_id=1, source_target_pairs={{0,4},{4,0},{8,12},{12,8},{16,20},{20,16},{24,28},{28,24},{32,36},... | collective-permute-start | bytes 6291464 | tf_op jit(solution)/shard_map/ppermute | solution.py:257
  146.2 18.3 %collective-permute-start.21 = (bf16[256,1024]{1,0:T(8,128)(2,1)}, bf16[256,1024]{1,0:T(8,128)(2,1)}, u32[]{:S(2)}, u32[]{:S(2)}) collective-permute-start(bf16[256,1024]{1,0:T(8,128)(2,1)} %param.21), channel_id=1, source_target_pairs={{0,1},{1,2},{2,3},{3,0},{4,5},{5,6},{6,7},{7,4},{8,9},{9,10},{10,1... | collective-permute-start | bytes 1572872 | tf_op jit(solution)/shard_map/ppermute | solution.py:280
  147.8 25.8 %collective-permute-start.22 = (bf16[256,1024]{1,0:T(8,128)(2,1)}, bf16[256,1024]{1,0:T(8,128)(2,1)}, u32[]{:S(2)}, u32[]{:S(2)}) collective-permute-start(bf16[256,1024]{1,0:T(8,128)(2,1)} %param.21), channel_id=1, source_target_pairs={{0,2},{1,3},{2,0},{3,1},{4,6},{5,7},{6,4},{7,5},{8,10},{9,11},{10,... | collective-permute-start | bytes 1572872 | tf_op jit(solution)/shard_map/ppermute | solution.py:280
  150.7 22.9 %collective-permute-start.23 = (bf16[256,1024]{1,0:T(8,128)(2,1)}, bf16[256,1024]{1,0:T(8,128)(2,1)}, u32[]{:S(2)}, u32[]{:S(2)}) collective-permute-start(bf16[256,1024]{1,0:T(8,128)(2,1)} %param.21), channel_id=1, source_target_pairs={{0,3},{1,0},{2,1},{3,2},{4,7},{5,4},{6,5},{7,6},{8,11},{9,8},{10,9... | collective-permute-start | bytes 1572872 | tf_op jit(solution)/shard_map/ppermute | solution.py:280
  153.2 2.3 collective-permute-start.6
  162.8 26.6 %collective-permute-start.9 = (bf16[2,2,2,2,4,64,128]{6,5,4,3,2,1,0:T(8,128)(2,1)}, bf16[2,2,2,2,4,64,128]{6,5,4,3,2,1,0:T(8,128)(2,1)}, u32[]{:S(2)}, u32[]{:S(2)}) collective-permute-start(bf16[2,2,2,2,4,64,128]{6,5,4,3,2,1,0:T(8,128)(2,1)} %fusion.18), channel_id=1, source_target_pairs={{0,8},{4,12},{8,0},{12,4},{16,24},{20,28},{24,16},{28,20},{32,40},... | collective-permute-start | bytes 3145736 | tf_op jit(solution)/shard_map/ppermute | solution.py:257
  164.2 24.7 %collective-permute-start.8 = (f32[2,2,2,2,8,128]{5,4,3,2,1,0:T(8,128)S(1)}, f32[2,2,2,2,8,128]{5,4,3,2,1,0:T(8,128)S(1)}, u32[]{:S(2)}, u32[]{:S(2)}) collective-permute-start(f32[2,2,2,2,8,128]{5,4,3,2,1,0:T(8,128)S(1)} %get-tuple-element.64), channel_id=1, source_target_pairs={{0,8},{4,12},{8,0},{12,4},{16,24},{20,28},{24,16},{28,20},{32,40},... | collective-permute-start | bytes 196616 | tf_op jit(solution)/shard_map/ppermute | solution.py:258
  189.0 4.5 %collective-permute-start.10 = (f32[2,2,2,8,128]{4,3,2,1,0:T(8,128)S(1)}, f32[2,2,2,8,128]{4,3,2,1,0:T(8,128)S(1)}, u32[]{:S(2)}, u32[]{:S(2)}) collective-permute-start(f32[2,2,2,8,128]{4,3,2,1,0:T(8,128)S(1)} %get-tuple-element.68), channel_id=1, source_target_pairs={{0,32},{4,36},{8,40},{12,44},{16,48},{20,52},{24,56},{28,60},{32,0... | collective-permute-start | bytes 98312 | tf_op jit(solution)/shard_map/ppermute | solution.py:258
  192.0 12.2 %collective-permute-start.11 = (bf16[2,2,2,4,64,128]{5,4,3,2,1,0:T(8,128)(2,1)S(1)}, bf16[2,2,2,4,64,128]{5,4,3,2,1,0:T(8,128)(2,1)S(1)}, u32[]{:S(2)}, u32[]{:S(2)}) collective-permute-start(bf16[2,2,2,4,64,128]{5,4,3,2,1,0:T(8,128)(2,1)S(1)} %fusion.38), channel_id=1, source_target_pairs={{0,32},{4,36},{8,40},{12,44},{16,48},{20,52},{24,56},{28,60},{32,0... | collective-permute-start | bytes 1572872 | tf_op jit(solution)/shard_map/ppermute | solution.py:257
  193.5 13.7 %collective-permute-start.12 = (f32[2,2,8,128]{3,2,1,0:T(8,128)S(1)}, f32[2,2,8,128]{3,2,1,0:T(8,128)S(1)}, u32[]{:S(2)}, u32[]{:S(2)}) collective-permute-start(f32[2,2,8,128]{3,2,1,0:T(8,128)S(1)} %get-tuple-element.70), channel_id=1, source_target_pairs={{0,16},{4,20},{8,24},{12,28},{16,0},{20,4},{24,8},{28,12},{32,48},... | collective-permute-start | bytes 49160 | tf_op jit(solution)/shard_map/ppermute | solution.py:258
  204.5 7.2 %collective-permute-start.13 = (bf16[2,2,4,64,128]{4,3,2,1,0:T(8,128)(2,1)S(1)}, bf16[2,2,4,64,128]{4,3,2,1,0:T(8,128)(2,1)S(1)}, u32[]{:S(2)}, u32[]{:S(2)}) collective-permute-start(bf16[2,2,4,64,128]{4,3,2,1,0:T(8,128)(2,1)S(1)} %fusion.45), channel_id=1, source_target_pairs={{0,16},{4,20},{8,24},{12,28},{16,0},{20,4},{24,8},{28,12},{32,48},... | collective-permute-start | bytes 786440 | tf_op jit(solution)/shard_map/ppermute | solution.py:257
  207.3 4.6 %collective-permute-start.14 = (f32[2,8,128]{2,1,0:T(8,128)S(1)}, f32[2,8,128]{2,1,0:T(8,128)S(1)}, u32[]{:S(2)}, u32[]{:S(2)}) collective-permute-start(f32[2,8,128]{2,1,0:T(8,128)S(1)} %get-tuple-element.72), channel_id=1, source_target_pairs={{0,64},{4,68},{8,72},{12,76},{16,80},{20,84},{24,88},{28,92},{32,9... | collective-permute-start | bytes 24584 | tf_op jit(solution)/shard_map/ppermute | solution.py:258
  211.8 8.3 %collective-permute-start.15 = (bf16[2,4,64,128]{3,2,1,0:T(8,128)(2,1)S(1)}, bf16[2,4,64,128]{3,2,1,0:T(8,128)(2,1)S(1)}, u32[]{:S(2)}, u32[]{:S(2)}) collective-permute-start(bf16[2,4,64,128]{3,2,1,0:T(8,128)(2,1)S(1)} %fusion.54), channel_id=1, source_target_pairs={{0,64},{4,68},{8,72},{12,76},{16,80},{20,84},{24,88},{28,92},{32,9... | collective-permute-start | bytes 393224 | tf_op jit(solution)/shard_map/ppermute | solution.py:257
  212.0 12.0 %collective-permute-start.16 = (f32[8,128]{1,0:T(8,128)S(1)}, f32[8,128]{1,0:T(8,128)S(1)}, u32[]{:S(2)}, u32[]{:S(2)}) collective-permute-start(f32[8,128]{1,0:T(8,128)S(1)} %get-tuple-element.74), channel_id=1, source_target_pairs={{0,128},{4,132},{8,136},{12,140},{16,144},{20,148},{24,152},{28,15... | collective-permute-start | bytes 12296 | tf_op jit(solution)/shard_map/ppermute | solution.py:258
  220.2 7.1 %collective-permute-start.17 = (bf16[4,64,128]{2,1,0:T(8,128)(2,1)S(1)}, bf16[4,64,128]{2,1,0:T(8,128)(2,1)S(1)}, u32[]{:S(2)}, u32[]{:S(2)}) collective-permute-start(bf16[4,64,128]{2,1,0:T(8,128)(2,1)S(1)} %fusion.58), channel_id=1, source_target_pairs={{0,128},{4,132},{8,136},{12,140},{16,144},{20,148},{24,152},{28,15... | collective-permute-start | bytes 196616 | tf_op jit(solution)/shard_map/ppermute | solution.py:257
  227.3 13.1 %collective-permute-start.18 = (bf16[128,256]{0,1:T(8,128)(2,1)S(1)}, bf16[128,256]{0,1:T(8,128)(2,1)S(1)}, u32[]{:S(2)}, u32[]{:S(2)}) collective-permute-start(bf16[128,256]{0,1:T(8,128)(2,1)S(1)} %bitcast.220), channel_id=1, source_target_pairs={{0,1},{1,2},{2,3},{3,0},{4,5},{5,6},{6,7},{7,4},{8,9},{9,10},{10,1... | collective-permute-start | bytes 196616 | tf_op jit(solution)/shard_map/ppermute | solution.py:280
  227.8 13.5 %collective-permute-start.19 = (bf16[128,256]{0,1:T(8,128)(2,1)S(1)}, bf16[128,256]{0,1:T(8,128)(2,1)S(1)}, u32[]{:S(2)}, u32[]{:S(2)}) collective-permute-start(bf16[128,256]{0,1:T(8,128)(2,1)S(1)} %bitcast.221), channel_id=1, source_target_pairs={{0,2},{1,3},{2,0},{3,1},{4,6},{5,7},{6,4},{7,5},{8,10},{9,11},{10,... | collective-permute-start | bytes 196616 | tf_op jit(solution)/shard_map/ppermute | solution.py:280
  237.2 4.7 %collective-permute-start.20 = (bf16[128,256]{0,1:T(8,128)(2,1)S(1)}, bf16[128,256]{0,1:T(8,128)(2,1)S(1)}, u32[]{:S(2)}, u32[]{:S(2)}) collective-permute-start(bf16[128,256]{0,1:T(8,128)(2,1)S(1)} %bitcast.222), channel_id=1, source_target_pairs={{0,3},{1,0},{2,1},{3,2},{4,7},{5,4},{6,5},{7,6},{8,11},{9,8},{10,9... | collective-permute-start | bytes 196616 | tf_op jit(solution)/shard_map/ppermute | solution.py:280
  278.6 10.2 %collective-permute-start.24 = (bf16[640,256]{1,0:T(8,128)(2,1)S(1)}, bf16[640,256]{1,0:T(8,128)(2,1)S(1)}, u32[]{:S(2)}, u32[]{:S(2)}) collective-permute-start(bf16[640,256]{1,0:T(8,128)(2,1)S(1)} %reshape_squeeze.3), channel_id=1, source_target_pairs={{0,1},{1,2},{2,3},{3,0},{4,5},{5,6},{6,7},{7,4},{8,9},{9,10},{10,1... | collective-permute-start | bytes 983048 | tf_op jit(solution)/shard_map/ppermute | solution.py:280
  279.7 17.0 %collective-permute-start.25 = (bf16[640,256]{1,0:T(8,128)(2,1)S(1)}, bf16[640,256]{1,0:T(8,128)(2,1)S(1)}, u32[]{:S(2)}, u32[]{:S(2)}) collective-permute-start(bf16[640,256]{1,0:T(8,128)(2,1)S(1)} %reshape_squeeze.3), channel_id=1, source_target_pairs={{0,2},{1,3},{2,0},{3,1},{4,6},{5,7},{6,4},{7,5},{8,10},{9,11},{10,... | collective-permute-start | bytes 983048 | tf_op jit(solution)/shard_map/ppermute | solution.py:280
  282.2 14.4 %collective-permute-start.26 = (bf16[640,256]{1,0:T(8,128)(2,1)S(1)}, bf16[640,256]{1,0:T(8,128)(2,1)S(1)}, u32[]{:S(2)}, u32[]{:S(2)}) collective-permute-start(bf16[640,256]{1,0:T(8,128)(2,1)S(1)} %reshape_squeeze.3), channel_id=1, source_target_pairs={{0,3},{1,0},{2,1},{3,2},{4,7},{5,4},{6,5},{7,6},{8,11},{9,8},{10,9... | collective-permute-start | bytes 983048 | tf_op jit(solution)/shard_map/ppermute | solution.py:280
  304.6 9.7 %collective-permute-start.27 = (bf16[640,256]{1,0:T(8,128)(2,1)}, bf16[640,256]{1,0:T(8,128)(2,1)S(1)}, u32[]{:S(2)}, u32[]{:S(2)}) collective-permute-start(bf16[640,256]{1,0:T(8,128)(2,1)} %get-tuple-element.44), channel_id=1, source_target_pairs={{0,1},{1,2},{2,3},{3,0},{4,5},{5,6},{6,7},{7,4},{8,9},{9,10},{10,1... | collective-permute-start | bytes 983048 | tf_op jit(solution)/shard_map/ppermute | solution.py:328
  305.9 17.4 %collective-permute-start.28 = (bf16[640,256]{1,0:T(8,128)(2,1)S(1)}, bf16[640,256]{1,0:T(8,128)(2,1)}, u32[]{:S(2)}, u32[]{:S(2)}) collective-permute-start(bf16[640,256]{1,0:T(8,128)(2,1)S(1)} %get-tuple-element.46), channel_id=1, source_target_pairs={{0,2},{1,3},{2,0},{3,1},{4,6},{5,7},{6,4},{7,5},{8,10},{9,11},{10,... | collective-permute-start | bytes 983048 | tf_op jit(solution)/shard_map/ppermute | solution.py:328
  308.6 14.6 %collective-permute-start.29 = (bf16[640,256]{1,0:T(8,128)(2,1)S(1)}, bf16[640,256]{1,0:T(8,128)(2,1)}, u32[]{:S(2)}, u32[]{:S(2)}) collective-permute-start(bf16[640,256]{1,0:T(8,128)(2,1)S(1)} %get-tuple-element.45), channel_id=1, source_target_pairs={{0,3},{1,0},{2,1},{3,2},{4,7},{5,4},{6,5},{7,6},{8,11},{9,8},{10,9... | collective-permute-start | bytes 983048 | tf_op jit(solution)/shard_map/ppermute | solution.py:328
  325.4 24.0 %all-to-all-start.1 = ((bf16[64,1,10,256]{3,2,1,0:T(8,128)(2,1)}), bf16[64,1,10,256]{3,2,1,0:T(8,128)(2,1)S(1)}, u32[]{:S(2)}, u32[]{:S(2)}) async-start(bf16[64,1,10,256]{3,2,1,0:T(8,128)(2,1)} %bitcast.84), calls=%async_computation.1 | async-start | bytes 1048576 | tf_op jit(solution)/shard_map/all_to_all | solution.py:332
  (14 other events, 72.9 us)

commit v4 on v2

--- a/solution.py
+++ b/solution.py
@@ -201,6 +201,11 @@
     sorted_offset = query_offsets[block_order]
     sorted_fresh = (block_order == page_count).astype(jnp.int32)
     sorted_page = jnp.minimum(block_order, page_count - 1)
+    block_tables = (sorted_owner, sorted_page, sorted_limit, sorted_offset, sorted_fresh)
+    fresh_kv = (
+        new_keys.reshape(1, tok_rows, local_heads * DH),
+        new_values.reshape(1, tok_rows, local_heads * DH),
+    )
     gathered = queries
     held_bits = []
     gather_count = seq_count.bit_length() - 1
@@ -213,8 +218,13 @@
             [jnp.where(low_side, gathered, got), jnp.where(low_side, got, gathered)], axis=position
         )
         held_bits.insert(position, bit)
+        if len(held_bits) == 1:
+            gathered, block_tables, fresh_kv = lax.optimization_barrier(
+                (gathered, block_tables, fresh_kv)
+            )
     everyone = gathered.reshape(request_total, span_rows, local_heads * DH)
     width_heads = local_heads * DH
+    sorted_owner, sorted_page, sorted_limit, sorted_offset, sorted_fresh = block_tables
     acc_out, stat_out = local_attention(
         sorted_owner,
         sorted_page,
@@ -224,8 +234,8 @@
         everyone,
         cache_k,
         cache_v,
-        new_keys.reshape(1, tok_rows, width_heads),
-        new_values.reshape(1, tok_rows, width_heads),
+        fresh_kv[0],
+        fresh_kv[1],
         local_heads,
         request_total,
         tok_rows,

time: 341 us -> 346 us (1.015)
  waiting for transfers between devices: 124 us -> 133 us
  starting transfers between devices: 64 us -> 56.2 us
    ppermute x6, waiting for transfers between devices: 44.3 us -> 49.8 us  [shards(): got = lax.ppermute(gathered, 'seq', pairs)]
    ppermute x6, starting transfers between devices: 13.1 us -> 8.49 us  [shards(): got_stats = lax.ppermute(send_stats, 'seq', pairs)]
    ppermute x6, waiting for transfers between devices: 10.5 us -> 14.5 us  [shards(): got_stats = lax.ppermute(send_stats, 'seq', pairs)]
    ppermute x9, waiting for transfers between devices: 25.3 us -> 21.8 us  [tp_gather(): lax.ppermute(value, 'tp', [(i, (i + k) % tp_count) for i in range(tp_coun...]
    unnamed x32 -> x34, local copies, waits for them, and re-layouts: 8.61 us -> 9.99 us
  transfers between devices with their start and end apart: 31 -> 31, of which waited for: 19 -> 21; matrix products, arithmetic and copies ran while one was open for 10% -> 11% of each run, Pallas kernels for 0% -> 0%
where the time goes in v4:
time: 346 us; the launch traced here: 345 us
  waiting for transfers between devices  133 us (38%)
  starting transfers between devices  56.2 us (16%)
  Pallas kernels  49.2 us (14%)
  other arithmetic  31.8 us (9%)
  blocking collectives  30.1 us (9%)
  local copies, waits for them, and re-layouts  29.6 us (9%)
  matrix products  14.3 us (4%)
    ppermute x6, waiting for transfers between devices, shards(): got = lax.ppermute(gathered, 'seq', pairs)  49.8 us
    pallas_call x1, Pallas kernels, local_attention(): pl.pallas_call(attend_kernel, grid_spec=grid_spec, out_shape=[jax.ShapeDt...  49.2 us
    all_to_all x1, blocking collectives, shards(): lax.all_to_all(outgoing, 'seq', split_axis=0, concat_axis=0, tiled=True)  30.1 us
    ppermute x9, waiting for transfers between devices, tp_gather(): lax.ppermute(value, 'tp', [(i, (i + k) % tp_count) for i in range(tp_coun...  21.8 us
    ppermute x6, waiting for transfers between devices, shards(): lax.ppermute(send_acc.astype(jnp.bfloat16), 'seq', pairs)  18.4 us
    ppermute x6, starting transfers between devices, shards(): got = lax.ppermute(gathered, 'seq', pairs)  16.8 us
    ppermute x6, waiting for transfers between devices, shards(): got_stats = lax.ppermute(send_stats, 'seq', pairs)  14.5 us
    ppermute x3, waiting for transfers between devices, shards(): lax.ppermute(target_cols, 'tp', [(i, (i + k) % tp_count) for i in range(t...  14.4 us
  transfers between devices with their start and end apart: 31, of which 21 were waited for; matrix products, arithmetic and copies ran while one was open for 11% of the time, Pallas kernels for 0%

profile of v4, /device:TPU:1, one launch (start us, length us, event | category | flops | bytes accessed | tf_op | source)
XLA Modules:
  0.0 344.8 jit_solution(9337354859614890706)
XLA Ops:
  2.6 7.8 %collective-permute-start = (bf16[128,256]{1,0:T(8,128)(2,1)S(1)}, bf16[128,256]{1,0:T(8,128)(2,1)S(1)}, u32[]{:S(2)}, u32[]{:S(2)}) collective-permute-start(bf16[128,256]{1,0:T(8,128)(2,1)S(1)} %convolution_convert_fusion.4), channel_id=1, source_target_pairs={{0,128},{4,132},{8,136},{12,140},{16,144},{20,148},{24,152},{28,15... | collective-permute-start | bytes 196616 | tf_op jit(solution)/shard_map/ppermute | solution.py:214
  23.9 7.5 %collective-permute-done.1 = bf16[2,128,256]{2,1,0:T(8,128)(2,1)S(1)} collective-permute-done((bf16[2,128,256]{2,1,0:T(8,128)(2,1)S(1)}, bf16[2,128,256]{2,1,0:T(8,128)(2,1)S(1)}, u32[]{:S(2)}, u32[]{:S(2)}) %collective-permute-start.1) | collective-permute-done | bytes 131104 | tf_op jit(solution)/shard_map/ppermute | solution.py:214
  31.4 2.8 collective-permute-start.2
  34.3 5.7 %collective-permute-done.2 = bf16[2,2,128,256]{3,2,0,1:T(8,128)(2,1)S(1)} collective-permute-done((bf16[2,2,128,256]{3,2,0,1:T(8,128)(2,1)S(1)}, bf16[2,2,128,256]{3,2,0,1:T(8,128)(2,1)S(1)}, u32[]{:S(2)}, u32[]{:S(2)}) %collective-permute-start.2) | collective-permute-done | bytes 262176 | tf_op jit(solution)/shard_map/ppermute | solution.py:214
  40.2 11.7 %collective-permute-done.3 = bf16[2,2,2,128,256]{4,3,0,1,2:T(8,128)(2,1)S(1)} collective-permute-done((bf16[2,2,2,128,256]{4,3,0,1,2:T(8,128)(2,1)S(1)}, bf16[2,2,2,128,256]{4,3,0,1,2:T(8,128)(2,1)S(1)}, u32[]{:S(2)}, u32[]{:S(2)}) %collective-permute-start.3) | collective-permute-done | bytes 524320 | tf_op jit(solution)/shard_map/ppermute | solution.py:214
  54.1 21.0 %collective-permute-done.4 = bf16[2,2,2,2,128,256]{5,4,0,1,3,2:T(8,128)(2,1)} collective-permute-done((bf16[2,2,2,2,128,256]{5,4,0,1,3,2:T(8,128)(2,1)S(1)}, bf16[2,2,2,2,128,256]{5,4,0,1,3,2:T(8,128)(2,1)}, u32[]{:S(2)}, u32[]{:S(2)}) %collective-permute-start.4) | collective-permute-done | bytes 1048608 | tf_op jit(solution)/shard_map/ppermute | solution.py:214
  78.1 3.5 %collective-permute-start.5 = (bf16[2,2,2,2,2,128,256]{6,5,0,1,3,2,4:T(8,128)(2,1)}, bf16[2,2,2,2,2,128,256]{6,5,0,1,3,2,4:T(8,128)(2,1)}, u32[]{:S(2)}, u32[]{:S(2)}) collective-permute-start(bf16[2,2,2,2,2,128,256]{6,5,0,1,3,2,4:T(8,128)(2,1)} %pad_maximum_fusion.1), channel_id=1, source_target_pairs={{0,4},{4,0},{8,12},{12,8},{16,20},{20,16},{24,28},{28,24},{32,36},... | collective-permute-start | bytes 6291464 | tf_op jit(solution)/shard_map/ppermute | solution.py:214
  81.7 4.0 %collective-permute-done.5 = bf16[2,2,2,2,2,128,256]{6,5,0,1,3,2,4:T(8,128)(2,1)} collective-permute-done((bf16[2,2,2,2,2,128,256]{6,5,0,1,3,2,4:T(8,128)(2,1)}, bf16[2,2,2,2,2,128,256]{6,5,0,1,3,2,4:T(8,128)(2,1)}, u32[]{:S(2)}, u32[]{:S(2)}) %collective-permute-start.5) | collective-permute-done | bytes 2097184 | tf_op jit(solution)/shard_map/ppermute | solution.py:214
  90.3 49.2 %shard_map.136 = (f32[4,16,4,64,128]{4,3,2,1,0:T(8,128)}, f32[4,16,8,128]{3,2,1,0:T(8,128)}) custom-call(s32[34]{0:T(128)} %copy-done.14, s32[34]{0:T(128)} %get-tuple-element.18.page_ref, s32[34]{0:T(128)} %gather_fusion.2, s32[34]{0:T(128)} %gather_fusion.3, s32[34]{0:T(128)} %compare_convert_fusion.fresh_ref, bf16[16,512,256]{2,1,0:T(8,128)(2,1)} %bitcast.204, ...), custom_call_target="tpu_custom_call" | custom-call | tf_op jit(solution)/shard_map/pallas_call | solution.py:130
  139.5 4.4 %broadcast_select_fusion = f32[4,16,4,64,128]{4,3,2,1,0:T(8,128)S(1)} fusion(f32[4,16,4,64,128]{4,3,2,1,0:T(8,128)} %get-tuple-element.25, pred[16]{0:T(512)(128)(4,1)S(1)} %fusion.84), kind=kLoop, calls=%fused_computation.12 | loop fusion | flops 2097152 | bytes 16777232 | tf_op jit(solution)/shard_map/jit(_where)/select_n | solution.py:247
  143.9 3.3 copy-done.1
  149.5 2.6 collective-permute-start.22
  159.9 4.0 %fusion = f32[2,2,2,2,2,4,64,128]{7,6,5,4,3,2,1,0:T(8,128)S(1)} fusion(bf16[2,2,2,2,2,4,64,128]{7,6,5,4,3,2,1,0:T(8,128)(2,1)} %collective-permute-done.7, f32[2,2,2,2,2,2,4,64,128]{8,7,6,5,4,3,2,1,0:T(8,128)} %bitcast.203, s32[]{:T(128)S(6)} %select_n.333, f32[2,2,2,2,2,4,128]{6,5,4,3,2,1,0:T(4,128)S(1)} %get-tuple-element.50, ...), kind=kLoop, calls=%fused_computation.10 | loop fusion | flops 4194304 | bytes 10616836 | tf_op jit(solution)/shard_map/add | solution.py:282
  169.3 5.8 %collective-permute-done.22 = bf16[256,1024]{1,0:T(8,128)(2,1)} collective-permute-done((bf16[256,1024]{1,0:T(8,128)(2,1)S(1)}, bf16[256,1024]{1,0:T(8,128)(2,1)}, u32[]{:S(2)}, u32[]{:S(2)}) %collective-permute-start.22) | collective-permute-done | bytes 524320 | tf_op jit(solution)/shard_map/ppermute | solution.py:293
  175.1 3.0 pad_maximum_fusion.2
  180.4 12.8 %collective-permute-done.8 = f32[2,2,2,2,8,128]{5,4,3,2,1,0:T(8,128)S(1)} collective-permute-done((f32[2,2,2,2,8,128]{5,4,3,2,1,0:T(8,128)}, f32[2,2,2,2,8,128]{5,4,3,2,1,0:T(8,128)S(1)}, u32[]{:S(2)}, u32[]{:S(2)}) %collective-permute-start.8) | collective-permute-done | bytes 65568 | tf_op jit(solution)/shard_map/ppermute | solution.py:271
  195.2 2.4 fusion.10
  199.3 2.8 collective-permute-start.12
  202.1 7.8 %collective-permute-done.11 = bf16[2,2,2,4,64,128]{5,4,3,2,1,0:T(8,128)(2,1)S(1)} collective-permute-done((bf16[2,2,2,4,64,128]{5,4,3,2,1,0:T(8,128)(2,1)S(1)}, bf16[2,2,2,4,64,128]{5,4,3,2,1,0:T(8,128)(2,1)S(1)}, u32[]{:S(2)}, u32[]{:S(2)}) %collective-permute-start.11) | collective-permute-done | bytes 524320 | tf_op jit(solution)/shard_map/ppermute | solution.py:270
  210.2 2.8 collective-permute-start.13
  214.8 2.6 collective-permute-done.13
  225.8 5.8 %collective-permute-done.17 = bf16[4,64,128]{2,1,0:T(8,128)(2,1)S(1)} collective-permute-done((bf16[4,64,128]{2,1,0:T(8,128)(2,1)S(1)}, bf16[4,64,128]{2,1,0:T(8,128)(2,1)S(1)}, u32[]{:S(2)}, u32[]{:S(2)}) %collective-permute-start.17) | collective-permute-done | bytes 65568 | tf_op jit(solution)/shard_map/ppermute | solution.py:270
  241.5 30.1 %all_to_all.10 = bf16[64,1,10,256]{3,2,1,0:T(8,128)(2,1)S(1)} all-to-all(bf16[64,1,10,256]{3,2,1,0:T(8,128)(2,1)S(1)} %bitcast.206), channel_id=1, replica_groups=mesh['seq'=64,'tp'=4] {'seq'}, dimensions={0} | all-to-all | bytes 655360 | tf_op jit(solution)/shard_map/all_to_all | solution.py:327
  272.8 2.5 collective-permute-start.25
  275.4 6.4 %collective-permute-done.24 = bf16[640,256]{1,0:T(8,128)(2,1)S(1)} collective-permute-done((bf16[640,256]{1,0:T(8,128)(2,1)S(1)}, bf16[640,256]{1,0:T(8,128)(2,1)S(1)}, u32[]{:S(2)}, u32[]{:S(2)}) %collective-permute-start.24) | collective-permute-done | bytes 327712 | tf_op jit(solution)/shard_map/ppermute | solution.py:293
  281.9 7.8 %collective-permute-done.25 = bf16[640,256]{1,0:T(8,128)(2,1)S(1)} collective-permute-done((bf16[640,256]{1,0:T(8,128)(2,1)S(1)}, bf16[640,256]{1,0:T(8,128)(2,1)S(1)}, u32[]{:S(2)}, u32[]{:S(2)}) %collective-permute-start.25) | collective-permute-done | bytes 327712 | tf_op jit(solution)/shard_map/ppermute | solution.py:293
  293.6 3.2 convolution_convert_fusion
  299.0 2.7 collective-permute-start.28
  302.0 5.5 %collective-permute-done.27 = bf16[640,256]{1,0:T(8,128)(2,1)S(1)} collective-permute-done((bf16[640,256]{1,0:T(8,128)(2,1)}, bf16[640,256]{1,0:T(8,128)(2,1)S(1)}, u32[]{:S(2)}, u32[]{:S(2)}) %collective-permute-start.27) | collective-permute-done | bytes 327712 | tf_op jit(solution)/shard_map/ppermute | solution.py:341
  307.6 8.8 %collective-permute-done.28 = bf16[640,256]{1,0:T(8,128)(2,1)} collective-permute-done((bf16[640,256]{1,0:T(8,128)(2,1)S(1)}, bf16[640,256]{1,0:T(8,128)(2,1)}, u32[]{:S(2)}, u32[]{:S(2)}) %collective-permute-start.28) | collective-permute-done | bytes 327712 | tf_op jit(solution)/shard_map/ppermute | solution.py:341
  318.6 6.3 %all-to-all-start.1 = ((bf16[64,1,10,256]{3,2,1,0:T(8,128)(2,1)}), bf16[64,1,10,256]{3,2,1,0:T(8,128)(2,1)S(1)}, u32[]{:S(2)}, u32[]{:S(2)}) async-start(bf16[64,1,10,256]{3,2,1,0:T(8,128)(2,1)} %bitcast.79), calls=%async_computation.1 | async-start | bytes 1048576 | tf_op jit(solution)/shard_map/all_to_all | solution.py:345
  328.5 14.1 %all-to-all-done.1 = bf16[64,1,10,256]{3,2,1,0:T(8,128)(2,1)S(1)} async-done(((bf16[64,1,10,256]{3,2,1,0:T(8,128)(2,1)}), bf16[64,1,10,256]{3,2,1,0:T(8,128)(2,1)S(1)}, u32[]{:S(2)}, u32[]{:S(2)}) %all-to-all-start.1) | async-done | bytes 327712 | tf_op jit(solution)/shard_map/all_to_all | solution.py:345
  (182 shorter events, 83.5 us)
Async XLA Ops:
  0.0 293.6 %copy-start = (bf16[1,352,1024]{2,1,0:T(8,128)(2,1)S(1)}, bf16[1,352,1024]{2,1,0:T(8,128)(2,1)}, u32[]{:S(2)}) copy-start(bf16[1,352,1024]{2,1,0:T(8,128)(2,1)} %param.27) | copy-start | bytes 2162692
  2.6 20.0 %collective-permute-start = (bf16[128,256]{1,0:T(8,128)(2,1)S(1)}, bf16[128,256]{1,0:T(8,128)(2,1)S(1)}, u32[]{:S(2)}, u32[]{:S(2)}) collective-permute-start(bf16[128,256]{1,0:T(8,128)(2,1)S(1)} %convolution_convert_fusion.4), channel_id=1, source_target_pairs={{0,128},{4,132},{8,136},{12,140},{16,144},{20,148},{24,152},{28,15... | collective-permute-start | bytes 196616 | tf_op jit(solution)/shard_map/ppermute | solution.py:214
  22.6 8.8 %collective-permute-start.1 = (bf16[2,128,256]{2,1,0:T(8,128)(2,1)S(1)}, bf16[2,128,256]{2,1,0:T(8,128)(2,1)S(1)}, u32[]{:S(2)}, u32[]{:S(2)}) collective-permute-start(bf16[2,128,256]{2,1,0:T(8,128)(2,1)S(1)} %pad_maximum_fusion.12), channel_id=1, source_target_pairs={{0,64},{4,68},{8,72},{12,76},{16,80},{20,84},{24,88},{28,92},{32,9... | collective-permute-start | bytes 393224 | tf_op jit(solution)/shard_map/ppermute | solution.py:214
  31.4 8.5 %collective-permute-start.2 = (bf16[2,2,128,256]{3,2,0,1:T(8,128)(2,1)S(1)}, bf16[2,2,128,256]{3,2,0,1:T(8,128)(2,1)S(1)}, u32[]{:S(2)}, u32[]{:S(2)}) collective-permute-start(bf16[2,2,128,256]{3,2,0,1:T(8,128)(2,1)S(1)} %pad_maximum_fusion.7), channel_id=1, source_target_pairs={{0,16},{4,20},{8,24},{12,28},{16,0},{20,4},{24,8},{28,12},{32,48},... | collective-permute-start | bytes 786440 | tf_op jit(solution)/shard_map/ppermute | solution.py:214
  40.1 11.8 %collective-permute-start.3 = (bf16[2,2,2,128,256]{4,3,0,1,2:T(8,128)(2,1)S(1)}, bf16[2,2,2,128,256]{4,3,0,1,2:T(8,128)(2,1)S(1)}, u32[]{:S(2)}, u32[]{:S(2)}) collective-permute-start(bf16[2,2,2,128,256]{4,3,0,1,2:T(8,128)(2,1)S(1)} %pad_maximum_fusion.6), channel_id=1, source_target_pairs={{0,32},{4,36},{8,40},{12,44},{16,48},{20,52},{24,56},{28,60},{32,0... | collective-permute-start | bytes 1572872 | tf_op jit(solution)/shard_map/ppermute | solution.py:214
  52.8 22.2 %collective-permute-start.4 = (bf16[2,2,2,2,128,256]{5,4,0,1,3,2:T(8,128)(2,1)S(1)}, bf16[2,2,2,2,128,256]{5,4,0,1,3,2:T(8,128)(2,1)}, u32[]{:S(2)}, u32[]{:S(2)}) collective-permute-start(bf16[2,2,2,2,128,256]{5,4,0,1,3,2:T(8,128)(2,1)S(1)} %pad_maximum_fusion.5), channel_id=1, source_target_pairs={{0,8},{4,12},{8,0},{12,4},{16,24},{20,28},{24,16},{28,20},{32,40},... | collective-permute-start | bytes 3145736 | tf_op jit(solution)/shard_map/ppermute | solution.py:214
  78.1 7.6 %collective-permute-start.5 = (bf16[2,2,2,2,2,128,256]{6,5,0,1,3,2,4:T(8,128)(2,1)}, bf16[2,2,2,2,2,128,256]{6,5,0,1,3,2,4:T(8,128)(2,1)}, u32[]{:S(2)}, u32[]{:S(2)}) collective-permute-start(bf16[2,2,2,2,2,128,256]{6,5,0,1,3,2,4:T(8,128)(2,1)} %pad_maximum_fusion.1), channel_id=1, source_target_pairs={{0,4},{4,0},{8,12},{12,8},{16,20},{20,16},{24,28},{28,24},{32,36},... | collective-permute-start | bytes 6291464 | tf_op jit(solution)/shard_map/ppermute | solution.py:214
  147.7 12.2 %collective-permute-start.7 = (bf16[2,2,2,2,2,4,64,128]{7,6,5,4,3,2,1,0:T(8,128)(2,1)S(1)}, bf16[2,2,2,2,2,4,64,128]{7,6,5,4,3,2,1,0:T(8,128)(2,1)}, u32[]{:S(2)}, u32[]{:S(2)}) collective-permute-start(bf16[2,2,2,2,2,4,64,128]{7,6,5,4,3,2,1,0:T(8,128)(2,1)S(1)} %fusion.1), channel_id=1, source_target_pairs={{0,4},{4,0},{8,12},{12,8},{16,20},{20,16},{24,28},{28,24},{32,36},... | collective-permute-start | bytes 6291464 | tf_op jit(solution)/shard_map/ppermute | solution.py:270
  148.2 21.1 %collective-permute-start.21 = (bf16[256,1024]{1,0:T(8,128)(2,1)S(1)}, bf16[256,1024]{1,0:T(8,128)(2,1)}, u32[]{:S(2)}, u32[]{:S(2)}) collective-permute-start(bf16[256,1024]{1,0:T(8,128)(2,1)S(1)} %copy-done.10), channel_id=1, source_target_pairs={{0,1},{1,2},{2,3},{3,0},{4,5},{5,6},{6,7},{7,4},{8,9},{9,10},{10,1... | collective-permute-start | bytes 1572872 | tf_op jit(solution)/shard_map/ppermute | solution.py:293
  149.5 25.6 %collective-permute-start.22 = (bf16[256,1024]{1,0:T(8,128)(2,1)S(1)}, bf16[256,1024]{1,0:T(8,128)(2,1)}, u32[]{:S(2)}, u32[]{:S(2)}) collective-permute-start(bf16[256,1024]{1,0:T(8,128)(2,1)S(1)} %copy-done.10), channel_id=1, source_target_pairs={{0,2},{1,3},{2,0},{3,1},{4,6},{5,7},{6,4},{7,5},{8,10},{9,11},{10,... | collective-permute-start | bytes 1572872 | tf_op jit(solution)/shard_map/ppermute | solution.py:293
  152.1 23.0 %collective-permute-start.23 = (bf16[256,1024]{1,0:T(8,128)(2,1)S(1)}, bf16[256,1024]{1,0:T(8,128)(2,1)}, u32[]{:S(2)}, u32[]{:S(2)}) collective-permute-start(bf16[256,1024]{1,0:T(8,128)(2,1)S(1)} %copy-done.10), channel_id=1, source_target_pairs={{0,3},{1,0},{2,1},{3,2},{4,7},{5,4},{6,5},{7,6},{8,11},{9,8},{10,9... | collective-permute-start | bytes 1572872 | tf_op jit(solution)/shard_map/ppermute | solution.py:293
  156.3 2.5 collective-permute-start.6
  167.1 28.1 %collective-permute-start.9 = (bf16[2,2,2,2,4,64,128]{6,5,4,3,2,1,0:T(8,128)(2,1)}, bf16[2,2,2,2,4,64,128]{6,5,4,3,2,1,0:T(8,128)(2,1)}, u32[]{:S(2)}, u32[]{:S(2)}) collective-permute-start(bf16[2,2,2,2,4,64,128]{6,5,4,3,2,1,0:T(8,128)(2,1)} %fusion.18), channel_id=1, source_target_pairs={{0,8},{4,12},{8,0},{12,4},{16,24},{20,28},{24,16},{28,20},{32,40},... | collective-permute-start | bytes 3145736 | tf_op jit(solution)/shard_map/ppermute | solution.py:270
  169.1 24.1 %collective-permute-start.8 = (f32[2,2,2,2,8,128]{5,4,3,2,1,0:T(8,128)}, f32[2,2,2,2,8,128]{5,4,3,2,1,0:T(8,128)S(1)}, u32[]{:S(2)}, u32[]{:S(2)}) collective-permute-start(f32[2,2,2,2,8,128]{5,4,3,2,1,0:T(8,128)} %get-tuple-element.80), channel_id=1, source_target_pairs={{0,8},{4,12},{8,0},{12,4},{16,24},{20,28},{24,16},{28,20},{32,40},... | collective-permute-start | bytes 196616 | tf_op jit(solution)/shard_map/ppermute | solution.py:271
  194.8 4.4 %collective-permute-start.10 = (f32[2,2,2,8,128]{4,3,2,1,0:T(8,128)S(1)}, f32[2,2,2,8,128]{4,3,2,1,0:T(8,128)S(1)}, u32[]{:S(2)}, u32[]{:S(2)}) collective-permute-start(f32[2,2,2,8,128]{4,3,2,1,0:T(8,128)S(1)} %get-tuple-element.84), channel_id=1, source_target_pairs={{0,32},{4,36},{8,40},{12,44},{16,48},{20,52},{24,56},{28,60},{32,0... | collective-permute-start | bytes 98312 | tf_op jit(solution)/shard_map/ppermute | solution.py:271
  197.7 12.2 %collective-permute-start.11 = (bf16[2,2,2,4,64,128]{5,4,3,2,1,0:T(8,128)(2,1)S(1)}, bf16[2,2,2,4,64,128]{5,4,3,2,1,0:T(8,128)(2,1)S(1)}, u32[]{:S(2)}, u32[]{:S(2)}) collective-permute-start(bf16[2,2,2,4,64,128]{5,4,3,2,1,0:T(8,128)(2,1)S(1)} %fusion.38), channel_id=1, source_target_pairs={{0,32},{4,36},{8,40},{12,44},{16,48},{20,52},{24,56},{28,60},{32,0... | collective-permute-start | bytes 1572872 | tf_op jit(solution)/shard_map/ppermute | solution.py:270
  199.3 13.7 %collective-permute-start.12 = (f32[2,2,8,128]{3,2,1,0:T(8,128)S(1)}, f32[2,2,8,128]{3,2,1,0:T(8,128)S(1)}, u32[]{:S(2)}, u32[]{:S(2)}) collective-permute-start(f32[2,2,8,128]{3,2,1,0:T(8,128)S(1)} %get-tuple-element.86), channel_id=1, source_target_pairs={{0,16},{4,20},{8,24},{12,28},{16,0},{20,4},{24,8},{28,12},{32,48},... | collective-permute-start | bytes 49160 | tf_op jit(solution)/shard_map/ppermute | solution.py:271
  210.2 7.2 %collective-permute-start.13 = (bf16[2,2,4,64,128]{4,3,2,1,0:T(8,128)(2,1)S(1)}, bf16[2,2,4,64,128]{4,3,2,1,0:T(8,128)(2,1)S(1)}, u32[]{:S(2)}, u32[]{:S(2)}) collective-permute-start(bf16[2,2,4,64,128]{4,3,2,1,0:T(8,128)(2,1)S(1)} %fusion.45), channel_id=1, source_target_pairs={{0,16},{4,20},{8,24},{12,28},{16,0},{20,4},{24,8},{28,12},{32,48},... | collective-permute-start | bytes 786440 | tf_op jit(solution)/shard_map/ppermute | solution.py:270
  213.1 6.3 %collective-permute-start.14 = (f32[2,8,128]{2,1,0:T(8,128)S(1)}, f32[2,8,128]{2,1,0:T(8,128)S(1)}, u32[]{:S(2)}, u32[]{:S(2)}) collective-permute-start(f32[2,8,128]{2,1,0:T(8,128)S(1)} %get-tuple-element.88), channel_id=1, source_target_pairs={{0,64},{4,68},{8,72},{12,76},{16,80},{20,84},{24,88},{28,92},{32,9... | collective-permute-start | bytes 24584 | tf_op jit(solution)/shard_map/ppermute | solution.py:271
  217.5 6.3 %collective-permute-start.15 = (bf16[2,4,64,128]{3,2,1,0:T(8,128)(2,1)S(1)}, bf16[2,4,64,128]{3,2,1,0:T(8,128)(2,1)S(1)}, u32[]{:S(2)}, u32[]{:S(2)}) collective-permute-start(bf16[2,4,64,128]{3,2,1,0:T(8,128)(2,1)S(1)} %fusion.54), channel_id=1, source_target_pairs={{0,64},{4,68},{8,72},{12,76},{16,80},{20,84},{24,88},{28,92},{32,9... | collective-permute-start | bytes 393224 | tf_op jit(solution)/shard_map/ppermute | solution.py:270
  219.4 6.5 %collective-permute-start.16 = (f32[8,128]{1,0:T(8,128)S(1)}, f32[8,128]{1,0:T(8,128)S(1)}, u32[]{:S(2)}, u32[]{:S(2)}) collective-permute-start(f32[8,128]{1,0:T(8,128)S(1)} %get-tuple-element.90), channel_id=1, source_target_pairs={{0,128},{4,132},{8,136},{12,140},{16,144},{20,148},{24,152},{28,15... | collective-permute-start | bytes 12296 | tf_op jit(solution)/shard_map/ppermute | solution.py:271
  223.8 7.8 %collective-permute-start.17 = (bf16[4,64,128]{2,1,0:T(8,128)(2,1)S(1)}, bf16[4,64,128]{2,1,0:T(8,128)(2,1)S(1)}, u32[]{:S(2)}, u32[]{:S(2)}) collective-permute-start(bf16[4,64,128]{2,1,0:T(8,128)(2,1)S(1)} %fusion.58), channel_id=1, source_target_pairs={{0,128},{4,132},{8,136},{12,140},{16,144},{20,148},{24,152},{28,15... | collective-permute-start | bytes 196616 | tf_op jit(solution)/shard_map/ppermute | solution.py:270
  231.6 4.7 %collective-permute-start.18 = (bf16[128,256]{0,1:T(8,128)(2,1)S(1)}, bf16[128,256]{0,1:T(8,128)(2,1)S(1)}, u32[]{:S(2)}, u32[]{:S(2)}) collective-permute-start(bf16[128,256]{0,1:T(8,128)(2,1)S(1)} %bitcast.212), channel_id=1, source_target_pairs={{0,1},{1,2},{2,3},{3,0},{4,5},{5,6},{6,7},{7,4},{8,9},{9,10},{10,1... | collective-permute-start | bytes 196616 | tf_op jit(solution)/shard_map/ppermute | solution.py:293
  232.1 4.6 %collective-permute-start.19 = (bf16[128,256]{0,1:T(8,128)(2,1)S(1)}, bf16[128,256]{0,1:T(8,128)(2,1)S(1)}, u32[]{:S(2)}, u32[]{:S(2)}) collective-permute-start(bf16[128,256]{0,1:T(8,128)(2,1)S(1)} %bitcast.213), channel_id=1, source_target_pairs={{0,2},{1,3},{2,0},{3,1},{4,6},{5,7},{6,4},{7,5},{8,10},{9,11},{10,... | collective-permute-start | bytes 196616 | tf_op jit(solution)/shard_map/ppermute | solution.py:293
  232.6 4.7 %collective-permute-start.20 = (bf16[128,256]{0,1:T(8,128)(2,1)S(1)}, bf16[128,256]{0,1:T(8,128)(2,1)S(1)}, u32[]{:S(2)}, u32[]{:S(2)}) collective-permute-start(bf16[128,256]{0,1:T(8,128)(2,1)S(1)} %bitcast.214), channel_id=1, source_target_pairs={{0,3},{1,0},{2,1},{3,2},{4,7},{5,4},{6,5},{7,6},{8,11},{9,8},{10,9... | collective-permute-start | bytes 196616 | tf_op jit(solution)/shard_map/ppermute | solution.py:293
  271.7 10.2 %collective-permute-start.24 = (bf16[640,256]{1,0:T(8,128)(2,1)S(1)}, bf16[640,256]{1,0:T(8,128)(2,1)S(1)}, u32[]{:S(2)}, u32[]{:S(2)}) collective-permute-start(bf16[640,256]{1,0:T(8,128)(2,1)S(1)} %reshape_squeeze.3), channel_id=1, source_target_pairs={{0,1},{1,2},{2,3},{3,0},{4,5},{5,6},{6,7},{7,4},{8,9},{9,10},{10,1... | collective-permute-start | bytes 983048 | tf_op jit(solution)/shard_map/ppermute | solution.py:293
  272.8 16.9 %collective-permute-start.25 = (bf16[640,256]{1,0:T(8,128)(2,1)S(1)}, bf16[640,256]{1,0:T(8,128)(2,1)S(1)}, u32[]{:S(2)}, u32[]{:S(2)}) collective-permute-start(bf16[640,256]{1,0:T(8,128)(2,1)S(1)} %reshape_squeeze.3), channel_id=1, source_target_pairs={{0,2},{1,3},{2,0},{3,1},{4,6},{5,7},{6,4},{7,5},{8,10},{9,11},{10,... | collective-permute-start | bytes 983048 | tf_op jit(solution)/shard_map/ppermute | solution.py:293
  275.3 14.4 %collective-permute-start.26 = (bf16[640,256]{1,0:T(8,128)(2,1)S(1)}, bf16[640,256]{1,0:T(8,128)(2,1)S(1)}, u32[]{:S(2)}, u32[]{:S(2)}) collective-permute-start(bf16[640,256]{1,0:T(8,128)(2,1)S(1)} %reshape_squeeze.3), channel_id=1, source_target_pairs={{0,3},{1,0},{2,1},{3,2},{4,7},{5,4},{6,5},{7,6},{8,11},{9,8},{10,9... | collective-permute-start | bytes 983048 | tf_op jit(solution)/shard_map/ppermute | solution.py:293
  297.7 9.9 %collective-permute-start.27 = (bf16[640,256]{1,0:T(8,128)(2,1)}, bf16[640,256]{1,0:T(8,128)(2,1)S(1)}, u32[]{:S(2)}, u32[]{:S(2)}) collective-permute-start(bf16[640,256]{1,0:T(8,128)(2,1)} %get-tuple-element.60), channel_id=1, source_target_pairs={{0,1},{1,2},{2,3},{3,0},{4,5},{5,6},{6,7},{7,4},{8,9},{9,10},{10,1... | collective-permute-start | bytes 983048 | tf_op jit(solution)/shard_map/ppermute | solution.py:341
  299.0 17.4 %collective-permute-start.28 = (bf16[640,256]{1,0:T(8,128)(2,1)S(1)}, bf16[640,256]{1,0:T(8,128)(2,1)}, u32[]{:S(2)}, u32[]{:S(2)}) collective-permute-start(bf16[640,256]{1,0:T(8,128)(2,1)S(1)} %get-tuple-element.62), channel_id=1, source_target_pairs={{0,2},{1,3},{2,0},{3,1},{4,6},{5,7},{6,4},{7,5},{8,10},{9,11},{10,... | collective-permute-start | bytes 983048 | tf_op jit(solution)/shard_map/ppermute | solution.py:341
  301.8 14.6 %collective-permute-start.29 = (bf16[640,256]{1,0:T(8,128)(2,1)S(1)}, bf16[640,256]{1,0:T(8,128)(2,1)}, u32[]{:S(2)}, u32[]{:S(2)}) collective-permute-start(bf16[640,256]{1,0:T(8,128)(2,1)S(1)} %get-tuple-element.61), channel_id=1, source_target_pairs={{0,3},{1,0},{2,1},{3,2},{4,7},{5,4},{6,5},{7,6},{8,11},{9,8},{10,9... | collective-permute-start | bytes 983048 | tf_op jit(solution)/shard_map/ppermute | solution.py:341
  318.6 24.0 %all-to-all-start.1 = ((bf16[64,1,10,256]{3,2,1,0:T(8,128)(2,1)}), bf16[64,1,10,256]{3,2,1,0:T(8,128)(2,1)S(1)}, u32[]{:S(2)}, u32[]{:S(2)}) async-start(bf16[64,1,10,256]{3,2,1,0:T(8,128)(2,1)} %bitcast.79), calls=%async_computation.1 | async-start | bytes 1048576 | tf_op jit(solution)/shard_map/all_to_all | solution.py:345
  (15 other events, 146.1 us)

commit v5 on v4

--- a/solution.py
+++ b/solution.py
@@ -218,7 +218,7 @@
             [jnp.where(low_side, gathered, got), jnp.where(low_side, got, gathered)], axis=position
         )
         held_bits.insert(position, bit)
-        if len(held_bits) == 1:
+        if len(held_bits) == gather_count - 1:
             gathered, block_tables, fresh_kv = lax.optimization_barrier(
                 (gathered, block_tables, fresh_kv)
             )

time: 346 us -> 332 us (0.960)
  waiting for transfers between devices: 133 us -> 117 us
  starting transfers between devices: 56.2 us -> 64.1 us
  other arithmetic: 31.8 us -> 28 us
  local copies, waits for them, and re-layouts: 29.6 us -> 26.1 us
    ppermute x6, waiting for transfers between devices: 49.8 us -> 37.6 us  [shards(): got = lax.ppermute(gathered, 'seq', pairs)]
    ppermute x6, waiting for transfers between devices: 14.5 us -> 9.84 us  [shards(): got_stats = lax.ppermute(send_stats, 'seq', pairs)]
    ppermute x6, starting transfers between devices: 8.49 us -> 12.8 us  [shards(): got_stats = lax.ppermute(send_stats, 'seq', pairs)]
    ppermute x9, waiting for transfers between devices: 21.8 us -> 25.9 us  [tp_gather(): lax.ppermute(value, 'tp', [(i, (i + k) % tp_count) for i in range(tp_coun...]
    unnamed x34 -> x32, local copies, waits for them, and re-layouts: 9.99 us -> 7.81 us
  transfers between devices with their start and end apart: 31 -> 31, of which waited for: 21 -> 20; matrix products, arithmetic and copies ran while one was open for 11% -> 10% of each run, Pallas kernels for 0% -> 0%
where the time goes in v5:
time: 332 us
  waiting for transfers between devices  117 us (35%)
  starting transfers between devices  64.1 us (19%)
  Pallas kernels  49.2 us (15%)
  blocking collectives  32.2 us (10%)
  other arithmetic  28 us (8%)
  local copies, waits for them, and re-layouts  26.1 us (8%)
  matrix products  14.2 us (4%)
    pallas_call x1, Pallas kernels, local_attention(): pl.pallas_call(attend_kernel, grid_spec=grid_spec, out_shape=[jax.ShapeDt...  49.2 us
    ppermute x6, waiting for transfers between devices, shards(): got = lax.ppermute(gathered, 'seq', pairs)  37.6 us
    all_to_all x1, blocking collectives, shards(): lax.all_to_all(outgoing, 'seq', split_axis=0, concat_axis=0, tiled=True)  32.2 us
    ppermute x9, waiting for transfers between devices, tp_gather(): lax.ppermute(value, 'tp', [(i, (i + k) % tp_count) for i in range(tp_coun...  25.9 us
    ppermute x6, starting transfers between devices, shards(): got = lax.ppermute(gathered, 'seq', pairs)  19.4 us
    ppermute x6, waiting for transfers between devices, shards(): lax.ppermute(send_acc.astype(jnp.bfloat16), 'seq', pairs)  15.3 us
    ppermute x3, waiting for transfers between devices, shards(): lax.ppermute(target_cols, 'tp', [(i, (i + k) % tp_count) for i in range(t...  14.4 us
    all_to_all x1, waiting for transfers between devices, shards(): lax.all_to_all(produced.astype(jnp.bfloat16), 'seq', split_axis=0, concat...  14.1 us
  transfers between devices with their start and end apart: 31, of which 20 were waited for; matrix products, arithmetic and copies ran while one was open for 10% of the time, Pallas kernels for 0%

profile of v5, /device:TPU:1, one launch (start us, length us, event | category | flops | bytes accessed | tf_op | source)
XLA Modules:
  0.0 331.6 jit_solution(10741186476095779880)
XLA Ops:
  2.6 7.8 %collective-permute-start = (bf16[128,256]{1,0:T(8,128)(2,1)S(1)}, bf16[128,256]{1,0:T(8,128)(2,1)S(1)}, u32[]{:S(2)}, u32[]{:S(2)}) collective-permute-start(bf16[128,256]{1,0:T(8,128)(2,1)S(1)} %convolution_convert_fusion.4), channel_id=1, source_target_pairs={{0,128},{4,132},{8,136},{12,140},{16,144},{20,148},{24,152},{28,15... | collective-permute-start | bytes 196616 | tf_op jit(solution)/shard_map/ppermute | solution.py:214
  13.7 5.4 %collective-permute-done.1 = bf16[2,128,256]{2,1,0:T(8,128)(2,1)S(1)} collective-permute-done((bf16[2,128,256]{2,1,0:T(8,128)(2,1)S(1)}, bf16[2,128,256]{2,1,0:T(8,128)(2,1)S(1)}, u32[]{:S(2)}, u32[]{:S(2)}) %collective-permute-start.1) | collective-permute-done | bytes 131104 | tf_op jit(solution)/shard_map/ppermute | solution.py:214
  19.1 4.6 %collective-permute-start.2 = (bf16[2,2,128,256]{3,2,0,1:T(8,128)(2,1)S(1)}, bf16[2,2,128,256]{3,2,0,1:T(8,128)(2,1)S(1)}, u32[]{:S(2)}, u32[]{:S(2)}) collective-permute-start(bf16[2,2,128,256]{3,2,0,1:T(8,128)(2,1)S(1)} %pad_maximum_fusion.7), channel_id=1, source_target_pairs={{0,16},{4,20},{8,24},{12,28},{16,0},{20,4},{24,8},{28,12},{32,48},... | collective-permute-start | bytes 786440 | tf_op jit(solution)/shard_map/ppermute | solution.py:214
  23.7 5.1 %collective-permute-done.2 = bf16[2,2,128,256]{3,2,0,1:T(8,128)(2,1)S(1)} collective-permute-done((bf16[2,2,128,256]{3,2,0,1:T(8,128)(2,1)S(1)}, bf16[2,2,128,256]{3,2,0,1:T(8,128)(2,1)S(1)}, u32[]{:S(2)}, u32[]{:S(2)}) %collective-permute-start.2) | collective-permute-done | bytes 262176 | tf_op jit(solution)/shard_map/ppermute | solution.py:214
  30.1 10.2 %collective-permute-done.3 = bf16[2,2,2,128,256]{4,3,0,1,2:T(8,128)(2,1)S(1)} collective-permute-done((bf16[2,2,2,128,256]{4,3,0,1,2:T(8,128)(2,1)S(1)}, bf16[2,2,2,128,256]{4,3,0,1,2:T(8,128)(2,1)S(1)}, u32[]{:S(2)}, u32[]{:S(2)}) %collective-permute-start.3) | collective-permute-done | bytes 524320 | tf_op jit(solution)/shard_map/ppermute | solution.py:214
  53.0 11.4 %collective-permute-done.4 = bf16[2,2,2,2,128,256]{5,4,0,1,3,2:T(8,128)(2,1)} collective-permute-done((bf16[2,2,2,2,128,256]{5,4,0,1,3,2:T(8,128)(2,1)}, bf16[2,2,2,2,128,256]{5,4,0,1,3,2:T(8,128)(2,1)}, u32[]{:S(2)}, u32[]{:S(2)}) %collective-permute-start.4) | collective-permute-done | bytes 1048608 | tf_op jit(solution)/shard_map/ppermute | solution.py:214
  65.9 3.6 %collective-permute-start.5 = (bf16[2,2,2,2,2,128,256]{6,5,0,1,3,2,4:T(8,128)(2,1)S(1)}, bf16[2,2,2,2,2,128,256]{6,5,0,1,3,2,4:T(8,128)(2,1)}, u32[]{:S(2)}, u32[]{:S(2)}) collective-permute-start(bf16[2,2,2,2,2,128,256]{6,5,0,1,3,2,4:T(8,128)(2,1)S(1)} %pad_maximum_fusion.1), channel_id=1, source_target_pairs={{0,4},{4,0},{8,12},{12,8},{16,20},{20,16},{24,28},{28,24},{32,36},... | collective-permute-start | bytes 6291464 | tf_op jit(solution)/shard_map/ppermute | solution.py:214
  69.6 3.8 %collective-permute-done.5 = bf16[2,2,2,2,2,128,256]{6,5,0,1,3,2,4:T(8,128)(2,1)} collective-permute-done((bf16[2,2,2,2,2,128,256]{6,5,0,1,3,2,4:T(8,128)(2,1)S(1)}, bf16[2,2,2,2,2,128,256]{6,5,0,1,3,2,4:T(8,128)(2,1)}, u32[]{:S(2)}, u32[]{:S(2)}) %collective-permute-start.5) | collective-permute-done | bytes 2097184 | tf_op jit(solution)/shard_map/ppermute | solution.py:214
  77.9 49.2 %shard_map.136 = (f32[4,16,4,64,128]{4,3,2,1,0:T(8,128)}, f32[4,16,8,128]{3,2,1,0:T(8,128)}) custom-call(s32[34]{0:T(128)} %copy-done.13, s32[34]{0:T(128)} %get-tuple-element.18.page_ref, s32[34]{0:T(128)} %gather_fusion.2, s32[34]{0:T(128)} %gather_fusion.3, s32[34]{0:T(128)} %compare_convert_fusion.fresh_ref, bf16[16,512,256]{2,1,0:T(8,128)(2,1)} %bitcast.204, ...), custom_call_target="tpu_custom_call" | custom-call | tf_op jit(solution)/shard_map/pallas_call | solution.py:130
  127.1 4.4 %broadcast_select_fusion = f32[4,16,4,64,128]{4,3,2,1,0:T(8,128)S(1)} fusion(f32[4,16,4,64,128]{4,3,2,1,0:T(8,128)} %get-tuple-element.25, pred[16]{0:T(512)(128)(4,1)S(1)} %fusion.84), kind=kLoop, calls=%fused_computation.12 | loop fusion | flops 2097152 | bytes 16777232 | tf_op jit(solution)/shard_map/jit(_where)/select_n | solution.py:247
  131.5 3.3 copy-done.2
  137.4 2.6 collective-permute-start.22
  144.7 4.0 %fusion = f32[2,2,2,2,2,4,64,128]{7,6,5,4,3,2,1,0:T(8,128)S(1)} fusion(bf16[2,2,2,2,2,4,64,128]{7,6,5,4,3,2,1,0:T(8,128)(2,1)} %collective-permute-done.7, f32[2,2,2,2,2,2,4,64,128]{8,7,6,5,4,3,2,1,0:T(8,128)} %bitcast.203, s32[]{:T(128)S(6)} %select_n.333, f32[2,2,2,2,2,4,128]{6,5,4,3,2,1,0:T(4,128)S(1)} %get-tuple-element.50, ...), kind=kLoop, calls=%fused_computation.10 | loop fusion | flops 4194304 | bytes 10616836 | tf_op jit(solution)/shard_map/add | solution.py:282
  153.5 9.9 %collective-permute-done.22 = bf16[256,1024]{1,0:T(8,128)(2,1)} collective-permute-done((bf16[256,1024]{1,0:T(8,128)(2,1)}, bf16[256,1024]{1,0:T(8,128)(2,1)}, u32[]{:S(2)}, u32[]{:S(2)}) %collective-permute-start.22) | collective-permute-done | bytes 524320 | tf_op jit(solution)/shard_map/ppermute | solution.py:293
  163.4 3.1 pad_maximum_fusion.2
  168.9 9.1 %collective-permute-done.8 = f32[2,2,2,2,8,128]{5,4,3,2,1,0:T(8,128)S(1)} collective-permute-done((f32[2,2,2,2,8,128]{5,4,3,2,1,0:T(8,128)S(1)}, f32[2,2,2,2,8,128]{5,4,3,2,1,0:T(8,128)S(1)}, u32[]{:S(2)}, u32[]{:S(2)}) %collective-permute-start.8) | collective-permute-done | bytes 65568 | tf_op jit(solution)/shard_map/ppermute | solution.py:271
  182.6 2.8 collective-permute-start.12
  185.4 7.7 %collective-permute-done.11 = bf16[2,2,2,4,64,128]{5,4,3,2,1,0:T(8,128)(2,1)S(1)} collective-permute-done((bf16[2,2,2,4,64,128]{5,4,3,2,1,0:T(8,128)(2,1)S(1)}, bf16[2,2,2,4,64,128]{5,4,3,2,1,0:T(8,128)(2,1)S(1)}, u32[]{:S(2)}, u32[]{:S(2)}) %collective-permute-start.11) | collective-permute-done | bytes 524320 | tf_op jit(solution)/shard_map/ppermute | solution.py:270
  193.4 2.9 collective-permute-start.13
  196.4 4.2 %collective-permute-done.13 = bf16[2,2,4,64,128]{4,3,2,1,0:T(8,128)(2,1)S(1)} collective-permute-done((bf16[2,2,4,64,128]{4,3,2,1,0:T(8,128)(2,1)S(1)}, bf16[2,2,4,64,128]{4,3,2,1,0:T(8,128)(2,1)S(1)}, u32[]{:S(2)}, u32[]{:S(2)}) %collective-permute-start.13) | collective-permute-done | bytes 262176 | tf_op jit(solution)/shard_map/ppermute | solution.py:270
  200.9 8.2 %collective-permute-start.16 = (f32[8,128]{1,0:T(8,128)S(1)}, f32[8,128]{1,0:T(8,128)S(1)}, u32[]{:S(2)}, u32[]{:S(2)}) collective-permute-start(f32[8,128]{1,0:T(8,128)S(1)} %get-tuple-element.90), channel_id=1, source_target_pairs={{0,128},{4,132},{8,136},{12,140},{16,144},{20,148},{24,152},{28,15... | collective-permute-start | bytes 12296 | tf_op jit(solution)/shard_map/ppermute | solution.py:271
  209.2 3.7 %collective-permute-start.17 = (bf16[4,64,128]{2,1,0:T(8,128)(2,1)S(1)}, bf16[4,64,128]{2,1,0:T(8,128)(2,1)S(1)}, u32[]{:S(2)}, u32[]{:S(2)}) collective-permute-start(bf16[4,64,128]{2,1,0:T(8,128)(2,1)S(1)} %fusion.58), channel_id=1, source_target_pairs={{0,128},{4,132},{8,136},{12,140},{16,144},{20,148},{24,152},{28,15... | collective-permute-start | bytes 196616 | tf_op jit(solution)/shard_map/ppermute | solution.py:270
  212.9 3.4 %collective-permute-done.17 = bf16[4,64,128]{2,1,0:T(8,128)(2,1)S(1)} collective-permute-done((bf16[4,64,128]{2,1,0:T(8,128)(2,1)S(1)}, bf16[4,64,128]{2,1,0:T(8,128)(2,1)S(1)}, u32[]{:S(2)}, u32[]{:S(2)}) %collective-permute-start.17) | collective-permute-done | bytes 65568 | tf_op jit(solution)/shard_map/ppermute | solution.py:270
  226.2 32.2 %all_to_all.10 = bf16[64,1,10,256]{3,2,1,0:T(8,128)(2,1)S(1)} all-to-all(bf16[64,1,10,256]{3,2,1,0:T(8,128)(2,1)S(1)} %bitcast.206), channel_id=1, replica_groups=mesh['seq'=64,'tp'=4] {'seq'}, dimensions={0} | all-to-all | bytes 655360 | tf_op jit(solution)/shard_map/all_to_all | solution.py:327
  262.3 6.4 %collective-permute-done.24 = bf16[640,256]{1,0:T(8,128)(2,1)S(1)} collective-permute-done((bf16[640,256]{1,0:T(8,128)(2,1)S(1)}, bf16[640,256]{1,0:T(8,128)(2,1)S(1)}, u32[]{:S(2)}, u32[]{:S(2)}) %collective-permute-start.24) | collective-permute-done | bytes 327712 | tf_op jit(solution)/shard_map/ppermute | solution.py:293
  268.7 7.8 %collective-permute-done.25 = bf16[640,256]{1,0:T(8,128)(2,1)S(1)} collective-permute-done((bf16[640,256]{1,0:T(8,128)(2,1)S(1)}, bf16[640,256]{1,0:T(8,128)(2,1)S(1)}, u32[]{:S(2)}, u32[]{:S(2)}) %collective-permute-start.25) | collective-permute-done | bytes 327712 | tf_op jit(solution)/shard_map/ppermute | solution.py:293
  280.4 3.2 convolution_convert_fusion
  285.9 2.7 collective-permute-start.28
  288.9 5.6 %collective-permute-done.27 = bf16[640,256]{1,0:T(8,128)(2,1)S(1)} collective-permute-done((bf16[640,256]{1,0:T(8,128)(2,1)}, bf16[640,256]{1,0:T(8,128)(2,1)S(1)}, u32[]{:S(2)}, u32[]{:S(2)}) %collective-permute-start.27) | collective-permute-done | bytes 327712 | tf_op jit(solution)/shard_map/ppermute | solution.py:341
  294.4 8.8 %collective-permute-done.28 = bf16[640,256]{1,0:T(8,128)(2,1)} collective-permute-done((bf16[640,256]{1,0:T(8,128)(2,1)S(1)}, bf16[640,256]{1,0:T(8,128)(2,1)}, u32[]{:S(2)}, u32[]{:S(2)}) %collective-permute-start.28) | collective-permute-done | bytes 327712 | tf_op jit(solution)/shard_map/ppermute | solution.py:341
  305.5 6.3 %all-to-all-start.1 = ((bf16[64,1,10,256]{3,2,1,0:T(8,128)(2,1)}), bf16[64,1,10,256]{3,2,1,0:T(8,128)(2,1)S(1)}, u32[]{:S(2)}, u32[]{:S(2)}) async-start(bf16[64,1,10,256]{3,2,1,0:T(8,128)(2,1)} %bitcast.79), calls=%async_computation.1 | async-start | bytes 1048576 | tf_op jit(solution)/shard_map/all_to_all | solution.py:345
  315.3 14.1 %all-to-all-done.1 = bf16[64,1,10,256]{3,2,1,0:T(8,128)(2,1)S(1)} async-done(((bf16[64,1,10,256]{3,2,1,0:T(8,128)(2,1)}), bf16[64,1,10,256]{3,2,1,0:T(8,128)(2,1)S(1)}, u32[]{:S(2)}, u32[]{:S(2)}) %all-to-all-start.1) | async-done | bytes 327712 | tf_op jit(solution)/shard_map/all_to_all | solution.py:345
  (180 shorter events, 73.4 us)
Async XLA Ops:
  0.0 280.4 %copy-start = (bf16[1,352,1024]{2,1,0:T(8,128)(2,1)S(1)}, bf16[1,352,1024]{2,1,0:T(8,128)(2,1)}, u32[]{:S(2)}) copy-start(bf16[1,352,1024]{2,1,0:T(8,128)(2,1)} %param.27) | copy-start | bytes 2162692
  2.6 9.6 %collective-permute-start = (bf16[128,256]{1,0:T(8,128)(2,1)S(1)}, bf16[128,256]{1,0:T(8,128)(2,1)S(1)}, u32[]{:S(2)}, u32[]{:S(2)}) collective-permute-start(bf16[128,256]{1,0:T(8,128)(2,1)S(1)} %convolution_convert_fusion.4), channel_id=1, source_target_pairs={{0,128},{4,132},{8,136},{12,140},{16,144},{20,148},{24,152},{28,15... | collective-permute-start | bytes 196616 | tf_op jit(solution)/shard_map/ppermute | solution.py:214
  12.2 6.9 %collective-permute-start.1 = (bf16[2,128,256]{2,1,0:T(8,128)(2,1)S(1)}, bf16[2,128,256]{2,1,0:T(8,128)(2,1)S(1)}, u32[]{:S(2)}, u32[]{:S(2)}) collective-permute-start(bf16[2,128,256]{2,1,0:T(8,128)(2,1)S(1)} %pad_maximum_fusion.12), channel_id=1, source_target_pairs={{0,64},{4,68},{8,72},{12,76},{16,80},{20,84},{24,88},{28,92},{32,9... | collective-permute-start | bytes 393224 | tf_op jit(solution)/shard_map/ppermute | solution.py:214
  19.1 9.7 %collective-permute-start.2 = (bf16[2,2,128,256]{3,2,0,1:T(8,128)(2,1)S(1)}, bf16[2,2,128,256]{3,2,0,1:T(8,128)(2,1)S(1)}, u32[]{:S(2)}, u32[]{:S(2)}) collective-permute-start(bf16[2,2,128,256]{3,2,0,1:T(8,128)(2,1)S(1)} %pad_maximum_fusion.7), channel_id=1, source_target_pairs={{0,16},{4,20},{8,24},{12,28},{16,0},{20,4},{24,8},{28,12},{32,48},... | collective-permute-start | bytes 786440 | tf_op jit(solution)/shard_map/ppermute | solution.py:214
  28.9 11.4 %collective-permute-start.3 = (bf16[2,2,2,128,256]{4,3,0,1,2:T(8,128)(2,1)S(1)}, bf16[2,2,2,128,256]{4,3,0,1,2:T(8,128)(2,1)S(1)}, u32[]{:S(2)}, u32[]{:S(2)}) collective-permute-start(bf16[2,2,2,128,256]{4,3,0,1,2:T(8,128)(2,1)S(1)} %pad_maximum_fusion.6), channel_id=1, source_target_pairs={{0,32},{4,36},{8,40},{12,44},{16,48},{20,52},{24,56},{28,60},{32,0... | collective-permute-start | bytes 1572872 | tf_op jit(solution)/shard_map/ppermute | solution.py:214
  41.5 22.8 %collective-permute-start.4 = (bf16[2,2,2,2,128,256]{5,4,0,1,3,2:T(8,128)(2,1)}, bf16[2,2,2,2,128,256]{5,4,0,1,3,2:T(8,128)(2,1)}, u32[]{:S(2)}, u32[]{:S(2)}) collective-permute-start(bf16[2,2,2,2,128,256]{5,4,0,1,3,2:T(8,128)(2,1)} %pad_maximum_fusion.5), channel_id=1, source_target_pairs={{0,8},{4,12},{8,0},{12,4},{16,24},{20,28},{24,16},{28,20},{32,40},... | collective-permute-start | bytes 3145736 | tf_op jit(solution)/shard_map/ppermute | solution.py:214
  65.9 7.5 %collective-permute-start.5 = (bf16[2,2,2,2,2,128,256]{6,5,0,1,3,2,4:T(8,128)(2,1)S(1)}, bf16[2,2,2,2,2,128,256]{6,5,0,1,3,2,4:T(8,128)(2,1)}, u32[]{:S(2)}, u32[]{:S(2)}) collective-permute-start(bf16[2,2,2,2,2,128,256]{6,5,0,1,3,2,4:T(8,128)(2,1)S(1)} %pad_maximum_fusion.1), channel_id=1, source_target_pairs={{0,4},{4,0},{8,12},{12,8},{16,20},{20,16},{24,28},{28,24},{32,36},... | collective-permute-start | bytes 6291464 | tf_op jit(solution)/shard_map/ppermute | solution.py:214
  135.3 9.3 %collective-permute-start.7 = (bf16[2,2,2,2,2,4,64,128]{7,6,5,4,3,2,1,0:T(8,128)(2,1)S(1)}, bf16[2,2,2,2,2,4,64,128]{7,6,5,4,3,2,1,0:T(8,128)(2,1)}, u32[]{:S(2)}, u32[]{:S(2)}) collective-permute-start(bf16[2,2,2,2,2,4,64,128]{7,6,5,4,3,2,1,0:T(8,128)(2,1)S(1)} %fusion.1), channel_id=1, source_target_pairs={{0,4},{4,0},{8,12},{12,8},{16,20},{20,16},{24,28},{28,24},{32,36},... | collective-permute-start | bytes 6291464 | tf_op jit(solution)/shard_map/ppermute | solution.py:270
  135.8 17.7 %collective-permute-start.21 = (bf16[256,1024]{1,0:T(8,128)(2,1)}, bf16[256,1024]{1,0:T(8,128)(2,1)}, u32[]{:S(2)}, u32[]{:S(2)}) collective-permute-start(bf16[256,1024]{1,0:T(8,128)(2,1)} %param.21), channel_id=1, source_target_pairs={{0,1},{1,2},{2,3},{3,0},{4,5},{5,6},{6,7},{7,4},{8,9},{9,10},{10,1... | collective-permute-start | bytes 1572872 | tf_op jit(solution)/shard_map/ppermute | solution.py:293
  137.4 26.1 %collective-permute-start.22 = (bf16[256,1024]{1,0:T(8,128)(2,1)}, bf16[256,1024]{1,0:T(8,128)(2,1)}, u32[]{:S(2)}, u32[]{:S(2)}) collective-permute-start(bf16[256,1024]{1,0:T(8,128)(2,1)} %param.21), channel_id=1, source_target_pairs={{0,2},{1,3},{2,0},{3,1},{4,6},{5,7},{6,4},{7,5},{8,10},{9,11},{10,... | collective-permute-start | bytes 1572872 | tf_op jit(solution)/shard_map/ppermute | solution.py:293
  140.0 23.5 %collective-permute-start.23 = (bf16[256,1024]{1,0:T(8,128)(2,1)}, bf16[256,1024]{1,0:T(8,128)(2,1)}, u32[]{:S(2)}, u32[]{:S(2)}) collective-permute-start(bf16[256,1024]{1,0:T(8,128)(2,1)} %param.21), channel_id=1, source_target_pairs={{0,3},{1,0},{2,1},{3,2},{4,7},{5,4},{6,5},{7,6},{8,11},{9,8},{10,9... | collective-permute-start | bytes 1572872 | tf_op jit(solution)/shard_map/ppermute | solution.py:293
  142.6 2.0 collective-permute-start.6
  151.9 26.5 %collective-permute-start.9 = (bf16[2,2,2,2,4,64,128]{6,5,4,3,2,1,0:T(8,128)(2,1)}, bf16[2,2,2,2,4,64,128]{6,5,4,3,2,1,0:T(8,128)(2,1)}, u32[]{:S(2)}, u32[]{:S(2)}) collective-permute-start(bf16[2,2,2,2,4,64,128]{6,5,4,3,2,1,0:T(8,128)(2,1)} %fusion.18), channel_id=1, source_target_pairs={{0,8},{4,12},{8,0},{12,4},{16,24},{20,28},{24,16},{28,20},{32,40},... | collective-permute-start | bytes 3145736 | tf_op jit(solution)/shard_map/ppermute | solution.py:270
  153.2 24.8 %collective-permute-start.8 = (f32[2,2,2,2,8,128]{5,4,3,2,1,0:T(8,128)S(1)}, f32[2,2,2,2,8,128]{5,4,3,2,1,0:T(8,128)S(1)}, u32[]{:S(2)}, u32[]{:S(2)}) collective-permute-start(f32[2,2,2,2,8,128]{5,4,3,2,1,0:T(8,128)S(1)} %get-tuple-element.80), channel_id=1, source_target_pairs={{0,8},{4,12},{8,0},{12,4},{16,24},{20,28},{24,16},{28,20},{32,40},... | collective-permute-start | bytes 196616 | tf_op jit(solution)/shard_map/ppermute | solution.py:271
  178.0 4.5 %collective-permute-start.10 = (f32[2,2,2,8,128]{4,3,2,1,0:T(8,128)S(1)}, f32[2,2,2,8,128]{4,3,2,1,0:T(8,128)S(1)}, u32[]{:S(2)}, u32[]{:S(2)}) collective-permute-start(f32[2,2,2,8,128]{4,3,2,1,0:T(8,128)S(1)} %get-tuple-element.84), channel_id=1, source_target_pairs={{0,32},{4,36},{8,40},{12,44},{16,48},{20,52},{24,56},{28,60},{32,0... | collective-permute-start | bytes 98312 | tf_op jit(solution)/shard_map/ppermute | solution.py:271
  180.9 12.2 %collective-permute-start.11 = (bf16[2,2,2,4,64,128]{5,4,3,2,1,0:T(8,128)(2,1)S(1)}, bf16[2,2,2,4,64,128]{5,4,3,2,1,0:T(8,128)(2,1)S(1)}, u32[]{:S(2)}, u32[]{:S(2)}) collective-permute-start(bf16[2,2,2,4,64,128]{5,4,3,2,1,0:T(8,128)(2,1)S(1)} %fusion.38), channel_id=1, source_target_pairs={{0,32},{4,36},{8,40},{12,44},{16,48},{20,52},{24,56},{28,60},{32,0... | collective-permute-start | bytes 1572872 | tf_op jit(solution)/shard_map/ppermute | solution.py:270
  182.6 13.7 %collective-permute-start.12 = (f32[2,2,8,128]{3,2,1,0:T(8,128)S(1)}, f32[2,2,8,128]{3,2,1,0:T(8,128)S(1)}, u32[]{:S(2)}, u32[]{:S(2)}) collective-permute-start(f32[2,2,8,128]{3,2,1,0:T(8,128)S(1)} %get-tuple-element.86), channel_id=1, source_target_pairs={{0,16},{4,20},{8,24},{12,28},{16,0},{20,4},{24,8},{28,12},{32,48},... | collective-permute-start | bytes 49160 | tf_op jit(solution)/shard_map/ppermute | solution.py:271
  193.4 7.2 %collective-permute-start.13 = (bf16[2,2,4,64,128]{4,3,2,1,0:T(8,128)(2,1)S(1)}, bf16[2,2,4,64,128]{4,3,2,1,0:T(8,128)(2,1)S(1)}, u32[]{:S(2)}, u32[]{:S(2)}) collective-permute-start(bf16[2,2,4,64,128]{4,3,2,1,0:T(8,128)(2,1)S(1)} %fusion.45), channel_id=1, source_target_pairs={{0,16},{4,20},{8,24},{12,28},{16,0},{20,4},{24,8},{28,12},{32,48},... | collective-permute-start | bytes 786440 | tf_op jit(solution)/shard_map/ppermute | solution.py:270
  196.3 4.5 %collective-permute-start.14 = (f32[2,8,128]{2,1,0:T(8,128)S(1)}, f32[2,8,128]{2,1,0:T(8,128)S(1)}, u32[]{:S(2)}, u32[]{:S(2)}) collective-permute-start(f32[2,8,128]{2,1,0:T(8,128)S(1)} %get-tuple-element.88), channel_id=1, source_target_pairs={{0,64},{4,68},{8,72},{12,76},{16,80},{20,84},{24,88},{28,92},{32,9... | collective-permute-start | bytes 24584 | tf_op jit(solution)/shard_map/ppermute | solution.py:271
  200.8 8.3 %collective-permute-start.15 = (bf16[2,4,64,128]{3,2,1,0:T(8,128)(2,1)S(1)}, bf16[2,4,64,128]{3,2,1,0:T(8,128)(2,1)S(1)}, u32[]{:S(2)}, u32[]{:S(2)}) collective-permute-start(bf16[2,4,64,128]{3,2,1,0:T(8,128)(2,1)S(1)} %fusion.54), channel_id=1, source_target_pairs={{0,64},{4,68},{8,72},{12,76},{16,80},{20,84},{24,88},{28,92},{32,9... | collective-permute-start | bytes 393224 | tf_op jit(solution)/shard_map/ppermute | solution.py:270
  200.9 12.0 %collective-permute-start.16 = (f32[8,128]{1,0:T(8,128)S(1)}, f32[8,128]{1,0:T(8,128)S(1)}, u32[]{:S(2)}, u32[]{:S(2)}) collective-permute-start(f32[8,128]{1,0:T(8,128)S(1)} %get-tuple-element.90), channel_id=1, source_target_pairs={{0,128},{4,132},{8,136},{12,140},{16,144},{20,148},{24,152},{28,15... | collective-permute-start | bytes 12296 | tf_op jit(solution)/shard_map/ppermute | solution.py:271
  209.2 7.1 %collective-permute-start.17 = (bf16[4,64,128]{2,1,0:T(8,128)(2,1)S(1)}, bf16[4,64,128]{2,1,0:T(8,128)(2,1)S(1)}, u32[]{:S(2)}, u32[]{:S(2)}) collective-permute-start(bf16[4,64,128]{2,1,0:T(8,128)(2,1)S(1)} %fusion.58), channel_id=1, source_target_pairs={{0,128},{4,132},{8,136},{12,140},{16,144},{20,148},{24,152},{28,15... | collective-permute-start | bytes 196616 | tf_op jit(solution)/shard_map/ppermute | solution.py:270
  216.3 4.4 %collective-permute-start.18 = (bf16[128,256]{0,1:T(8,128)(2,1)S(1)}, bf16[128,256]{0,1:T(8,128)(2,1)S(1)}, u32[]{:S(2)}, u32[]{:S(2)}) collective-permute-start(bf16[128,256]{0,1:T(8,128)(2,1)S(1)} %bitcast.211), channel_id=1, source_target_pairs={{0,1},{1,2},{2,3},{3,0},{4,5},{5,6},{6,7},{7,4},{8,9},{9,10},{10,1... | collective-permute-start | bytes 196616 | tf_op jit(solution)/shard_map/ppermute | solution.py:293
  216.8 4.6 %collective-permute-start.19 = (bf16[128,256]{0,1:T(8,128)(2,1)S(1)}, bf16[128,256]{0,1:T(8,128)(2,1)S(1)}, u32[]{:S(2)}, u32[]{:S(2)}) collective-permute-start(bf16[128,256]{0,1:T(8,128)(2,1)S(1)} %bitcast.212), channel_id=1, source_target_pairs={{0,2},{1,3},{2,0},{3,1},{4,6},{5,7},{6,4},{7,5},{8,10},{9,11},{10,... | collective-permute-start | bytes 196616 | tf_op jit(solution)/shard_map/ppermute | solution.py:293
  217.3 4.7 %collective-permute-start.20 = (bf16[128,256]{0,1:T(8,128)(2,1)S(1)}, bf16[128,256]{0,1:T(8,128)(2,1)S(1)}, u32[]{:S(2)}, u32[]{:S(2)}) collective-permute-start(bf16[128,256]{0,1:T(8,128)(2,1)S(1)} %bitcast.213), channel_id=1, source_target_pairs={{0,3},{1,0},{2,1},{3,2},{4,7},{5,4},{6,5},{7,6},{8,11},{9,8},{10,9... | collective-permute-start | bytes 196616 | tf_op jit(solution)/shard_map/ppermute | solution.py:293
  258.6 10.2 %collective-permute-start.24 = (bf16[640,256]{1,0:T(8,128)(2,1)S(1)}, bf16[640,256]{1,0:T(8,128)(2,1)S(1)}, u32[]{:S(2)}, u32[]{:S(2)}) collective-permute-start(bf16[640,256]{1,0:T(8,128)(2,1)S(1)} %reshape_squeeze.3), channel_id=1, source_target_pairs={{0,1},{1,2},{2,3},{3,0},{4,5},{5,6},{6,7},{7,4},{8,9},{9,10},{10,1... | collective-permute-start | bytes 983048 | tf_op jit(solution)/shard_map/ppermute | solution.py:293
  259.7 16.9 %collective-permute-start.25 = (bf16[640,256]{1,0:T(8,128)(2,1)S(1)}, bf16[640,256]{1,0:T(8,128)(2,1)S(1)}, u32[]{:S(2)}, u32[]{:S(2)}) collective-permute-start(bf16[640,256]{1,0:T(8,128)(2,1)S(1)} %reshape_squeeze.3), channel_id=1, source_target_pairs={{0,2},{1,3},{2,0},{3,1},{4,6},{5,7},{6,4},{7,5},{8,10},{9,11},{10,... | collective-permute-start | bytes 983048 | tf_op jit(solution)/shard_map/ppermute | solution.py:293
  262.1 14.4 %collective-permute-start.26 = (bf16[640,256]{1,0:T(8,128)(2,1)S(1)}, bf16[640,256]{1,0:T(8,128)(2,1)S(1)}, u32[]{:S(2)}, u32[]{:S(2)}) collective-permute-start(bf16[640,256]{1,0:T(8,128)(2,1)S(1)} %reshape_squeeze.3), channel_id=1, source_target_pairs={{0,3},{1,0},{2,1},{3,2},{4,7},{5,4},{6,5},{7,6},{8,11},{9,8},{10,9... | collective-permute-start | bytes 983048 | tf_op jit(solution)/shard_map/ppermute | solution.py:293
  284.5 9.9 %collective-permute-start.27 = (bf16[640,256]{1,0:T(8,128)(2,1)}, bf16[640,256]{1,0:T(8,128)(2,1)S(1)}, u32[]{:S(2)}, u32[]{:S(2)}) collective-permute-start(bf16[640,256]{1,0:T(8,128)(2,1)} %get-tuple-element.60), channel_id=1, source_target_pairs={{0,1},{1,2},{2,3},{3,0},{4,5},{5,6},{6,7},{7,4},{8,9},{9,10},{10,1... | collective-permute-start | bytes 983048 | tf_op jit(solution)/shard_map/ppermute | solution.py:341
  285.9 17.4 %collective-permute-start.28 = (bf16[640,256]{1,0:T(8,128)(2,1)S(1)}, bf16[640,256]{1,0:T(8,128)(2,1)}, u32[]{:S(2)}, u32[]{:S(2)}) collective-permute-start(bf16[640,256]{1,0:T(8,128)(2,1)S(1)} %get-tuple-element.62), channel_id=1, source_target_pairs={{0,2},{1,3},{2,0},{3,1},{4,6},{5,7},{6,4},{7,5},{8,10},{9,11},{10,... | collective-permute-start | bytes 983048 | tf_op jit(solution)/shard_map/ppermute | solution.py:341
  288.6 14.7 %collective-permute-start.29 = (bf16[640,256]{1,0:T(8,128)(2,1)S(1)}, bf16[640,256]{1,0:T(8,128)(2,1)}, u32[]{:S(2)}, u32[]{:S(2)}) collective-permute-start(bf16[640,256]{1,0:T(8,128)(2,1)S(1)} %get-tuple-element.61), channel_id=1, source_target_pairs={{0,3},{1,0},{2,1},{3,2},{4,7},{5,4},{6,5},{7,6},{8,11},{9,8},{10,9... | collective-permute-start | bytes 983048 | tf_op jit(solution)/shard_map/ppermute | solution.py:341
  305.5 24.0 %all-to-all-start.1 = ((bf16[64,1,10,256]{3,2,1,0:T(8,128)(2,1)}), bf16[64,1,10,256]{3,2,1,0:T(8,128)(2,1)S(1)}, u32[]{:S(2)}, u32[]{:S(2)}) async-start(bf16[64,1,10,256]{3,2,1,0:T(8,128)(2,1)} %bitcast.79), calls=%async_computation.1 | async-start | bytes 1048576 | tf_op jit(solution)/shard_map/all_to_all | solution.py:345
  (14 other events, 142.1 us)

commit v6 on v5

--- a/solution.py
+++ b/solution.py
@@ -255,6 +255,13 @@
     bit_names += [quarter_bits + k for k in range(request_bits - 1, -1, -1)]
     acc_names = bit_names + ["h", "d", "q"]
     stat_names = bit_names + ["s", "q"]
+    flat_ids = expert_ids.reshape(-1)
+    onehot = (flat_ids[:, None] == jnp.arange(EXPERTS, dtype=jnp.int32)[None, :]).astype(jnp.int32)
+    ranks = jnp.sum((jnp.cumsum(onehot, axis=0) - 1) * onehot, axis=1)
+    target = (flat_ids * CAP + ranks).reshape(tok_rows, TOP)
+    slot_hits = target[:, :, None] == jnp.arange(EXPERTS * CAP, dtype=jnp.int32)[None, None, :]
+    placing = jnp.any(slot_hits, axis=1).astype(jnp.bfloat16)
+    routing = (target, placing)
     bit_count = request_bits + quarter_bits
     for bit in ([0, 1, 3, 2, 4, 5] if bit_count == 6 else list(range(bit_count))):
         acc_axis = acc_names.index(bit)
@@ -283,6 +290,9 @@
             got_factor, d_axis
         )
         stats = jnp.concatenate([m_new, l_new], axis=s_axis)
+        if bit == 0:
+            acc_req, stats, routing = lax.optimization_barrier((acc_req, stats, routing))
+    target, placing = routing
     attention = acc_req / stats[local_heads:][:, None, :]
     attention = jnp.transpose(attention, (2, 0, 1)).reshape(tok_rows, -1).astype(jnp.bfloat16)
     tp_count = lax.axis_size("tp")
@@ -306,12 +316,7 @@
     logits = jnp.dot(moe_in.astype(jnp.float32), router, precision=lax.Precision.HIGHEST)
     chosen = jax.nn.sigmoid(jnp.take_along_axis(logits, expert_ids, axis=1))
     gates = chosen / jnp.sum(chosen, axis=1, keepdims=True)
-    flat_ids = expert_ids.reshape(-1)
-    onehot = (flat_ids[:, None] == jnp.arange(EXPERTS, dtype=jnp.int32)[None, :]).astype(jnp.int32)
-    ranks = jnp.sum((jnp.cumsum(onehot, axis=0) - 1) * onehot, axis=1)
-    target = (flat_ids * CAP + ranks).reshape(tok_rows, TOP)
     hits = target[:, :, None] == jnp.arange(EXPERTS * CAP, dtype=jnp.int32)[None, None, :]
-    placing = jnp.any(hits, axis=1).astype(jnp.bfloat16)
     combining = jnp.sum(jnp.where(hits, gates[:, :, None], 0.0), axis=1)
     width = moe_in.shape[1]
     tp_width = width // tp_count

time: 332 us -> 334 us (level)
    unnamed x32 -> x38, local copies, waits for them, and re-layouts: 7.81 us -> 8.39 us
  transfers between devices with their start and end apart: 31 -> 31, of which waited for: 20 -> 19; matrix products, arithmetic and copies ran while one was open for 10% -> 10% of each run, Pallas kernels for 0% -> 0%
where the time goes in v6:
time: 334 us; the launch traced here: 333 us
  waiting for transfers between devices  117 us (35%)
  starting transfers between devices  63.9 us (19%)
  Pallas kernels  49.2 us (15%)
  blocking collectives  32.1 us (10%)
  other arithmetic  28.5 us (9%)
  local copies, waits for them, and re-layouts  27.3 us (8%)
  matrix products  14.3 us (4%)
    pallas_call x1, Pallas kernels, local_attention(): pl.pallas_call(attend_kernel, grid_spec=grid_spec, out_shape=[jax.ShapeDt...  49.2 us
    ppermute x6, waiting for transfers between devices, shards(): got = lax.ppermute(gathered, 'seq', pairs)  37.7 us
    all_to_all x1, blocking collectives, shards(): lax.all_to_all(outgoing, 'seq', split_axis=0, concat_axis=0, tiled=True)  32.1 us
    ppermute x9, waiting for transfers between devices, tp_gather(): lax.ppermute(value, 'tp', [(i, (i + k) % tp_count) for i in range(tp_coun...  24.7 us
    ppermute x6, starting transfers between devices, shards(): got = lax.ppermute(gathered, 'seq', pairs)  19.4 us
    ppermute x6, waiting for transfers between devices, shards(): lax.ppermute(send_acc.astype(jnp.bfloat16), 'seq', pairs)  15.9 us
    ppermute x3, waiting for transfers between devices, shards(): lax.ppermute(target_cols, 'tp', [(i, (i + k) % tp_count) for i in range(t...  14.4 us
    all_to_all x1, waiting for transfers between devices, shards(): lax.all_to_all(produced.astype(jnp.bfloat16), 'seq', split_axis=0, concat...  14.1 us
  transfers between devices with their start and end apart: 31, of which 19 were waited for; matrix products, arithmetic and copies ran while one was open for 10% of the time, Pallas kernels for 0%

profile of v6, /device:TPU:1, one launch (start us, length us, event | category | flops | bytes accessed | tf_op | source)
XLA Modules:
  0.0 333.3 jit_solution(12888613761535668315)
XLA Ops:
  2.6 7.8 %collective-permute-start = (bf16[128,256]{1,0:T(8,128)(2,1)S(1)}, bf16[128,256]{1,0:T(8,128)(2,1)S(1)}, u32[]{:S(2)}, u32[]{:S(2)}) collective-permute-start(bf16[128,256]{1,0:T(8,128)(2,1)S(1)} %convolution_convert_fusion.4), channel_id=1, source_target_pairs={{0,128},{4,132},{8,136},{12,140},{16,144},{20,148},{24,152},{28,15... | collective-permute-start | bytes 196616 | tf_op jit(solution)/shard_map/ppermute | solution.py:214
  13.7 5.4 %collective-permute-done.1 = bf16[2,128,256]{2,1,0:T(8,128)(2,1)S(1)} collective-permute-done((bf16[2,128,256]{2,1,0:T(8,128)(2,1)S(1)}, bf16[2,128,256]{2,1,0:T(8,128)(2,1)S(1)}, u32[]{:S(2)}, u32[]{:S(2)}) %collective-permute-start.1) | collective-permute-done | bytes 131104 | tf_op jit(solution)/shard_map/ppermute | solution.py:214
  19.1 4.6 %collective-permute-start.2 = (bf16[2,2,128,256]{3,2,0,1:T(8,128)(2,1)S(1)}, bf16[2,2,128,256]{3,2,0,1:T(8,128)(2,1)S(1)}, u32[]{:S(2)}, u32[]{:S(2)}) collective-permute-start(bf16[2,2,128,256]{3,2,0,1:T(8,128)(2,1)S(1)} %pad_maximum_fusion.7), channel_id=1, source_target_pairs={{0,16},{4,20},{8,24},{12,28},{16,0},{20,4},{24,8},{28,12},{32,48},... | collective-permute-start | bytes 786440 | tf_op jit(solution)/shard_map/ppermute | solution.py:214
  23.7 5.1 %collective-permute-done.2 = bf16[2,2,128,256]{3,2,0,1:T(8,128)(2,1)S(1)} collective-permute-done((bf16[2,2,128,256]{3,2,0,1:T(8,128)(2,1)S(1)}, bf16[2,2,128,256]{3,2,0,1:T(8,128)(2,1)S(1)}, u32[]{:S(2)}, u32[]{:S(2)}) %collective-permute-start.2) | collective-permute-done | bytes 262176 | tf_op jit(solution)/shard_map/ppermute | solution.py:214
  30.1 10.2 %collective-permute-done.3 = bf16[2,2,2,128,256]{4,3,0,1,2:T(8,128)(2,1)S(1)} collective-permute-done((bf16[2,2,2,128,256]{4,3,0,1,2:T(8,128)(2,1)S(1)}, bf16[2,2,2,128,256]{4,3,0,1,2:T(8,128)(2,1)S(1)}, u32[]{:S(2)}, u32[]{:S(2)}) %collective-permute-start.3) | collective-permute-done | bytes 524320 | tf_op jit(solution)/shard_map/ppermute | solution.py:214
  52.8 11.5 %collective-permute-done.4 = bf16[2,2,2,2,128,256]{5,4,0,1,3,2:T(8,128)(2,1)} collective-permute-done((bf16[2,2,2,2,128,256]{5,4,0,1,3,2:T(8,128)(2,1)}, bf16[2,2,2,2,128,256]{5,4,0,1,3,2:T(8,128)(2,1)}, u32[]{:S(2)}, u32[]{:S(2)}) %collective-permute-start.4) | collective-permute-done | bytes 1048608 | tf_op jit(solution)/shard_map/ppermute | solution.py:214
  65.9 3.6 %collective-permute-start.5 = (bf16[2,2,2,2,2,128,256]{6,5,0,1,3,2,4:T(8,128)(2,1)S(1)}, bf16[2,2,2,2,2,128,256]{6,5,0,1,3,2,4:T(8,128)(2,1)}, u32[]{:S(2)}, u32[]{:S(2)}) collective-permute-start(bf16[2,2,2,2,2,128,256]{6,5,0,1,3,2,4:T(8,128)(2,1)S(1)} %pad_maximum_fusion.1), channel_id=1, source_target_pairs={{0,4},{4,0},{8,12},{12,8},{16,20},{20,16},{24,28},{28,24},{32,36},... | collective-permute-start | bytes 6291464 | tf_op jit(solution)/shard_map/ppermute | solution.py:214
  69.6 3.8 %collective-permute-done.5 = bf16[2,2,2,2,2,128,256]{6,5,0,1,3,2,4:T(8,128)(2,1)} collective-permute-done((bf16[2,2,2,2,2,128,256]{6,5,0,1,3,2,4:T(8,128)(2,1)S(1)}, bf16[2,2,2,2,2,128,256]{6,5,0,1,3,2,4:T(8,128)(2,1)}, u32[]{:S(2)}, u32[]{:S(2)}) %collective-permute-start.5) | collective-permute-done | bytes 2097184 | tf_op jit(solution)/shard_map/ppermute | solution.py:214
  77.9 49.2 %shard_map.136 = (f32[4,16,4,64,128]{4,3,2,1,0:T(8,128)}, f32[4,16,8,128]{3,2,1,0:T(8,128)}) custom-call(s32[34]{0:T(128)} %copy-done.16, s32[34]{0:T(128)} %get-tuple-element.22.page_ref, s32[34]{0:T(128)} %gather_fusion.2, s32[34]{0:T(128)} %gather_fusion.3, s32[34]{0:T(128)} %compare_convert_fusion.fresh_ref, bf16[16,512,256]{2,1,0:T(8,128)(2,1)} %bitcast.204, ...), custom_call_target="tpu_custom_call" | custom-call | tf_op jit(solution)/shard_map/pallas_call | solution.py:130
  127.1 4.4 %broadcast_select_fusion = f32[4,16,4,64,128]{4,3,2,1,0:T(8,128)S(1)} fusion(f32[4,16,4,64,128]{4,3,2,1,0:T(8,128)} %get-tuple-element.29, pred[16]{0:T(512)(128)(4,1)S(1)} %fusion.80), kind=kLoop, calls=%fused_computation.12 | loop fusion | flops 2097152 | bytes 16777232 | tf_op jit(solution)/shard_map/jit(_where)/select_n | solution.py:247
  131.6 3.3 copy-done.2
  137.3 2.6 collective-permute-start.22
  145.8 4.0 %fusion = f32[2,2,2,2,2,4,64,128]{7,6,5,4,3,2,1,0:T(8,128)S(1)} fusion(bf16[2,2,2,2,2,4,64,128]{7,6,5,4,3,2,1,0:T(8,128)(2,1)} %collective-permute-done.7, f32[2,2,2,2,2,2,4,64,128]{8,7,6,5,4,3,2,1,0:T(8,128)} %bitcast.203, s32[]{:T(128)S(6)} %select_n.333, f32[2,2,2,2,2,4,128]{6,5,4,3,2,1,0:T(4,128)S(1)} %get-tuple-element.58, ...), kind=kLoop, calls=%fused_computation.10 | loop fusion | flops 4194304 | bytes 10616836 | tf_op jit(solution)/shard_map/add | solution.py:289
  154.7 8.7 %collective-permute-done.22 = bf16[256,1024]{1,0:T(8,128)(2,1)} collective-permute-done((bf16[256,1024]{1,0:T(8,128)(2,1)}, bf16[256,1024]{1,0:T(8,128)(2,1)}, u32[]{:S(2)}, u32[]{:S(2)}) %collective-permute-start.22) | collective-permute-done | bytes 524320 | tf_op jit(solution)/shard_map/ppermute | solution.py:303
  163.4 3.2 pad_maximum_fusion.2
  168.8 10.6 %collective-permute-done.8 = f32[2,2,2,2,8,128]{5,4,3,2,1,0:T(8,128)S(1)} collective-permute-done((f32[2,2,2,2,8,128]{5,4,3,2,1,0:T(8,128)S(1)}, f32[2,2,2,2,8,128]{5,4,3,2,1,0:T(8,128)S(1)}, u32[]{:S(2)}, u32[]{:S(2)}) %collective-permute-start.8) | collective-permute-done | bytes 65568 | tf_op jit(solution)/shard_map/ppermute | solution.py:278
  183.9 2.8 collective-permute-start.12
  186.8 8.0 %collective-permute-done.11 = bf16[2,2,2,4,64,128]{5,4,3,2,1,0:T(8,128)(2,1)S(1)} collective-permute-done((bf16[2,2,2,4,64,128]{5,4,3,2,1,0:T(8,128)(2,1)S(1)}, bf16[2,2,2,4,64,128]{5,4,3,2,1,0:T(8,128)(2,1)S(1)}, u32[]{:S(2)}, u32[]{:S(2)}) %collective-permute-start.11) | collective-permute-done | bytes 524320 | tf_op jit(solution)/shard_map/ppermute | solution.py:277
  195.1 2.8 collective-permute-start.13
  198.0 4.5 %collective-permute-done.13 = bf16[2,2,4,64,128]{4,3,2,1,0:T(8,128)(2,1)S(1)} collective-permute-done((bf16[2,2,4,64,128]{4,3,2,1,0:T(8,128)(2,1)S(1)}, bf16[2,2,4,64,128]{4,3,2,1,0:T(8,128)(2,1)S(1)}, u32[]{:S(2)}, u32[]{:S(2)}) %collective-permute-start.13) | collective-permute-done | bytes 262176 | tf_op jit(solution)/shard_map/ppermute | solution.py:277
  202.8 8.1 %collective-permute-start.16 = (f32[8,128]{1,0:T(8,128)S(1)}, f32[8,128]{1,0:T(8,128)S(1)}, u32[]{:S(2)}, u32[]{:S(2)}) collective-permute-start(f32[8,128]{1,0:T(8,128)S(1)} %get-tuple-element.98), channel_id=1, source_target_pairs={{0,128},{4,132},{8,136},{12,140},{16,144},{20,148},{24,152},{28,15... | collective-permute-start | bytes 12296 | tf_op jit(solution)/shard_map/ppermute | solution.py:278
  211.0 3.8 %collective-permute-start.17 = (bf16[4,64,128]{2,1,0:T(8,128)(2,1)S(1)}, bf16[4,64,128]{2,1,0:T(8,128)(2,1)S(1)}, u32[]{:S(2)}, u32[]{:S(2)}) collective-permute-start(bf16[4,64,128]{2,1,0:T(8,128)(2,1)S(1)} %fusion.58), channel_id=1, source_target_pairs={{0,128},{4,132},{8,136},{12,140},{16,144},{20,148},{24,152},{28,15... | collective-permute-start | bytes 196616 | tf_op jit(solution)/shard_map/ppermute | solution.py:277
  214.7 3.3 %collective-permute-done.17 = bf16[4,64,128]{2,1,0:T(8,128)(2,1)S(1)} collective-permute-done((bf16[4,64,128]{2,1,0:T(8,128)(2,1)S(1)}, bf16[4,64,128]{2,1,0:T(8,128)(2,1)S(1)}, u32[]{:S(2)}, u32[]{:S(2)}) %collective-permute-start.17) | collective-permute-done | bytes 65568 | tf_op jit(solution)/shard_map/ppermute | solution.py:277
  228.0 32.1 %all_to_all.10 = bf16[64,1,10,256]{3,2,1,0:T(8,128)(2,1)S(1)} all-to-all(bf16[64,1,10,256]{3,2,1,0:T(8,128)(2,1)S(1)} %bitcast.206), channel_id=1, replica_groups=mesh['seq'=64,'tp'=4] {'seq'}, dimensions={0} | all-to-all | bytes 655360 | tf_op jit(solution)/shard_map/all_to_all | solution.py:332
  263.9 6.4 %collective-permute-done.24 = bf16[640,256]{1,0:T(8,128)(2,1)S(1)} collective-permute-done((bf16[640,256]{1,0:T(8,128)(2,1)S(1)}, bf16[640,256]{1,0:T(8,128)(2,1)S(1)}, u32[]{:S(2)}, u32[]{:S(2)}) %collective-permute-start.24) | collective-permute-done | bytes 327712 | tf_op jit(solution)/shard_map/ppermute | solution.py:303
  270.3 7.8 %collective-permute-done.25 = bf16[640,256]{1,0:T(8,128)(2,1)S(1)} collective-permute-done((bf16[640,256]{1,0:T(8,128)(2,1)S(1)}, bf16[640,256]{1,0:T(8,128)(2,1)S(1)}, u32[]{:S(2)}, u32[]{:S(2)}) %collective-permute-start.25) | collective-permute-done | bytes 327712 | tf_op jit(solution)/shard_map/ppermute | solution.py:303
  282.1 3.2 convolution_convert_fusion
  287.5 2.7 collective-permute-start.28
  290.5 5.5 %collective-permute-done.27 = bf16[640,256]{1,0:T(8,128)(2,1)S(1)} collective-permute-done((bf16[640,256]{1,0:T(8,128)(2,1)}, bf16[640,256]{1,0:T(8,128)(2,1)S(1)}, u32[]{:S(2)}, u32[]{:S(2)}) %collective-permute-start.27) | collective-permute-done | bytes 327712 | tf_op jit(solution)/shard_map/ppermute | solution.py:346
  296.1 8.8 %collective-permute-done.28 = bf16[640,256]{1,0:T(8,128)(2,1)} collective-permute-done((bf16[640,256]{1,0:T(8,128)(2,1)S(1)}, bf16[640,256]{1,0:T(8,128)(2,1)}, u32[]{:S(2)}, u32[]{:S(2)}) %collective-permute-start.28) | collective-permute-done | bytes 327712 | tf_op jit(solution)/shard_map/ppermute | solution.py:346
  307.1 6.3 %all-to-all-start.1 = ((bf16[64,1,10,256]{3,2,1,0:T(8,128)(2,1)}), bf16[64,1,10,256]{3,2,1,0:T(8,128)(2,1)S(1)}, u32[]{:S(2)}, u32[]{:S(2)}) async-start(bf16[64,1,10,256]{3,2,1,0:T(8,128)(2,1)} %bitcast.79), calls=%async_computation.1 | async-start | bytes 1048576 | tf_op jit(solution)/shard_map/all_to_all | solution.py:350
  316.9 14.1 %all-to-all-done.1 = bf16[64,1,10,256]{3,2,1,0:T(8,128)(2,1)S(1)} async-done(((bf16[64,1,10,256]{3,2,1,0:T(8,128)(2,1)}), bf16[64,1,10,256]{3,2,1,0:T(8,128)(2,1)S(1)}, u32[]{:S(2)}, u32[]{:S(2)}) %all-to-all-start.1) | async-done | bytes 327712 | tf_op jit(solution)/shard_map/all_to_all | solution.py:350
  (188 shorter events, 74.3 us)
Async XLA Ops:
  0.0 282.1 %copy-start = (bf16[1,352,1024]{2,1,0:T(8,128)(2,1)S(1)}, bf16[1,352,1024]{2,1,0:T(8,128)(2,1)}, u32[]{:S(2)}) copy-start(bf16[1,352,1024]{2,1,0:T(8,128)(2,1)} %param.27) | copy-start | bytes 2162692
  2.6 9.6 %collective-permute-start = (bf16[128,256]{1,0:T(8,128)(2,1)S(1)}, bf16[128,256]{1,0:T(8,128)(2,1)S(1)}, u32[]{:S(2)}, u32[]{:S(2)}) collective-permute-start(bf16[128,256]{1,0:T(8,128)(2,1)S(1)} %convolution_convert_fusion.4), channel_id=1, source_target_pairs={{0,128},{4,132},{8,136},{12,140},{16,144},{20,148},{24,152},{28,15... | collective-permute-start | bytes 196616 | tf_op jit(solution)/shard_map/ppermute | solution.py:214
  12.2 6.9 %collective-permute-start.1 = (bf16[2,128,256]{2,1,0:T(8,128)(2,1)S(1)}, bf16[2,128,256]{2,1,0:T(8,128)(2,1)S(1)}, u32[]{:S(2)}, u32[]{:S(2)}) collective-permute-start(bf16[2,128,256]{2,1,0:T(8,128)(2,1)S(1)} %pad_maximum_fusion.12), channel_id=1, source_target_pairs={{0,64},{4,68},{8,72},{12,76},{16,80},{20,84},{24,88},{28,92},{32,9... | collective-permute-start | bytes 393224 | tf_op jit(solution)/shard_map/ppermute | solution.py:214
  19.1 9.7 %collective-permute-start.2 = (bf16[2,2,128,256]{3,2,0,1:T(8,128)(2,1)S(1)}, bf16[2,2,128,256]{3,2,0,1:T(8,128)(2,1)S(1)}, u32[]{:S(2)}, u32[]{:S(2)}) collective-permute-start(bf16[2,2,128,256]{3,2,0,1:T(8,128)(2,1)S(1)} %pad_maximum_fusion.7), channel_id=1, source_target_pairs={{0,16},{4,20},{8,24},{12,28},{16,0},{20,4},{24,8},{28,12},{32,48},... | collective-permute-start | bytes 786440 | tf_op jit(solution)/shard_map/ppermute | solution.py:214
  28.9 11.4 %collective-permute-start.3 = (bf16[2,2,2,128,256]{4,3,0,1,2:T(8,128)(2,1)S(1)}, bf16[2,2,2,128,256]{4,3,0,1,2:T(8,128)(2,1)S(1)}, u32[]{:S(2)}, u32[]{:S(2)}) collective-permute-start(bf16[2,2,2,128,256]{4,3,0,1,2:T(8,128)(2,1)S(1)} %pad_maximum_fusion.6), channel_id=1, source_target_pairs={{0,32},{4,36},{8,40},{12,44},{16,48},{20,52},{24,56},{28,60},{32,0... | collective-permute-start | bytes 1572872 | tf_op jit(solution)/shard_map/ppermute | solution.py:214
  41.5 22.8 %collective-permute-start.4 = (bf16[2,2,2,2,128,256]{5,4,0,1,3,2:T(8,128)(2,1)}, bf16[2,2,2,2,128,256]{5,4,0,1,3,2:T(8,128)(2,1)}, u32[]{:S(2)}, u32[]{:S(2)}) collective-permute-start(bf16[2,2,2,2,128,256]{5,4,0,1,3,2:T(8,128)(2,1)} %pad_maximum_fusion.5), channel_id=1, source_target_pairs={{0,8},{4,12},{8,0},{12,4},{16,24},{20,28},{24,16},{28,20},{32,40},... | collective-permute-start | bytes 3145736 | tf_op jit(solution)/shard_map/ppermute | solution.py:214
  65.9 7.5 %collective-permute-start.5 = (bf16[2,2,2,2,2,128,256]{6,5,0,1,3,2,4:T(8,128)(2,1)S(1)}, bf16[2,2,2,2,2,128,256]{6,5,0,1,3,2,4:T(8,128)(2,1)}, u32[]{:S(2)}, u32[]{:S(2)}) collective-permute-start(bf16[2,2,2,2,2,128,256]{6,5,0,1,3,2,4:T(8,128)(2,1)S(1)} %pad_maximum_fusion.1), channel_id=1, source_target_pairs={{0,4},{4,0},{8,12},{12,8},{16,20},{20,16},{24,28},{28,24},{32,36},... | collective-permute-start | bytes 6291464 | tf_op jit(solution)/shard_map/ppermute | solution.py:214
  135.3 10.5 %collective-permute-start.7 = (bf16[2,2,2,2,2,4,64,128]{7,6,5,4,3,2,1,0:T(8,128)(2,1)S(1)}, bf16[2,2,2,2,2,4,64,128]{7,6,5,4,3,2,1,0:T(8,128)(2,1)}, u32[]{:S(2)}, u32[]{:S(2)}) collective-permute-start(bf16[2,2,2,2,2,4,64,128]{7,6,5,4,3,2,1,0:T(8,128)(2,1)S(1)} %fusion.1), channel_id=1, source_target_pairs={{0,4},{4,0},{8,12},{12,8},{16,20},{20,16},{24,28},{28,24},{32,36},... | collective-permute-start | bytes 6291464 | tf_op jit(solution)/shard_map/ppermute | solution.py:277
  135.8 18.9 %collective-permute-start.21 = (bf16[256,1024]{1,0:T(8,128)(2,1)}, bf16[256,1024]{1,0:T(8,128)(2,1)}, u32[]{:S(2)}, u32[]{:S(2)}) collective-permute-start(bf16[256,1024]{1,0:T(8,128)(2,1)} %param.21), channel_id=1, source_target_pairs={{0,1},{1,2},{2,3},{3,0},{4,5},{5,6},{6,7},{7,4},{8,9},{9,10},{10,1... | collective-permute-start | bytes 1572872 | tf_op jit(solution)/shard_map/ppermute | solution.py:303
  137.3 26.0 %collective-permute-start.22 = (bf16[256,1024]{1,0:T(8,128)(2,1)}, bf16[256,1024]{1,0:T(8,128)(2,1)}, u32[]{:S(2)}, u32[]{:S(2)}) collective-permute-start(bf16[256,1024]{1,0:T(8,128)(2,1)} %param.21), channel_id=1, source_target_pairs={{0,2},{1,3},{2,0},{3,1},{4,6},{5,7},{6,4},{7,5},{8,10},{9,11},{10,... | collective-permute-start | bytes 1572872 | tf_op jit(solution)/shard_map/ppermute | solution.py:303
  139.9 23.4 %collective-permute-start.23 = (bf16[256,1024]{1,0:T(8,128)(2,1)}, bf16[256,1024]{1,0:T(8,128)(2,1)}, u32[]{:S(2)}, u32[]{:S(2)}) collective-permute-start(bf16[256,1024]{1,0:T(8,128)(2,1)} %param.21), channel_id=1, source_target_pairs={{0,3},{1,0},{2,1},{3,2},{4,7},{5,4},{6,5},{7,6},{8,11},{9,8},{10,9... | collective-permute-start | bytes 1572872 | tf_op jit(solution)/shard_map/ppermute | solution.py:303
  143.3 2.4 collective-permute-start.6
  153.1 26.8 %collective-permute-start.9 = (bf16[2,2,2,2,4,64,128]{6,5,4,3,2,1,0:T(8,128)(2,1)}, bf16[2,2,2,2,4,64,128]{6,5,4,3,2,1,0:T(8,128)(2,1)}, u32[]{:S(2)}, u32[]{:S(2)}) collective-permute-start(bf16[2,2,2,2,4,64,128]{6,5,4,3,2,1,0:T(8,128)(2,1)} %fusion.18), channel_id=1, source_target_pairs={{0,8},{4,12},{8,0},{12,4},{16,24},{20,28},{24,16},{28,20},{32,40},... | collective-permute-start | bytes 3145736 | tf_op jit(solution)/shard_map/ppermute | solution.py:277
  154.3 25.0 %collective-permute-start.8 = (f32[2,2,2,2,8,128]{5,4,3,2,1,0:T(8,128)S(1)}, f32[2,2,2,2,8,128]{5,4,3,2,1,0:T(8,128)S(1)}, u32[]{:S(2)}, u32[]{:S(2)}) collective-permute-start(f32[2,2,2,2,8,128]{5,4,3,2,1,0:T(8,128)S(1)} %get-tuple-element.88), channel_id=1, source_target_pairs={{0,8},{4,12},{8,0},{12,4},{16,24},{20,28},{24,16},{28,20},{32,40},... | collective-permute-start | bytes 196616 | tf_op jit(solution)/shard_map/ppermute | solution.py:278
  179.4 4.4 %collective-permute-start.10 = (f32[2,2,2,8,128]{4,3,2,1,0:T(8,128)S(1)}, f32[2,2,2,8,128]{4,3,2,1,0:T(8,128)S(1)}, u32[]{:S(2)}, u32[]{:S(2)}) collective-permute-start(f32[2,2,2,8,128]{4,3,2,1,0:T(8,128)S(1)} %get-tuple-element.92), channel_id=1, source_target_pairs={{0,32},{4,36},{8,40},{12,44},{16,48},{20,52},{24,56},{28,60},{32,0... | collective-permute-start | bytes 98312 | tf_op jit(solution)/shard_map/ppermute | solution.py:278
  182.3 12.4 %collective-permute-start.11 = (bf16[2,2,2,4,64,128]{5,4,3,2,1,0:T(8,128)(2,1)S(1)}, bf16[2,2,2,4,64,128]{5,4,3,2,1,0:T(8,128)(2,1)S(1)}, u32[]{:S(2)}, u32[]{:S(2)}) collective-permute-start(bf16[2,2,2,4,64,128]{5,4,3,2,1,0:T(8,128)(2,1)S(1)} %fusion.38), channel_id=1, source_target_pairs={{0,32},{4,36},{8,40},{12,44},{16,48},{20,52},{24,56},{28,60},{32,0... | collective-permute-start | bytes 1572872 | tf_op jit(solution)/shard_map/ppermute | solution.py:277
  183.9 13.9 %collective-permute-start.12 = (f32[2,2,8,128]{3,2,1,0:T(8,128)S(1)}, f32[2,2,8,128]{3,2,1,0:T(8,128)S(1)}, u32[]{:S(2)}, u32[]{:S(2)}) collective-permute-start(f32[2,2,8,128]{3,2,1,0:T(8,128)S(1)} %get-tuple-element.94), channel_id=1, source_target_pairs={{0,16},{4,20},{8,24},{12,28},{16,0},{20,4},{24,8},{28,12},{32,48},... | collective-permute-start | bytes 49160 | tf_op jit(solution)/shard_map/ppermute | solution.py:278
  195.1 7.4 %collective-permute-start.13 = (bf16[2,2,4,64,128]{4,3,2,1,0:T(8,128)(2,1)S(1)}, bf16[2,2,4,64,128]{4,3,2,1,0:T(8,128)(2,1)S(1)}, u32[]{:S(2)}, u32[]{:S(2)}) collective-permute-start(bf16[2,2,4,64,128]{4,3,2,1,0:T(8,128)(2,1)S(1)} %fusion.45), channel_id=1, source_target_pairs={{0,16},{4,20},{8,24},{12,28},{16,0},{20,4},{24,8},{28,12},{32,48},... | collective-permute-start | bytes 786440 | tf_op jit(solution)/shard_map/ppermute | solution.py:277
  197.9 4.9 %collective-permute-start.14 = (f32[2,8,128]{2,1,0:T(8,128)S(1)}, f32[2,8,128]{2,1,0:T(8,128)S(1)}, u32[]{:S(2)}, u32[]{:S(2)}) collective-permute-start(f32[2,8,128]{2,1,0:T(8,128)S(1)} %get-tuple-element.96), channel_id=1, source_target_pairs={{0,64},{4,68},{8,72},{12,76},{16,80},{20,84},{24,88},{28,92},{32,9... | collective-permute-start | bytes 24584 | tf_op jit(solution)/shard_map/ppermute | solution.py:278
  202.7 8.2 %collective-permute-start.15 = (bf16[2,4,64,128]{3,2,1,0:T(8,128)(2,1)S(1)}, bf16[2,4,64,128]{3,2,1,0:T(8,128)(2,1)S(1)}, u32[]{:S(2)}, u32[]{:S(2)}) collective-permute-start(bf16[2,4,64,128]{3,2,1,0:T(8,128)(2,1)S(1)} %fusion.54), channel_id=1, source_target_pairs={{0,64},{4,68},{8,72},{12,76},{16,80},{20,84},{24,88},{28,92},{32,9... | collective-permute-start | bytes 393224 | tf_op jit(solution)/shard_map/ppermute | solution.py:277
  202.8 11.9 %collective-permute-start.16 = (f32[8,128]{1,0:T(8,128)S(1)}, f32[8,128]{1,0:T(8,128)S(1)}, u32[]{:S(2)}, u32[]{:S(2)}) collective-permute-start(f32[8,128]{1,0:T(8,128)S(1)} %get-tuple-element.98), channel_id=1, source_target_pairs={{0,128},{4,132},{8,136},{12,140},{16,144},{20,148},{24,152},{28,15... | collective-permute-start | bytes 12296 | tf_op jit(solution)/shard_map/ppermute | solution.py:278
  211.0 7.1 %collective-permute-start.17 = (bf16[4,64,128]{2,1,0:T(8,128)(2,1)S(1)}, bf16[4,64,128]{2,1,0:T(8,128)(2,1)S(1)}, u32[]{:S(2)}, u32[]{:S(2)}) collective-permute-start(bf16[4,64,128]{2,1,0:T(8,128)(2,1)S(1)} %fusion.58), channel_id=1, source_target_pairs={{0,128},{4,132},{8,136},{12,140},{16,144},{20,148},{24,152},{28,15... | collective-permute-start | bytes 196616 | tf_op jit(solution)/shard_map/ppermute | solution.py:277
  218.1 4.4 %collective-permute-start.18 = (bf16[128,256]{0,1:T(8,128)(2,1)S(1)}, bf16[128,256]{0,1:T(8,128)(2,1)S(1)}, u32[]{:S(2)}, u32[]{:S(2)}) collective-permute-start(bf16[128,256]{0,1:T(8,128)(2,1)S(1)} %bitcast.211), channel_id=1, source_target_pairs={{0,1},{1,2},{2,3},{3,0},{4,5},{5,6},{6,7},{7,4},{8,9},{9,10},{10,1... | collective-permute-start | bytes 196616 | tf_op jit(solution)/shard_map/ppermute | solution.py:303
  218.6 4.6 %collective-permute-start.19 = (bf16[128,256]{0,1:T(8,128)(2,1)S(1)}, bf16[128,256]{0,1:T(8,128)(2,1)S(1)}, u32[]{:S(2)}, u32[]{:S(2)}) collective-permute-start(bf16[128,256]{0,1:T(8,128)(2,1)S(1)} %bitcast.212), channel_id=1, source_target_pairs={{0,2},{1,3},{2,0},{3,1},{4,6},{5,7},{6,4},{7,5},{8,10},{9,11},{10,... | collective-permute-start | bytes 196616 | tf_op jit(solution)/shard_map/ppermute | solution.py:303
  219.1 4.7 %collective-permute-start.20 = (bf16[128,256]{0,1:T(8,128)(2,1)S(1)}, bf16[128,256]{0,1:T(8,128)(2,1)S(1)}, u32[]{:S(2)}, u32[]{:S(2)}) collective-permute-start(bf16[128,256]{0,1:T(8,128)(2,1)S(1)} %bitcast.213), channel_id=1, source_target_pairs={{0,3},{1,0},{2,1},{3,2},{4,7},{5,4},{6,5},{7,6},{8,11},{9,8},{10,9... | collective-permute-start | bytes 196616 | tf_op jit(solution)/shard_map/ppermute | solution.py:303
  260.2 10.2 %collective-permute-start.24 = (bf16[640,256]{1,0:T(8,128)(2,1)S(1)}, bf16[640,256]{1,0:T(8,128)(2,1)S(1)}, u32[]{:S(2)}, u32[]{:S(2)}) collective-permute-start(bf16[640,256]{1,0:T(8,128)(2,1)S(1)} %reshape_squeeze.3), channel_id=1, source_target_pairs={{0,1},{1,2},{2,3},{3,0},{4,5},{5,6},{6,7},{7,4},{8,9},{9,10},{10,1... | collective-permute-start | bytes 983048 | tf_op jit(solution)/shard_map/ppermute | solution.py:303
  261.3 16.9 %collective-permute-start.25 = (bf16[640,256]{1,0:T(8,128)(2,1)S(1)}, bf16[640,256]{1,0:T(8,128)(2,1)S(1)}, u32[]{:S(2)}, u32[]{:S(2)}) collective-permute-start(bf16[640,256]{1,0:T(8,128)(2,1)S(1)} %reshape_squeeze.3), channel_id=1, source_target_pairs={{0,2},{1,3},{2,0},{3,1},{4,6},{5,7},{6,4},{7,5},{8,10},{9,11},{10,... | collective-permute-start | bytes 983048 | tf_op jit(solution)/shard_map/ppermute | solution.py:303
  263.8 14.4 %collective-permute-start.26 = (bf16[640,256]{1,0:T(8,128)(2,1)S(1)}, bf16[640,256]{1,0:T(8,128)(2,1)S(1)}, u32[]{:S(2)}, u32[]{:S(2)}) collective-permute-start(bf16[640,256]{1,0:T(8,128)(2,1)S(1)} %reshape_squeeze.3), channel_id=1, source_target_pairs={{0,3},{1,0},{2,1},{3,2},{4,7},{5,4},{6,5},{7,6},{8,11},{9,8},{10,9... | collective-permute-start | bytes 983048 | tf_op jit(solution)/shard_map/ppermute | solution.py:303
  286.2 9.9 %collective-permute-start.27 = (bf16[640,256]{1,0:T(8,128)(2,1)}, bf16[640,256]{1,0:T(8,128)(2,1)S(1)}, u32[]{:S(2)}, u32[]{:S(2)}) collective-permute-start(bf16[640,256]{1,0:T(8,128)(2,1)} %get-tuple-element.68), channel_id=1, source_target_pairs={{0,1},{1,2},{2,3},{3,0},{4,5},{5,6},{6,7},{7,4},{8,9},{9,10},{10,1... | collective-permute-start | bytes 983048 | tf_op jit(solution)/shard_map/ppermute | solution.py:346
  287.5 17.4 %collective-permute-start.28 = (bf16[640,256]{1,0:T(8,128)(2,1)S(1)}, bf16[640,256]{1,0:T(8,128)(2,1)}, u32[]{:S(2)}, u32[]{:S(2)}) collective-permute-start(bf16[640,256]{1,0:T(8,128)(2,1)S(1)} %get-tuple-element.70), channel_id=1, source_target_pairs={{0,2},{1,3},{2,0},{3,1},{4,6},{5,7},{6,4},{7,5},{8,10},{9,11},{10,... | collective-permute-start | bytes 983048 | tf_op jit(solution)/shard_map/ppermute | solution.py:346
  290.2 14.6 %collective-permute-start.29 = (bf16[640,256]{1,0:T(8,128)(2,1)S(1)}, bf16[640,256]{1,0:T(8,128)(2,1)}, u32[]{:S(2)}, u32[]{:S(2)}) collective-permute-start(bf16[640,256]{1,0:T(8,128)(2,1)S(1)} %get-tuple-element.69), channel_id=1, source_target_pairs={{0,3},{1,0},{2,1},{3,2},{4,7},{5,4},{6,5},{7,6},{8,11},{9,8},{10,9... | collective-permute-start | bytes 983048 | tf_op jit(solution)/shard_map/ppermute | solution.py:346
  307.1 24.0 %all-to-all-start.1 = ((bf16[64,1,10,256]{3,2,1,0:T(8,128)(2,1)}), bf16[64,1,10,256]{3,2,1,0:T(8,128)(2,1)S(1)}, u32[]{:S(2)}, u32[]{:S(2)}) async-start(bf16[64,1,10,256]{3,2,1,0:T(8,128)(2,1)} %bitcast.79), calls=%async_computation.1 | async-start | bytes 1048576 | tf_op jit(solution)/shard_map/all_to_all | solution.py:350
  (17 other events, 153.7 us)

commit v7 on v5

--- a/solution.py
+++ b/solution.py
@@ -206,6 +206,12 @@
         new_keys.reshape(1, tok_rows, local_heads * DH),
         new_values.reshape(1, tok_rows, local_heads * DH),
     )
+    flat_ids = expert_ids.reshape(-1)
+    onehot = (flat_ids[:, None] == jnp.arange(EXPERTS, dtype=jnp.int32)[None, :]).astype(jnp.int32)
+    ranks = jnp.sum((jnp.cumsum(onehot, axis=0) - 1) * onehot, axis=1)
+    target = (flat_ids * CAP + ranks).reshape(tok_rows, TOP)
+    slot_hits = target[:, :, None] == jnp.arange(EXPERTS * CAP, dtype=jnp.int32)[None, None, :]
+    routing = (target, jnp.any(slot_hits, axis=1).astype(jnp.bfloat16))
     gathered = queries
     held_bits = []
     gather_count = seq_count.bit_length() - 1
@@ -219,8 +225,8 @@
         )
         held_bits.insert(position, bit)
         if len(held_bits) == gather_count - 1:
-            gathered, block_tables, fresh_kv = lax.optimization_barrier(
-                (gathered, block_tables, fresh_kv)
+            gathered, block_tables, fresh_kv, routing = lax.optimization_barrier(
+                (gathered, block_tables, fresh_kv, routing)
             )
     everyone = gathered.reshape(request_total, span_rows, local_heads * DH)
     width_heads = local_heads * DH
@@ -306,12 +312,8 @@
     logits = jnp.dot(moe_in.astype(jnp.float32), router, precision=lax.Precision.HIGHEST)
     chosen = jax.nn.sigmoid(jnp.take_along_axis(logits, expert_ids, axis=1))
     gates = chosen / jnp.sum(chosen, axis=1, keepdims=True)
-    flat_ids = expert_ids.reshape(-1)
-    onehot = (flat_ids[:, None] == jnp.arange(EXPERTS, dtype=jnp.int32)[None, :]).astype(jnp.int32)
-    ranks = jnp.sum((jnp.cumsum(onehot, axis=0) - 1) * onehot, axis=1)
-    target = (flat_ids * CAP + ranks).reshape(tok_rows, TOP)
+    target, placing = routing
     hits = target[:, :, None] == jnp.arange(EXPERTS * CAP, dtype=jnp.int32)[None, None, :]
-    placing = jnp.any(hits, axis=1).astype(jnp.bfloat16)
     combining = jnp.sum(jnp.where(hits, gates[:, :, None], 0.0), axis=1)
     width = moe_in.shape[1]
     tp_width = width // tp_count

time: 332 us -> 328 us (0.988)
  waiting for transfers between devices: 117 us -> 111 us
    ppermute x6, waiting for transfers between devices: 9.84 us -> 5.13 us  [shards(): got_stats = lax.ppermute(send_stats, 'seq', pairs)]
    ppermute x6, waiting for transfers between devices: 37.6 us -> 33.6 us  [shards(): got = lax.ppermute(gathered, 'seq', pairs)]
    unnamed x32 -> x36, local copies, waits for them, and re-layouts: 7.81 us -> 9.21 us
  transfers between devices with their start and end apart: 31 -> 31, of which waited for: 20 -> 19; matrix products, arithmetic and copies ran while one was open for 10% -> 10% of each run, Pallas kernels for 0% -> 0%
where the time goes in v7:
time: 328 us; the launch traced here: 327 us
  waiting for transfers between devices  111 us (34%)
  starting transfers between devices  65.3 us (20%)
  Pallas kernels  49.2 us (15%)
  blocking collectives  32.4 us (10%)
  local copies, waits for them, and re-layouts  27.5 us (8%)
  other arithmetic  26.4 us (8%)
  matrix products  15.3 us (5%)
    pallas_call x1, Pallas kernels, local_attention(): pl.pallas_call(attend_kernel, grid_spec=grid_spec, out_shape=[jax.ShapeDt...  49.2 us
    ppermute x6, waiting for transfers between devices, shards(): got = lax.ppermute(gathered, 'seq', pairs)  33.6 us
    all_to_all x1, blocking collectives, shards(): lax.all_to_all(outgoing, 'seq', split_axis=0, concat_axis=0, tiled=True)  32.4 us
    ppermute x9, waiting for transfers between devices, tp_gather(): lax.ppermute(value, 'tp', [(i, (i + k) % tp_count) for i in range(tp_coun...  28.8 us
    ppermute x6, starting transfers between devices, shards(): got = lax.ppermute(gathered, 'seq', pairs)  19.4 us
    ppermute x6, waiting for transfers between devices, shards(): lax.ppermute(send_acc.astype(jnp.bfloat16), 'seq', pairs)  14.7 us
    ppermute x3, waiting for transfers between devices, shards(): lax.ppermute(target_cols, 'tp', [(i, (i + k) % tp_count) for i in range(t...  14.4 us
    all_to_all x1, waiting for transfers between devices, shards(): lax.all_to_all(produced.astype(jnp.bfloat16), 'seq', split_axis=0, concat...  14.1 us
  transfers between devices with their start and end apart: 31, of which 19 were waited for; matrix products, arithmetic and copies ran while one was open for 10% of the time, Pallas kernels for 0%

profile of v7, /device:TPU:1, one launch (start us, length us, event | category | flops | bytes accessed | tf_op | source)
XLA Modules:
  0.0 327.5 jit_solution(11376156042657927003)
XLA Ops:
  2.6 7.8 %collective-permute-start = (bf16[128,256]{1,0:T(8,128)(2,1)S(1)}, bf16[128,256]{1,0:T(8,128)(2,1)S(1)}, u32[]{:S(2)}, u32[]{:S(2)}) collective-permute-start(bf16[128,256]{1,0:T(8,128)(2,1)S(1)} %convolution_convert_fusion.4), channel_id=1, source_target_pairs={{0,128},{4,132},{8,136},{12,140},{16,144},{20,148},{24,152},{28,15... | collective-permute-start | bytes 196616 | tf_op jit(solution)/shard_map/ppermute | solution.py:220
  15.6 3.5 %collective-permute-done.1 = bf16[2,128,256]{2,1,0:T(8,128)(2,1)S(1)} collective-permute-done((bf16[2,128,256]{2,1,0:T(8,128)(2,1)S(1)}, bf16[2,128,256]{2,1,0:T(8,128)(2,1)S(1)}, u32[]{:S(2)}, u32[]{:S(2)}) %collective-permute-start.1) | collective-permute-done | bytes 131104 | tf_op jit(solution)/shard_map/ppermute | solution.py:220
  19.1 4.6 %collective-permute-start.2 = (bf16[2,2,128,256]{3,2,0,1:T(8,128)(2,1)S(1)}, bf16[2,2,128,256]{3,2,0,1:T(8,128)(2,1)S(1)}, u32[]{:S(2)}, u32[]{:S(2)}) collective-permute-start(bf16[2,2,128,256]{3,2,0,1:T(8,128)(2,1)S(1)} %pad_maximum_fusion.7), channel_id=1, source_target_pairs={{0,16},{4,20},{8,24},{12,28},{16,0},{20,4},{24,8},{28,12},{32,48},... | collective-permute-start | bytes 786440 | tf_op jit(solution)/shard_map/ppermute | solution.py:220
  25.9 3.0 collective-permute-done.2
  33.6 6.8 %collective-permute-done.3 = bf16[2,2,2,128,256]{4,3,0,1,2:T(8,128)(2,1)S(1)} collective-permute-done((bf16[2,2,2,128,256]{4,3,0,1,2:T(8,128)(2,1)S(1)}, bf16[2,2,2,128,256]{4,3,0,1,2:T(8,128)(2,1)S(1)}, u32[]{:S(2)}, u32[]{:S(2)}) %collective-permute-start.3) | collective-permute-done | bytes 524320 | tf_op jit(solution)/shard_map/ppermute | solution.py:220
  48.3 15.8 %collective-permute-done.4 = bf16[2,2,2,2,128,256]{5,4,0,1,3,2:T(8,128)(2,1)S(1)} collective-permute-done((bf16[2,2,2,2,128,256]{5,4,0,1,3,2:T(8,128)(2,1)}, bf16[2,2,2,2,128,256]{5,4,0,1,3,2:T(8,128)(2,1)S(1)}, u32[]{:S(2)}, u32[]{:S(2)}) %collective-permute-start.4) | collective-permute-done | bytes 1048608 | tf_op jit(solution)/shard_map/ppermute | solution.py:220
  64.5 3.6 %collective-permute-start.5 = (bf16[2,2,2,2,2,128,256]{6,5,0,1,3,2,4:T(8,128)(2,1)S(1)}, bf16[2,2,2,2,2,128,256]{6,5,0,1,3,2,4:T(8,128)(2,1)}, u32[]{:S(2)}, u32[]{:S(2)}) collective-permute-start(bf16[2,2,2,2,2,128,256]{6,5,0,1,3,2,4:T(8,128)(2,1)S(1)} %pad_maximum_fusion.1), channel_id=1, source_target_pairs={{0,4},{4,0},{8,12},{12,8},{16,20},{20,16},{24,28},{28,24},{32,36},... | collective-permute-start | bytes 6291464 | tf_op jit(solution)/shard_map/ppermute | solution.py:220
  68.2 3.8 %collective-permute-done.5 = bf16[2,2,2,2,2,128,256]{6,5,0,1,3,2,4:T(8,128)(2,1)} collective-permute-done((bf16[2,2,2,2,2,128,256]{6,5,0,1,3,2,4:T(8,128)(2,1)S(1)}, bf16[2,2,2,2,2,128,256]{6,5,0,1,3,2,4:T(8,128)(2,1)}, u32[]{:S(2)}, u32[]{:S(2)}) %collective-permute-start.5) | collective-permute-done | bytes 2097184 | tf_op jit(solution)/shard_map/ppermute | solution.py:220
  76.6 49.2 %shard_map.136 = (f32[4,16,4,64,128]{4,3,2,1,0:T(8,128)}, f32[4,16,8,128]{3,2,1,0:T(8,128)}) custom-call(s32[34]{0:T(128)} %copy-done.15, s32[34]{0:T(128)} %get-tuple-element.20.page_ref, s32[34]{0:T(128)} %gather_fusion.2, s32[34]{0:T(128)} %gather_fusion.3, s32[34]{0:T(128)} %compare_convert_fusion.fresh_ref, bf16[16,512,256]{2,1,0:T(8,128)(2,1)} %bitcast.204, ...), custom_call_target="tpu_custom_call" | custom-call | tf_op jit(solution)/shard_map/pallas_call | solution.py:130
  125.8 4.4 %broadcast_select_fusion = f32[4,16,4,64,128]{4,3,2,1,0:T(8,128)S(1)} fusion(f32[4,16,4,64,128]{4,3,2,1,0:T(8,128)} %get-tuple-element.27, pred[16]{0:T(512)(128)(4,1)S(1)} %fusion.84), kind=kLoop, calls=%fused_computation.12 | loop fusion | flops 2097152 | bytes 16777232 | tf_op jit(solution)/shard_map/jit(_where)/select_n | solution.py:253
  130.2 3.3 copy-done.2
  140.3 4.0 %fusion = f32[2,2,2,2,2,4,64,128]{7,6,5,4,3,2,1,0:T(8,128)S(1)} fusion(bf16[2,2,2,2,2,4,64,128]{7,6,5,4,3,2,1,0:T(8,128)(2,1)} %collective-permute-done.7, f32[2,2,2,2,2,2,4,64,128]{8,7,6,5,4,3,2,1,0:T(8,128)} %bitcast.203, s32[]{:T(128)S(6)} %select_n.333, f32[2,2,2,2,2,4,128]{6,5,4,3,2,1,0:T(4,128)S(1)} %get-tuple-element.54, ...), kind=kLoop, calls=%fused_computation.10 | loop fusion | flops 4194304 | bytes 10616836 | tf_op jit(solution)/shard_map/add | solution.py:288
  150.4 12.1 %collective-permute-done.22 = bf16[256,1024]{1,0:T(8,128)(2,1)} collective-permute-done((bf16[256,1024]{1,0:T(8,128)(2,1)}, bf16[256,1024]{1,0:T(8,128)(2,1)}, u32[]{:S(2)}, u32[]{:S(2)}) %collective-permute-start.22) | collective-permute-done | bytes 524320 | tf_op jit(solution)/shard_map/ppermute | solution.py:299
  162.6 3.0 pad_maximum_fusion.2
  167.9 5.1 %collective-permute-done.8 = f32[2,2,2,2,8,128]{5,4,3,2,1,0:T(8,128)S(1)} collective-permute-done((f32[2,2,2,2,8,128]{5,4,3,2,1,0:T(8,128)S(1)}, f32[2,2,2,2,8,128]{5,4,3,2,1,0:T(8,128)S(1)}, u32[]{:S(2)}, u32[]{:S(2)}) %collective-permute-start.8) | collective-permute-done | bytes 65568 | tf_op jit(solution)/shard_map/ppermute | solution.py:277
  177.5 2.8 collective-permute-start.12
  180.3 7.1 %collective-permute-done.11 = bf16[2,2,2,4,64,128]{5,4,3,2,1,0:T(8,128)(2,1)S(1)} collective-permute-done((bf16[2,2,2,4,64,128]{5,4,3,2,1,0:T(8,128)(2,1)S(1)}, bf16[2,2,2,4,64,128]{5,4,3,2,1,0:T(8,128)(2,1)S(1)}, u32[]{:S(2)}, u32[]{:S(2)}) %collective-permute-start.11) | collective-permute-done | bytes 524320 | tf_op jit(solution)/shard_map/ppermute | solution.py:276
  187.8 2.9 collective-permute-start.13
  190.8 3.8 %collective-permute-done.13 = bf16[2,2,4,64,128]{4,3,2,1,0:T(8,128)(2,1)S(1)} collective-permute-done((bf16[2,2,4,64,128]{4,3,2,1,0:T(8,128)(2,1)S(1)}, bf16[2,2,4,64,128]{4,3,2,1,0:T(8,128)(2,1)S(1)}, u32[]{:S(2)}, u32[]{:S(2)}) %collective-permute-start.13) | collective-permute-done | bytes 262176 | tf_op jit(solution)/shard_map/ppermute | solution.py:276
  194.9 8.0 %collective-permute-start.16 = (f32[8,128]{1,0:T(8,128)S(1)}, f32[8,128]{1,0:T(8,128)S(1)}, u32[]{:S(2)}, u32[]{:S(2)}) collective-permute-start(f32[8,128]{1,0:T(8,128)S(1)} %get-tuple-element.94), channel_id=1, source_target_pairs={{0,128},{4,132},{8,136},{12,140},{16,144},{20,148},{24,152},{28,15... | collective-permute-start | bytes 12296 | tf_op jit(solution)/shard_map/ppermute | solution.py:277
  203.0 3.8 %collective-permute-start.17 = (bf16[4,64,128]{2,1,0:T(8,128)(2,1)S(1)}, bf16[4,64,128]{2,1,0:T(8,128)(2,1)S(1)}, u32[]{:S(2)}, u32[]{:S(2)}) collective-permute-start(bf16[4,64,128]{2,1,0:T(8,128)(2,1)S(1)} %fusion.58), channel_id=1, source_target_pairs={{0,128},{4,132},{8,136},{12,140},{16,144},{20,148},{24,152},{28,15... | collective-permute-start | bytes 196616 | tf_op jit(solution)/shard_map/ppermute | solution.py:276
  206.7 3.8 %collective-permute-done.17 = bf16[4,64,128]{2,1,0:T(8,128)(2,1)S(1)} collective-permute-done((bf16[4,64,128]{2,1,0:T(8,128)(2,1)S(1)}, bf16[4,64,128]{2,1,0:T(8,128)(2,1)S(1)}, u32[]{:S(2)}, u32[]{:S(2)}) %collective-permute-start.17) | collective-permute-done | bytes 65568 | tf_op jit(solution)/shard_map/ppermute | solution.py:276
  211.0 3.5 %collective-permute-start.19 = (bf16[128,256]{0,1:T(8,128)(2,1)S(1)}, bf16[128,256]{0,1:T(8,128)(2,1)S(1)}, u32[]{:S(2)}, u32[]{:S(2)}) collective-permute-start(bf16[128,256]{0,1:T(8,128)(2,1)S(1)} %bitcast.213), channel_id=1, source_target_pairs={{0,2},{1,3},{2,0},{3,1},{4,6},{5,7},{6,4},{7,5},{8,10},{9,11},{10,... | collective-permute-start | bytes 196616 | tf_op jit(solution)/shard_map/ppermute | solution.py:299
  221.8 32.4 %all_to_all.10 = bf16[64,1,10,256]{3,2,1,0:T(8,128)(2,1)S(1)} all-to-all(bf16[64,1,10,256]{3,2,1,0:T(8,128)(2,1)S(1)} %bitcast.206), channel_id=1, replica_groups=mesh['seq'=64,'tp'=4] {'seq'}, dimensions={0} | all-to-all | bytes 655360 | tf_op jit(solution)/shard_map/all_to_all | solution.py:329
  258.1 6.5 %collective-permute-done.24 = bf16[640,256]{1,0:T(8,128)(2,1)S(1)} collective-permute-done((bf16[640,256]{1,0:T(8,128)(2,1)S(1)}, bf16[640,256]{1,0:T(8,128)(2,1)S(1)}, u32[]{:S(2)}, u32[]{:S(2)}) %collective-permute-start.24) | collective-permute-done | bytes 327712 | tf_op jit(solution)/shard_map/ppermute | solution.py:299
  264.6 7.8 %collective-permute-done.25 = bf16[640,256]{1,0:T(8,128)(2,1)S(1)} collective-permute-done((bf16[640,256]{1,0:T(8,128)(2,1)S(1)}, bf16[640,256]{1,0:T(8,128)(2,1)S(1)}, u32[]{:S(2)}, u32[]{:S(2)}) %collective-permute-start.25) | collective-permute-done | bytes 327712 | tf_op jit(solution)/shard_map/ppermute | solution.py:299
  276.2 3.2 convolution_convert_fusion
  281.6 2.9 collective-permute-start.28
  284.7 5.6 %collective-permute-done.27 = bf16[640,256]{1,0:T(8,128)(2,1)S(1)} collective-permute-done((bf16[640,256]{1,0:T(8,128)(2,1)}, bf16[640,256]{1,0:T(8,128)(2,1)S(1)}, u32[]{:S(2)}, u32[]{:S(2)}) %collective-permute-start.27) | collective-permute-done | bytes 327712 | tf_op jit(solution)/shard_map/ppermute | solution.py:343
  290.3 8.8 %collective-permute-done.28 = bf16[640,256]{1,0:T(8,128)(2,1)} collective-permute-done((bf16[640,256]{1,0:T(8,128)(2,1)S(1)}, bf16[640,256]{1,0:T(8,128)(2,1)}, u32[]{:S(2)}, u32[]{:S(2)}) %collective-permute-start.28) | collective-permute-done | bytes 327712 | tf_op jit(solution)/shard_map/ppermute | solution.py:343
  301.3 6.3 %all-to-all-start.1 = ((bf16[64,1,10,256]{3,2,1,0:T(8,128)(2,1)}), bf16[64,1,10,256]{3,2,1,0:T(8,128)(2,1)S(1)}, u32[]{:S(2)}, u32[]{:S(2)}) async-start(bf16[64,1,10,256]{3,2,1,0:T(8,128)(2,1)} %bitcast.79), calls=%async_computation.1 | async-start | bytes 1048576 | tf_op jit(solution)/shard_map/all_to_all | solution.py:347
  311.1 14.1 %all-to-all-done.1 = bf16[64,1,10,256]{3,2,1,0:T(8,128)(2,1)S(1)} async-done(((bf16[64,1,10,256]{3,2,1,0:T(8,128)(2,1)}), bf16[64,1,10,256]{3,2,1,0:T(8,128)(2,1)S(1)}, u32[]{:S(2)}, u32[]{:S(2)}) %all-to-all-start.1) | async-done | bytes 327712 | tf_op jit(solution)/shard_map/all_to_all | solution.py:347
  (185 shorter events, 73.5 us)
Async XLA Ops:
  0.0 276.2 %copy-start = (bf16[1,352,1024]{2,1,0:T(8,128)(2,1)S(1)}, bf16[1,352,1024]{2,1,0:T(8,128)(2,1)}, u32[]{:S(2)}) copy-start(bf16[1,352,1024]{2,1,0:T(8,128)(2,1)} %param.27) | copy-start | bytes 2162692
  2.6 9.6 %collective-permute-start = (bf16[128,256]{1,0:T(8,128)(2,1)S(1)}, bf16[128,256]{1,0:T(8,128)(2,1)S(1)}, u32[]{:S(2)}, u32[]{:S(2)}) collective-permute-start(bf16[128,256]{1,0:T(8,128)(2,1)S(1)} %convolution_convert_fusion.4), channel_id=1, source_target_pairs={{0,128},{4,132},{8,136},{12,140},{16,144},{20,148},{24,152},{28,15... | collective-permute-start | bytes 196616 | tf_op jit(solution)/shard_map/ppermute | solution.py:220
  12.2 6.9 %collective-permute-start.1 = (bf16[2,128,256]{2,1,0:T(8,128)(2,1)S(1)}, bf16[2,128,256]{2,1,0:T(8,128)(2,1)S(1)}, u32[]{:S(2)}, u32[]{:S(2)}) collective-permute-start(bf16[2,128,256]{2,1,0:T(8,128)(2,1)S(1)} %pad_maximum_fusion.12), channel_id=1, source_target_pairs={{0,64},{4,68},{8,72},{12,76},{16,80},{20,84},{24,88},{28,92},{32,9... | collective-permute-start | bytes 393224 | tf_op jit(solution)/shard_map/ppermute | solution.py:220
  19.1 9.7 %collective-permute-start.2 = (bf16[2,2,128,256]{3,2,0,1:T(8,128)(2,1)S(1)}, bf16[2,2,128,256]{3,2,0,1:T(8,128)(2,1)S(1)}, u32[]{:S(2)}, u32[]{:S(2)}) collective-permute-start(bf16[2,2,128,256]{3,2,0,1:T(8,128)(2,1)S(1)} %pad_maximum_fusion.7), channel_id=1, source_target_pairs={{0,16},{4,20},{8,24},{12,28},{16,0},{20,4},{24,8},{28,12},{32,48},... | collective-permute-start | bytes 786440 | tf_op jit(solution)/shard_map/ppermute | solution.py:220
  28.9 11.4 %collective-permute-start.3 = (bf16[2,2,2,128,256]{4,3,0,1,2:T(8,128)(2,1)S(1)}, bf16[2,2,2,128,256]{4,3,0,1,2:T(8,128)(2,1)S(1)}, u32[]{:S(2)}, u32[]{:S(2)}) collective-permute-start(bf16[2,2,2,128,256]{4,3,0,1,2:T(8,128)(2,1)S(1)} %pad_maximum_fusion.6), channel_id=1, source_target_pairs={{0,32},{4,36},{8,40},{12,44},{16,48},{20,52},{24,56},{28,60},{32,0... | collective-permute-start | bytes 1572872 | tf_op jit(solution)/shard_map/ppermute | solution.py:220
  41.5 22.7 %collective-permute-start.4 = (bf16[2,2,2,2,128,256]{5,4,0,1,3,2:T(8,128)(2,1)}, bf16[2,2,2,2,128,256]{5,4,0,1,3,2:T(8,128)(2,1)S(1)}, u32[]{:S(2)}, u32[]{:S(2)}) collective-permute-start(bf16[2,2,2,2,128,256]{5,4,0,1,3,2:T(8,128)(2,1)} %pad_maximum_fusion.5), channel_id=1, source_target_pairs={{0,8},{4,12},{8,0},{12,4},{16,24},{20,28},{24,16},{28,20},{32,40},... | collective-permute-start | bytes 3145736 | tf_op jit(solution)/shard_map/ppermute | solution.py:220
  64.5 7.5 %collective-permute-start.5 = (bf16[2,2,2,2,2,128,256]{6,5,0,1,3,2,4:T(8,128)(2,1)S(1)}, bf16[2,2,2,2,2,128,256]{6,5,0,1,3,2,4:T(8,128)(2,1)}, u32[]{:S(2)}, u32[]{:S(2)}) collective-permute-start(bf16[2,2,2,2,2,128,256]{6,5,0,1,3,2,4:T(8,128)(2,1)S(1)} %pad_maximum_fusion.1), channel_id=1, source_target_pairs={{0,4},{4,0},{8,12},{12,8},{16,20},{20,16},{24,28},{28,24},{32,36},... | collective-permute-start | bytes 6291464 | tf_op jit(solution)/shard_map/ppermute | solution.py:220
  134.0 6.3 %collective-permute-start.7 = (bf16[2,2,2,2,2,4,64,128]{7,6,5,4,3,2,1,0:T(8,128)(2,1)S(1)}, bf16[2,2,2,2,2,4,64,128]{7,6,5,4,3,2,1,0:T(8,128)(2,1)}, u32[]{:S(2)}, u32[]{:S(2)}) collective-permute-start(bf16[2,2,2,2,2,4,64,128]{7,6,5,4,3,2,1,0:T(8,128)(2,1)S(1)} %fusion.1), channel_id=1, source_target_pairs={{0,4},{4,0},{8,12},{12,8},{16,20},{20,16},{24,28},{28,24},{32,36},... | collective-permute-start | bytes 6291464 | tf_op jit(solution)/shard_map/ppermute | solution.py:276
  134.6 5.7 %collective-permute-start.6 = (f32[2,2,2,2,2,8,128]{6,5,4,3,2,1,0:T(8,128)S(1)}, f32[2,2,2,2,2,8,128]{6,5,4,3,2,1,0:T(8,128)S(1)}, u32[]{:S(2)}, u32[]{:S(2)}) collective-permute-start(f32[2,2,2,2,2,8,128]{6,5,4,3,2,1,0:T(8,128)S(1)} %get-tuple-element.80), channel_id=1, source_target_pairs={{0,4},{4,0},{8,12},{12,8},{16,20},{20,16},{24,28},{28,24},{32,36},... | collective-permute-start | bytes 393224 | tf_op jit(solution)/shard_map/ppermute | solution.py:277
  135.0 15.4 %collective-permute-start.21 = (bf16[256,1024]{1,0:T(8,128)(2,1)}, bf16[256,1024]{1,0:T(8,128)(2,1)}, u32[]{:S(2)}, u32[]{:S(2)}) collective-permute-start(bf16[256,1024]{1,0:T(8,128)(2,1)} %param.21), channel_id=1, source_target_pairs={{0,1},{1,2},{2,3},{3,0},{4,5},{5,6},{6,7},{7,4},{8,9},{9,10},{10,1... | collective-permute-start | bytes 1572872 | tf_op jit(solution)/shard_map/ppermute | solution.py:299
  136.6 26.0 %collective-permute-start.22 = (bf16[256,1024]{1,0:T(8,128)(2,1)}, bf16[256,1024]{1,0:T(8,128)(2,1)}, u32[]{:S(2)}, u32[]{:S(2)}) collective-permute-start(bf16[256,1024]{1,0:T(8,128)(2,1)} %param.21), channel_id=1, source_target_pairs={{0,2},{1,3},{2,0},{3,1},{4,6},{5,7},{6,4},{7,5},{8,10},{9,11},{10,... | collective-permute-start | bytes 1572872 | tf_op jit(solution)/shard_map/ppermute | solution.py:299
  139.2 23.4 %collective-permute-start.23 = (bf16[256,1024]{1,0:T(8,128)(2,1)}, bf16[256,1024]{1,0:T(8,128)(2,1)}, u32[]{:S(2)}, u32[]{:S(2)}) collective-permute-start(bf16[256,1024]{1,0:T(8,128)(2,1)} %param.21), channel_id=1, source_target_pairs={{0,3},{1,0},{2,1},{3,2},{4,7},{5,4},{6,5},{7,6},{8,11},{9,8},{10,9... | collective-permute-start | bytes 1572872 | tf_op jit(solution)/shard_map/ppermute | solution.py:299
  147.6 25.9 %collective-permute-start.9 = (bf16[2,2,2,2,4,64,128]{6,5,4,3,2,1,0:T(8,128)(2,1)}, bf16[2,2,2,2,4,64,128]{6,5,4,3,2,1,0:T(8,128)(2,1)}, u32[]{:S(2)}, u32[]{:S(2)}) collective-permute-start(bf16[2,2,2,2,4,64,128]{6,5,4,3,2,1,0:T(8,128)(2,1)} %fusion.18), channel_id=1, source_target_pairs={{0,8},{4,12},{8,0},{12,4},{16,24},{20,28},{24,16},{28,20},{32,40},... | collective-permute-start | bytes 3145736 | tf_op jit(solution)/shard_map/ppermute | solution.py:276
  148.8 24.1 %collective-permute-start.8 = (f32[2,2,2,2,8,128]{5,4,3,2,1,0:T(8,128)S(1)}, f32[2,2,2,2,8,128]{5,4,3,2,1,0:T(8,128)S(1)}, u32[]{:S(2)}, u32[]{:S(2)}) collective-permute-start(f32[2,2,2,2,8,128]{5,4,3,2,1,0:T(8,128)S(1)} %get-tuple-element.84), channel_id=1, source_target_pairs={{0,8},{4,12},{8,0},{12,4},{16,24},{20,28},{24,16},{28,20},{32,40},... | collective-permute-start | bytes 196616 | tf_op jit(solution)/shard_map/ppermute | solution.py:277
  173.1 4.4 %collective-permute-start.10 = (f32[2,2,2,8,128]{4,3,2,1,0:T(8,128)S(1)}, f32[2,2,2,8,128]{4,3,2,1,0:T(8,128)S(1)}, u32[]{:S(2)}, u32[]{:S(2)}) collective-permute-start(f32[2,2,2,8,128]{4,3,2,1,0:T(8,128)S(1)} %get-tuple-element.88), channel_id=1, source_target_pairs={{0,32},{4,36},{8,40},{12,44},{16,48},{20,52},{24,56},{28,60},{32,0... | collective-permute-start | bytes 98312 | tf_op jit(solution)/shard_map/ppermute | solution.py:277
  175.9 11.5 %collective-permute-start.11 = (bf16[2,2,2,4,64,128]{5,4,3,2,1,0:T(8,128)(2,1)S(1)}, bf16[2,2,2,4,64,128]{5,4,3,2,1,0:T(8,128)(2,1)S(1)}, u32[]{:S(2)}, u32[]{:S(2)}) collective-permute-start(bf16[2,2,2,4,64,128]{5,4,3,2,1,0:T(8,128)(2,1)S(1)} %fusion.38), channel_id=1, source_target_pairs={{0,32},{4,36},{8,40},{12,44},{16,48},{20,52},{24,56},{28,60},{32,0... | collective-permute-start | bytes 1572872 | tf_op jit(solution)/shard_map/ppermute | solution.py:276
  177.5 13.1 %collective-permute-start.12 = (f32[2,2,8,128]{3,2,1,0:T(8,128)S(1)}, f32[2,2,8,128]{3,2,1,0:T(8,128)S(1)}, u32[]{:S(2)}, u32[]{:S(2)}) collective-permute-start(f32[2,2,8,128]{3,2,1,0:T(8,128)S(1)} %get-tuple-element.90), channel_id=1, source_target_pairs={{0,16},{4,20},{8,24},{12,28},{16,0},{20,4},{24,8},{28,12},{32,48},... | collective-permute-start | bytes 49160 | tf_op jit(solution)/shard_map/ppermute | solution.py:277
  187.8 6.8 %collective-permute-start.13 = (bf16[2,2,4,64,128]{4,3,2,1,0:T(8,128)(2,1)S(1)}, bf16[2,2,4,64,128]{4,3,2,1,0:T(8,128)(2,1)S(1)}, u32[]{:S(2)}, u32[]{:S(2)}) collective-permute-start(bf16[2,2,4,64,128]{4,3,2,1,0:T(8,128)(2,1)S(1)} %fusion.45), channel_id=1, source_target_pairs={{0,16},{4,20},{8,24},{12,28},{16,0},{20,4},{24,8},{28,12},{32,48},... | collective-permute-start | bytes 786440 | tf_op jit(solution)/shard_map/ppermute | solution.py:276
  190.7 4.2 %collective-permute-start.14 = (f32[2,8,128]{2,1,0:T(8,128)S(1)}, f32[2,8,128]{2,1,0:T(8,128)S(1)}, u32[]{:S(2)}, u32[]{:S(2)}) collective-permute-start(f32[2,8,128]{2,1,0:T(8,128)S(1)} %get-tuple-element.92), channel_id=1, source_target_pairs={{0,64},{4,68},{8,72},{12,76},{16,80},{20,84},{24,88},{28,92},{32,9... | collective-permute-start | bytes 24584 | tf_op jit(solution)/shard_map/ppermute | solution.py:277
  194.7 8.2 %collective-permute-start.15 = (bf16[2,4,64,128]{3,2,1,0:T(8,128)(2,1)S(1)}, bf16[2,4,64,128]{3,2,1,0:T(8,128)(2,1)S(1)}, u32[]{:S(2)}, u32[]{:S(2)}) collective-permute-start(bf16[2,4,64,128]{3,2,1,0:T(8,128)(2,1)S(1)} %fusion.54), channel_id=1, source_target_pairs={{0,64},{4,68},{8,72},{12,76},{16,80},{20,84},{24,88},{28,92},{32,9... | collective-permute-start | bytes 393224 | tf_op jit(solution)/shard_map/ppermute | solution.py:276
  194.9 11.8 %collective-permute-start.16 = (f32[8,128]{1,0:T(8,128)S(1)}, f32[8,128]{1,0:T(8,128)S(1)}, u32[]{:S(2)}, u32[]{:S(2)}) collective-permute-start(f32[8,128]{1,0:T(8,128)S(1)} %get-tuple-element.94), channel_id=1, source_target_pairs={{0,128},{4,132},{8,136},{12,140},{16,144},{20,148},{24,152},{28,15... | collective-permute-start | bytes 12296 | tf_op jit(solution)/shard_map/ppermute | solution.py:277
  203.0 7.5 %collective-permute-start.17 = (bf16[4,64,128]{2,1,0:T(8,128)(2,1)S(1)}, bf16[4,64,128]{2,1,0:T(8,128)(2,1)S(1)}, u32[]{:S(2)}, u32[]{:S(2)}) collective-permute-start(bf16[4,64,128]{2,1,0:T(8,128)(2,1)S(1)} %fusion.58), channel_id=1, source_target_pairs={{0,128},{4,132},{8,136},{12,140},{16,144},{20,148},{24,152},{28,15... | collective-permute-start | bytes 196616 | tf_op jit(solution)/shard_map/ppermute | solution.py:276
  210.5 6.0 %collective-permute-start.18 = (bf16[128,256]{0,1:T(8,128)(2,1)S(1)}, bf16[128,256]{0,1:T(8,128)(2,1)S(1)}, u32[]{:S(2)}, u32[]{:S(2)}) collective-permute-start(bf16[128,256]{0,1:T(8,128)(2,1)S(1)} %bitcast.212), channel_id=1, source_target_pairs={{0,1},{1,2},{2,3},{3,0},{4,5},{5,6},{6,7},{7,4},{8,9},{9,10},{10,1... | collective-permute-start | bytes 196616 | tf_op jit(solution)/shard_map/ppermute | solution.py:299
  211.0 5.9 %collective-permute-start.19 = (bf16[128,256]{0,1:T(8,128)(2,1)S(1)}, bf16[128,256]{0,1:T(8,128)(2,1)S(1)}, u32[]{:S(2)}, u32[]{:S(2)}) collective-permute-start(bf16[128,256]{0,1:T(8,128)(2,1)S(1)} %bitcast.213), channel_id=1, source_target_pairs={{0,2},{1,3},{2,0},{3,1},{4,6},{5,7},{6,4},{7,5},{8,10},{9,11},{10,... | collective-permute-start | bytes 196616 | tf_op jit(solution)/shard_map/ppermute | solution.py:299
  214.5 3.1 collective-permute-start.20
  254.4 10.2 %collective-permute-start.24 = (bf16[640,256]{1,0:T(8,128)(2,1)S(1)}, bf16[640,256]{1,0:T(8,128)(2,1)S(1)}, u32[]{:S(2)}, u32[]{:S(2)}) collective-permute-start(bf16[640,256]{1,0:T(8,128)(2,1)S(1)} %reshape_squeeze.3), channel_id=1, source_target_pairs={{0,1},{1,2},{2,3},{3,0},{4,5},{5,6},{6,7},{7,4},{8,9},{9,10},{10,1... | collective-permute-start | bytes 983048 | tf_op jit(solution)/shard_map/ppermute | solution.py:299
  255.4 17.0 %collective-permute-start.25 = (bf16[640,256]{1,0:T(8,128)(2,1)S(1)}, bf16[640,256]{1,0:T(8,128)(2,1)S(1)}, u32[]{:S(2)}, u32[]{:S(2)}) collective-permute-start(bf16[640,256]{1,0:T(8,128)(2,1)S(1)} %reshape_squeeze.3), channel_id=1, source_target_pairs={{0,2},{1,3},{2,0},{3,1},{4,6},{5,7},{6,4},{7,5},{8,10},{9,11},{10,... | collective-permute-start | bytes 983048 | tf_op jit(solution)/shard_map/ppermute | solution.py:299
  257.9 14.4 %collective-permute-start.26 = (bf16[640,256]{1,0:T(8,128)(2,1)S(1)}, bf16[640,256]{1,0:T(8,128)(2,1)S(1)}, u32[]{:S(2)}, u32[]{:S(2)}) collective-permute-start(bf16[640,256]{1,0:T(8,128)(2,1)S(1)} %reshape_squeeze.3), channel_id=1, source_target_pairs={{0,3},{1,0},{2,1},{3,2},{4,7},{5,4},{6,5},{7,6},{8,11},{9,8},{10,9... | collective-permute-start | bytes 983048 | tf_op jit(solution)/shard_map/ppermute | solution.py:299
  280.3 10.0 %collective-permute-start.27 = (bf16[640,256]{1,0:T(8,128)(2,1)}, bf16[640,256]{1,0:T(8,128)(2,1)S(1)}, u32[]{:S(2)}, u32[]{:S(2)}) collective-permute-start(bf16[640,256]{1,0:T(8,128)(2,1)} %get-tuple-element.64), channel_id=1, source_target_pairs={{0,1},{1,2},{2,3},{3,0},{4,5},{5,6},{6,7},{7,4},{8,9},{9,10},{10,1... | collective-permute-start | bytes 983048 | tf_op jit(solution)/shard_map/ppermute | solution.py:343
  281.6 17.5 %collective-permute-start.28 = (bf16[640,256]{1,0:T(8,128)(2,1)S(1)}, bf16[640,256]{1,0:T(8,128)(2,1)}, u32[]{:S(2)}, u32[]{:S(2)}) collective-permute-start(bf16[640,256]{1,0:T(8,128)(2,1)S(1)} %get-tuple-element.66), channel_id=1, source_target_pairs={{0,2},{1,3},{2,0},{3,1},{4,6},{5,7},{6,4},{7,5},{8,10},{9,11},{10,... | collective-permute-start | bytes 983048 | tf_op jit(solution)/shard_map/ppermute | solution.py:343
  284.5 14.6 %collective-permute-start.29 = (bf16[640,256]{1,0:T(8,128)(2,1)S(1)}, bf16[640,256]{1,0:T(8,128)(2,1)}, u32[]{:S(2)}, u32[]{:S(2)}) collective-permute-start(bf16[640,256]{1,0:T(8,128)(2,1)S(1)} %get-tuple-element.65), channel_id=1, source_target_pairs={{0,3},{1,0},{2,1},{3,2},{4,7},{5,4},{6,5},{7,6},{8,11},{9,8},{10,9... | collective-permute-start | bytes 983048 | tf_op jit(solution)/shard_map/ppermute | solution.py:343
  301.3 24.0 %all-to-all-start.1 = ((bf16[64,1,10,256]{3,2,1,0:T(8,128)(2,1)}), bf16[64,1,10,256]{3,2,1,0:T(8,128)(2,1)S(1)}, u32[]{:S(2)}, u32[]{:S(2)}) async-start(bf16[64,1,10,256]{3,2,1,0:T(8,128)(2,1)} %bitcast.79), calls=%async_computation.1 | async-start | bytes 1048576 | tf_op jit(solution)/shard_map/all_to_all | solution.py:347
  (16 other events, 158.5 us)
